TPU v7x, 128 devices: a whole 4x4x4 slice. The times are simulated.
128 devices in a mesh: lat: 16 (over z_lo, x, core), freq: 8 (over z_hi, y).
Axes of the slice: x: 4, y: 4, z: 4 (z_hi: 2, z_lo: 2; z = z_hi * 2 + z_lo), core: 2. Of those that a mesh axis runs over, the one named last changes fastest.
Arguments:
- gravity: float32 [256, 21600], P('lat', 'freq'), may hold values from -6 to 6
- coef: bfloat16 [2176, 2, 2176], P(('lat', 'freq')), may hold values from -0.125 to 0.125
- legendre: bfloat16 [2176, 2176, 256], P(('lat', 'freq')), may hold values from -6 to 6
- order_table: int32 [2176], replicated, may hold values from 0 to 2175, as said below
- band_rows: int32 [256], P('lat'), may hold values from 0 to 2399, as said below
- kernel: bfloat16 [511, 10800], P(None, 'freq'), may hold values from -0.375 to 0.375
Outputs:
- geoid: float32 [256, 21600], P('lat', 'freq')
Inputs may be any that keep to these rules, and one draw needn't show every extreme that they name: `order_table`: A permutation of the orders 0 to 2175; the slot s lies in the block of slots s // 17, and its order m has m % 8 == (s // 17) % 8. `band_rows`: strictly increasing; the first row is parallel 0 and the last is parallel 2400 - 1.
All inputs are finite; a program needn't handle non-finite values.
Results may differ from a plain program's by a relative error of at most 0.0032.
Values may be sent and summed in bfloat16 or wider, within the bound.
No kernel may reach another device: no remote copies, remote signals or barrier semaphores. Data moves between devices by JAX's collectives and lax.ppermute only.
A program may use at most 128 MiB of HBM per device.

v0:
```python
import jax
import jax.numpy as jnp
import numpy as np
from jax import lax
from jax.sharding import PartitionSpec as P

L = 21600
PA = 144
PB = 150
PH = 75


highest = lax.Precision.HIGHEST


def passed_along(block, axis, distance):
    devices = range(lax.axis_size(axis))
    route = [((i - distance) % len(devices), i) for i in devices]
    return lax.ppermute(block, axis, route)


def angle_table(first, second, period):
    phase = first * second % period
    return phase.astype(jnp.float32) * (2.0 * np.pi / period)


def forward_bands(grid, first_start, bands):
    rows = grid.shape[0]
    count_one = grid.shape[1]
    first_index = first_start + jnp.arange(count_one, dtype=jnp.int32)
    freq_one = jnp.arange(PA, dtype=jnp.int32)
    theta_one = angle_table(first_index[:, None], freq_one[None, :], PA)
    section_re = jnp.einsum("rab,ak->rbk", grid, jnp.cos(theta_one), precision=highest)
    section_im = -jnp.einsum("rab,ak->rbk", grid, jnp.sin(theta_one), precision=highest)
    second_index = jnp.arange(PB, dtype=jnp.int32)
    twist = angle_table(second_index[:, None], freq_one[None, :], L)
    twist_cos = jnp.cos(twist)
    twist_sin = jnp.sin(twist)
    turned_re = section_re * twist_cos + section_im * twist_sin
    turned_im = section_im * twist_cos - section_re * twist_sin
    freq_two = jnp.arange(PH, dtype=jnp.int32)
    theta_two = angle_table(second_index[:, None], freq_two[None, :], PB)
    cos_two = jnp.cos(theta_two)
    sin_two = jnp.sin(theta_two)
    spec_re = jnp.einsum("rbk,bm->rkm", turned_re, cos_two, precision=highest) + jnp.einsum(
        "rbk,bm->rkm", turned_im, sin_two, precision=highest
    )
    spec_im = jnp.einsum("rbk,bm->rkm", turned_im, cos_two, precision=highest) - jnp.einsum(
        "rbk,bm->rkm", turned_re, sin_two, precision=highest
    )
    scale = (2.0 / L) ** 0.5
    stacked = jnp.stack([spec_re, spec_im]) * scale
    span = PA // bands
    stacked = stacked.reshape(2, rows, span, bands, PH).transpose(3, 1, 0, 4, 2)
    return stacked.reshape(bands, rows, 2, PH * span)


def inverse_rows(spectra, band_ids, bands):
    count = spectra.shape[0]
    rows = spectra.shape[1]
    span = PA // bands
    parts = spectra.reshape(count, rows, 2, PH, span)
    part_re = parts[:, :, 0]
    part_im = parts[:, :, 1]
    freq_two = jnp.arange(PH, dtype=jnp.int32)
    second_index = jnp.arange(PB, dtype=jnp.int32)
    theta_two = angle_table(freq_two[:, None], second_index[None, :], PB)
    cos_two = jnp.cos(theta_two)
    sin_two = jnp.sin(theta_two)
    middle_re = jnp.einsum("brms,mn->brsn", part_re, cos_two, precision=highest) - jnp.einsum(
        "brms,mn->brsn", part_im, sin_two, precision=highest
    )
    middle_im = jnp.einsum("brms,mn->brsn", part_im, cos_two, precision=highest) + jnp.einsum(
        "brms,mn->brsn", part_re, sin_two, precision=highest
    )
    freq_one = jnp.arange(span, dtype=jnp.int32)[None, :] * bands + band_ids[:, None]
    twist = angle_table(freq_one[:, :, None], second_index[None, None, :], L)
    twist_cos = jnp.cos(twist)[:, None]
    twist_sin = jnp.sin(twist)[:, None]
    turned_re = middle_re * twist_cos - middle_im * twist_sin
    turned_im = middle_re * twist_sin + middle_im * twist_cos
    first_index = jnp.arange(PA, dtype=jnp.int32)
    theta_one = angle_table(freq_one[:, :, None], first_index[None, None, :], PA)
    grid = jnp.einsum(
        "brsn,bsa->ran", turned_re, jnp.cos(theta_one), precision=highest
    ) - jnp.einsum("brsn,bsa->ran", turned_im, jnp.sin(theta_one), precision=highest)
    return grid * (2.0 / L) ** 0.5


def per_device(gravity, coef, legendre, order_table, band_rows, kernel):
    bands = lax.axis_size("freq")
    blocks = lax.axis_size("lat")
    band_self = lax.axis_index("freq")
    block_self = lax.axis_index("lat")
    rows = gravity.shape[0]
    span = PA // bands
    local_grid = gravity.reshape(rows, span, PB)
    terms = forward_bands(local_grid, band_self * span, bands)
    observed = lax.psum_scatter(terms, "freq", scatter_dimension=0, tiled=True)[0]
    band_width = observed.shape[2]
    synth = jnp.einsum("ocn,onq->ocq", coef, legendre, preferred_element_type=jnp.float32).astype(
        jnp.bfloat16
    )
    routed = lax.all_to_all(synth, "lat", split_axis=2, concat_axis=0, tiled=True)
    per_slot = coef.shape[0]
    slot_ids = (
        (jnp.arange(blocks, dtype=jnp.int32)[:, None] * bands + band_self) * per_slot
        + jnp.arange(per_slot, dtype=jnp.int32)[None, :]
    ).reshape(-1)
    positions = order_table[slot_ids] // bands
    selector = (positions[:, None] == jnp.arange(band_width, dtype=jnp.int32)[None, :]).astype(
        jnp.bfloat16
    )
    model = jnp.einsum("jcr,jt->rct", routed, selector, preferred_element_type=jnp.float32)
    weight = jnp.cos((20.0 + band_rows.astype(jnp.float32) / 60.0) * (np.pi / 180.0))
    weighted = ((observed - model) * weight[:, None, None]).astype(jnp.bfloat16)
    total_rows = rows * blocks
    offsets = np.arange(rows)[None, :] - np.arange(rows)[:, None] + rows - 1

    def gather_terms(source, owner):
        first = (owner - block_self) * rows + total_rows - rows
        window = lax.dynamic_slice_in_dim(kernel, first, 2 * rows - 1, 0)
        toeplitz = window[offsets]
        return jnp.einsum("pqk,qck->pck", toeplitz, source, preferred_element_type=jnp.float32)

    stokes = gather_terms(weighted, block_self)

    def advance(count, carry):
        total, moving = carry
        moving = passed_along(moving, "lat", 1)
        owner = (block_self - count) % blocks
        return (total + gather_terms(moving, owner), moving)

    stokes, carried = lax.fori_loop(1, blocks, advance, (stokes, weighted))
    grid_terms = inverse_rows(stokes[None], jnp.reshape(band_self, (1,)), bands)
    geoid = lax.psum_scatter(grid_terms, "freq", scatter_dimension=1, tiled=True)
    return geoid.reshape(rows, span * PB)


def solution(mesh):
    return jax.shard_map(
        per_device,
        mesh=mesh,
        in_specs=(
            P("lat", "freq"),
            P(("lat", "freq"), None, None),
            P(("lat", "freq"), None, None),
            P(),
            P("lat"),
            P(None, "freq"),
        ),
        out_specs=P("lat", "freq"),
        check_vma=False,
    )
```

profile of v0, /device:TPU:0, one launch (start us, length us, event | category | flops | bytes accessed | tf_op | source)
XLA Modules:
  0.0 473.8 jit_solution(18244841325527985102)
XLA Ops:
  7.7 2.2 fusion.101
  9.9 2.2 fusion.103
  12.8 2.5 fusion.12
  15.2 2.5 fusion.8
  17.7 3.0 fusion.6
  20.7 2.5 fusion.5
  23.5 7.7 %copy.47 = f32[8,16,2,75,18]{4,3,1,2,0:T(8,128)} copy(f32[8,16,2,75,18]{3,0,4,1,2:T(8,128)S(1)} %fusion.1) | data formatting | bytes 2764800 | tf_op jit(solution)/shard_map/transpose | solution.py:54
  31.2 8.0 %reshape.326 = f32[8,16,2,1350]{3,1,2,0:T(8,128)} reshape(f32[8,16,2,75,18]{4,3,1,2,0:T(8,128)} %copy.47) | data formatting | bytes 2764800 | tf_op jit(solution)/shard_map/reshape | solution.py:55
  39.2 8.9 %convolution_convert_fusion = bf16[17,2,256]{2,1,0:T(2,128)(2,1)S(1)} fusion(bf16[17,2,2176]{2,1,0:T(2,128)(2,1)S(1)} %copy-done, bf16[17,2176,256]{2,1,0:T(8,128)(2,1)} %param.13), kind=kOutput, calls=%fused_computation.25 | convolution fusion | flops 37888512 | bytes 19105280 | tf_op jit(solution)/shard_map/ocn,onq->ocq/dot_general | solution.py:101
  49.1 5.9 %all-to-all-start = ((bf16[16,2,272]{2,1,0:T(2,128)(2,1)}), bf16[16,2,272]{2,1,0:T(2,128)(2,1)S(1)}, u32[]{:S(2)}, u32[]{:S(2)}) async-start(bf16[16,2,272]{2,1,0:T(2,128)(2,1)} %reshape.372), calls=%async_computation.1 | async-start | bytes 49152 | tf_op jit(solution)/shard_map/all_to_all | solution.py:104
  55.5 2.2 gather_fusion.1
  58.0 1.8 copy.51
  61.1 6.4 %copy.53 = bf16[16,16,1350]{1,0,2:T(8,128)(2,1)} copy(bf16[16,16,1350]{2,1,0:T(8,128)(2,1)S(1)} %bitcast.121) | data formatting | bytes 1382400 | tf_op jit(solution)/shard_map/gather | solution.py:123
  68.4 48.0 %reduce-scatter.3.cloned.1.call-done = f32[1,16,2,1350]{3,1,2,0:T(8,128)} async-done(((f32[8,16,2,1350]{3,1,2,0:T(8,128)}), f32[1,16,2,1350]{3,1,2,0:T(8,128)}) %reduce-scatter.3.cloned.1.call-update) | async-done | bytes 172816 | tf_op jit(solution)/shard_map/reduce_scatter | solution.py:99
  118.4 6.6 %convolution_bitcast_fusion.1 = f32[16,2,1350]{0,1,2:T(2,128)} fusion(bf16[16,2,1350]{0,1,2:T(2,128)(2,1)S(1)} %copy.52, bf16[16,16,1350]{1,0,2:T(8,128)(2,1)} %copy.53), kind=kOutput, calls=%fused_computation.18 | convolution fusion | flops 1382400 | bytes 950400 | tf_op jit(solution)/shard_map/pqk,qck->pck/dot_general | solution.py:124
  125.0 246.9 %while.20 = (s32[]{:T(128)}, f32[16,2,1350]{0,1,2:T(2,128)}, bf16[16,2,1350]{2,0,1:T(8,128)(2,1)S(1)}, s32[]{:T(128)}, bf16[511,1350]{1,0:T(8,128)(2,1)S(1)}, /*...) while((s32[]{:T(128)}, f32[16,2,1350]{0,1,2:T(2,128)}, ...), condition=%wide.region_2.3_spmd.clone, body=%wide.region_1.2_spmd.sunk.clone.sunk | while | flops 1426644 | bytes 4753096 | solution.py:134
  125.1 1.3 gather_fusion
  126.4 6.4 %copy.71 = bf16[16,16,1350]{1,0,2:T(8,128)(2,1)} copy(bf16[16,16,1350]{2,1,0:T(8,128)(2,1)S(1)} %bitcast.120) | data formatting | bytes 1382400 | tf_op jit(solution)/shard_map/while/body/eval_jaxpr/gather | solution.py:123
  133.7 7.1 %fusion.195 = f32[16,2,1350]{0,1,2:T(2,128)} fusion(f32[16,2,1350]{0,1,2:T(2,128)} %get-tuple-element.336, bf16[16,16,1350]{1,0,2:T(8,128)(2,1)} %copy.71, bf16[16,2,1350]{0,1,2:T(2,128)(2,1)S(1)} %copy.72), kind=kOutput, calls=%fused_computation.4.clone.1 | convolution fusion | flops 1425600 | bytes 1123200 | tf_op jit(solution)/shard_map/while/body/eval_jaxpr/pqk,qck->pck/dot_general | solution.py:124
  140.8 1.6 collective-permute-start
  142.5 1.3 gather_fusion
  143.8 6.4 %copy.71 = bf16[16,16,1350]{1,0,2:T(8,128)(2,1)} copy(bf16[16,16,1350]{2,1,0:T(8,128)(2,1)S(1)} %bitcast.120) | data formatting | bytes 1382400 | tf_op jit(solution)/shard_map/while/body/eval_jaxpr/gather | solution.py:123
  151.1 7.1 %fusion.195 = f32[16,2,1350]{0,1,2:T(2,128)} fusion(f32[16,2,1350]{0,1,2:T(2,128)} %get-tuple-element.336, bf16[16,16,1350]{1,0,2:T(8,128)(2,1)} %copy.71, bf16[16,2,1350]{0,1,2:T(2,128)(2,1)S(1)} %copy.72), kind=kOutput, calls=%fused_computation.4.clone.1 | convolution fusion | flops 1425600 | bytes 1123200 | tf_op jit(solution)/shard_map/while/body/eval_jaxpr/pqk,qck->pck/dot_general | solution.py:124
  158.3 1.3 gather_fusion
  159.6 6.4 %copy.71 = bf16[16,16,1350]{1,0,2:T(8,128)(2,1)} copy(bf16[16,16,1350]{2,1,0:T(8,128)(2,1)S(1)} %bitcast.120) | data formatting | bytes 1382400 | tf_op jit(solution)/shard_map/while/body/eval_jaxpr/gather | solution.py:123
  166.9 7.1 %fusion.195 = f32[16,2,1350]{0,1,2:T(2,128)} fusion(f32[16,2,1350]{0,1,2:T(2,128)} %get-tuple-element.336, bf16[16,16,1350]{1,0,2:T(8,128)(2,1)} %copy.71, bf16[16,2,1350]{0,1,2:T(2,128)(2,1)S(1)} %copy.72), kind=kOutput, calls=%fused_computation.4.clone.1 | convolution fusion | flops 1425600 | bytes 1123200 | tf_op jit(solution)/shard_map/while/body/eval_jaxpr/pqk,qck->pck/dot_general | solution.py:124
  174.0 1.6 collective-permute-start
  175.7 1.3 gather_fusion
  177.0 6.4 %copy.71 = bf16[16,16,1350]{1,0,2:T(8,128)(2,1)} copy(bf16[16,16,1350]{2,1,0:T(8,128)(2,1)S(1)} %bitcast.120) | data formatting | bytes 1382400 | tf_op jit(solution)/shard_map/while/body/eval_jaxpr/gather | solution.py:123
  184.3 7.1 %fusion.195 = f32[16,2,1350]{0,1,2:T(2,128)} fusion(f32[16,2,1350]{0,1,2:T(2,128)} %get-tuple-element.336, bf16[16,16,1350]{1,0,2:T(8,128)(2,1)} %copy.71, bf16[16,2,1350]{0,1,2:T(2,128)(2,1)S(1)} %copy.72), kind=kOutput, calls=%fused_computation.4.clone.1 | convolution fusion | flops 1425600 | bytes 1123200 | tf_op jit(solution)/shard_map/while/body/eval_jaxpr/pqk,qck->pck/dot_general | solution.py:124
  191.5 1.3 gather_fusion
  192.8 6.4 %copy.71 = bf16[16,16,1350]{1,0,2:T(8,128)(2,1)} copy(bf16[16,16,1350]{2,1,0:T(8,128)(2,1)S(1)} %bitcast.120) | data formatting | bytes 1382400 | tf_op jit(solution)/shard_map/while/body/eval_jaxpr/gather | solution.py:123
  200.1 7.1 %fusion.195 = f32[16,2,1350]{0,1,2:T(2,128)} fusion(f32[16,2,1350]{0,1,2:T(2,128)} %get-tuple-element.336, bf16[16,16,1350]{1,0,2:T(8,128)(2,1)} %copy.71, bf16[16,2,1350]{0,1,2:T(2,128)(2,1)S(1)} %copy.72), kind=kOutput, calls=%fused_computation.4.clone.1 | convolution fusion | flops 1425600 | bytes 1123200 | tf_op jit(solution)/shard_map/while/body/eval_jaxpr/pqk,qck->pck/dot_general | solution.py:124
  207.2 1.3 collective-permute-start
  209.9 6.4 %copy.71 = bf16[16,16,1350]{1,0,2:T(8,128)(2,1)} copy(bf16[16,16,1350]{2,1,0:T(8,128)(2,1)S(1)} %bitcast.120) | data formatting | bytes 1382400 | tf_op jit(solution)/shard_map/while/body/eval_jaxpr/gather | solution.py:123
  217.2 7.1 %fusion.195 = f32[16,2,1350]{0,1,2:T(2,128)} fusion(f32[16,2,1350]{0,1,2:T(2,128)} %get-tuple-element.336, bf16[16,16,1350]{1,0,2:T(8,128)(2,1)} %copy.71, bf16[16,2,1350]{0,1,2:T(2,128)(2,1)S(1)} %copy.72), kind=kOutput, calls=%fused_computation.4.clone.1 | convolution fusion | flops 1425600 | bytes 1123200 | tf_op jit(solution)/shard_map/while/body/eval_jaxpr/pqk,qck->pck/dot_general | solution.py:124
  224.5 1.3 gather_fusion
  225.8 6.4 %copy.71 = bf16[16,16,1350]{1,0,2:T(8,128)(2,1)} copy(bf16[16,16,1350]{2,1,0:T(8,128)(2,1)S(1)} %bitcast.120) | data formatting | bytes 1382400 | tf_op jit(solution)/shard_map/while/body/eval_jaxpr/gather | solution.py:123
  233.1 7.1 %fusion.195 = f32[16,2,1350]{0,1,2:T(2,128)} fusion(f32[16,2,1350]{0,1,2:T(2,128)} %get-tuple-element.336, bf16[16,16,1350]{1,0,2:T(8,128)(2,1)} %copy.71, bf16[16,2,1350]{0,1,2:T(2,128)(2,1)S(1)} %copy.72), kind=kOutput, calls=%fused_computation.4.clone.1 | convolution fusion | flops 1425600 | bytes 1123200 | tf_op jit(solution)/shard_map/while/body/eval_jaxpr/pqk,qck->pck/dot_general | solution.py:124
  242.3 6.4 %copy.71 = bf16[16,16,1350]{1,0,2:T(8,128)(2,1)} copy(bf16[16,16,1350]{2,1,0:T(8,128)(2,1)S(1)} %bitcast.120) | data formatting | bytes 1382400 | tf_op jit(solution)/shard_map/while/body/eval_jaxpr/gather | solution.py:123
  249.6 7.1 %fusion.195 = f32[16,2,1350]{0,1,2:T(2,128)} fusion(f32[16,2,1350]{0,1,2:T(2,128)} %get-tuple-element.336, bf16[16,16,1350]{1,0,2:T(8,128)(2,1)} %copy.71, bf16[16,2,1350]{0,1,2:T(2,128)(2,1)S(1)} %copy.72), kind=kOutput, calls=%fused_computation.4.clone.1 | convolution fusion | flops 1425600 | bytes 1123200 | tf_op jit(solution)/shard_map/while/body/eval_jaxpr/pqk,qck->pck/dot_general | solution.py:124
  256.9 1.3 gather_fusion
  258.2 6.4 %copy.71 = bf16[16,16,1350]{1,0,2:T(8,128)(2,1)} copy(bf16[16,16,1350]{2,1,0:T(8,128)(2,1)S(1)} %bitcast.120) | data formatting | bytes 1382400 | tf_op jit(solution)/shard_map/while/body/eval_jaxpr/gather | solution.py:123
  265.5 7.1 %fusion.195 = f32[16,2,1350]{0,1,2:T(2,128)} fusion(f32[16,2,1350]{0,1,2:T(2,128)} %get-tuple-element.336, bf16[16,16,1350]{1,0,2:T(8,128)(2,1)} %copy.71, bf16[16,2,1350]{0,1,2:T(2,128)(2,1)S(1)} %copy.72), kind=kOutput, calls=%fused_computation.4.clone.1 | convolution fusion | flops 1425600 | bytes 1123200 | tf_op jit(solution)/shard_map/while/body/eval_jaxpr/pqk,qck->pck/dot_general | solution.py:124
  272.6 1.6 collective-permute-start
  274.2 1.3 gather_fusion
  275.5 6.4 %copy.71 = bf16[16,16,1350]{1,0,2:T(8,128)(2,1)} copy(bf16[16,16,1350]{2,1,0:T(8,128)(2,1)S(1)} %bitcast.120) | data formatting | bytes 1382400 | tf_op jit(solution)/shard_map/while/body/eval_jaxpr/gather | solution.py:123
  282.8 7.1 %fusion.195 = f32[16,2,1350]{0,1,2:T(2,128)} fusion(f32[16,2,1350]{0,1,2:T(2,128)} %get-tuple-element.336, bf16[16,16,1350]{1,0,2:T(8,128)(2,1)} %copy.71, bf16[16,2,1350]{0,1,2:T(2,128)(2,1)S(1)} %copy.72), kind=kOutput, calls=%fused_computation.4.clone.1 | convolution fusion | flops 1425600 | bytes 1123200 | tf_op jit(solution)/shard_map/while/body/eval_jaxpr/pqk,qck->pck/dot_general | solution.py:124
  291.4 6.4 %copy.71 = bf16[16,16,1350]{1,0,2:T(8,128)(2,1)} copy(bf16[16,16,1350]{2,1,0:T(8,128)(2,1)S(1)} %bitcast.120) | data formatting | bytes 1382400 | tf_op jit(solution)/shard_map/while/body/eval_jaxpr/gather | solution.py:123
  298.7 7.1 %fusion.195 = f32[16,2,1350]{0,1,2:T(2,128)} fusion(f32[16,2,1350]{0,1,2:T(2,128)} %get-tuple-element.336, bf16[16,16,1350]{1,0,2:T(8,128)(2,1)} %copy.71, bf16[16,2,1350]{0,1,2:T(2,128)(2,1)S(1)} %copy.72), kind=kOutput, calls=%fused_computation.4.clone.1 | convolution fusion | flops 1425600 | bytes 1123200 | tf_op jit(solution)/shard_map/while/body/eval_jaxpr/pqk,qck->pck/dot_general | solution.py:124
  305.8 1.6 collective-permute-start
  308.8 6.4 %copy.71 = bf16[16,16,1350]{1,0,2:T(8,128)(2,1)} copy(bf16[16,16,1350]{2,1,0:T(8,128)(2,1)S(1)} %bitcast.120) | data formatting | bytes 1382400 | tf_op jit(solution)/shard_map/while/body/eval_jaxpr/gather | solution.py:123
  316.1 7.1 %fusion.195 = f32[16,2,1350]{0,1,2:T(2,128)} fusion(f32[16,2,1350]{0,1,2:T(2,128)} %get-tuple-element.336, bf16[16,16,1350]{1,0,2:T(8,128)(2,1)} %copy.71, bf16[16,2,1350]{0,1,2:T(2,128)(2,1)S(1)} %copy.72), kind=kOutput, calls=%fused_computation.4.clone.1 | convolution fusion | flops 1425600 | bytes 1123200 | tf_op jit(solution)/shard_map/while/body/eval_jaxpr/pqk,qck->pck/dot_general | solution.py:124
  324.6 6.4 %copy.71 = bf16[16,16,1350]{1,0,2:T(8,128)(2,1)} copy(bf16[16,16,1350]{2,1,0:T(8,128)(2,1)S(1)} %bitcast.120) | data formatting | bytes 1382400 | tf_op jit(solution)/shard_map/while/body/eval_jaxpr/gather | solution.py:123
  331.9 7.1 %fusion.195 = f32[16,2,1350]{0,1,2:T(2,128)} fusion(f32[16,2,1350]{0,1,2:T(2,128)} %get-tuple-element.336, bf16[16,16,1350]{1,0,2:T(8,128)(2,1)} %copy.71, bf16[16,2,1350]{0,1,2:T(2,128)(2,1)S(1)} %copy.72), kind=kOutput, calls=%fused_computation.4.clone.1 | convolution fusion | flops 1425600 | bytes 1123200 | tf_op jit(solution)/shard_map/while/body/eval_jaxpr/pqk,qck->pck/dot_general | solution.py:124
  341.7 6.4 %copy.71 = bf16[16,16,1350]{1,0,2:T(8,128)(2,1)} copy(bf16[16,16,1350]{2,1,0:T(8,128)(2,1)S(1)} %bitcast.120) | data formatting | bytes 1382400 | tf_op jit(solution)/shard_map/while/body/eval_jaxpr/gather | solution.py:123
  349.0 7.1 %fusion.195 = f32[16,2,1350]{0,1,2:T(2,128)} fusion(f32[16,2,1350]{0,1,2:T(2,128)} %get-tuple-element.336, bf16[16,16,1350]{1,0,2:T(8,128)(2,1)} %copy.71, bf16[16,2,1350]{0,1,2:T(2,128)(2,1)S(1)} %copy.72), kind=kOutput, calls=%fused_computation.4.clone.1 | convolution fusion | flops 1425600 | bytes 1123200 | tf_op jit(solution)/shard_map/while/body/eval_jaxpr/pqk,qck->pck/dot_general | solution.py:124
  357.6 6.4 %copy.71 = bf16[16,16,1350]{1,0,2:T(8,128)(2,1)} copy(bf16[16,16,1350]{2,1,0:T(8,128)(2,1)S(1)} %bitcast.120) | data formatting | bytes 1382400 | tf_op jit(solution)/shard_map/while/body/eval_jaxpr/gather | solution.py:123
  364.9 7.1 %fusion.195 = f32[16,2,1350]{0,1,2:T(2,128)} fusion(f32[16,2,1350]{0,1,2:T(2,128)} %get-tuple-element.336, bf16[16,16,1350]{1,0,2:T(8,128)(2,1)} %copy.71, bf16[16,2,1350]{0,1,2:T(2,128)(2,1)S(1)} %copy.72), kind=kOutput, calls=%fused_computation.4.clone.1 | convolution fusion | flops 1425600 | bytes 1123200 | tf_op jit(solution)/shard_map/while/body/eval_jaxpr/pqk,qck->pck/dot_general | solution.py:124
  372.0 2.9 fusion.180
  379.4 2.2 fusion.17
  381.7 2.4 multiply_bitcast_fusion
  384.1 2.8 copy.58
  386.9 77.9 %reduce-scatter.5.cloned.1.call-done = f32[16,18,150]{2,0,1:T(8,128)} async-done(((f32[16,144,150]{2,0,1:T(8,128)}), f32[16,18,150]{2,0,1:T(8,128)}) %reduce-scatter.5.cloned.1.call-update) | async-done | bytes 172816 | tf_op jit(solution)/shard_map/reduce_scatter | solution.py:136
  (139 shorter events, 40.4 us)
Async XLA Ops:
  6.5 32.7 %copy-start = (bf16[17,2,2176]{2,1,0:T(2,128)(2,1)S(1)}, bf16[17,2,2176]{2,1,0:T(2,128)(2,1)}, u32[]{:S(2)}) copy-start(bf16[17,2,2176]{2,1,0:T(2,128)(2,1)} %param.12) | copy-start | bytes 443908
  6.5 109.9 %reduce-scatter.3.cloned.1.call-start = ((), (), s32[]{:S(2)}) async-start(), calls=%async_computation.3 | async-start | bytes 1622016 | tf_op jit(solution)/shard_map/reduce_scatter | solution.py:99
  39.2 16.2 %copy-start.2 = (s32[2176]{0:T(1024)S(1)}, s32[2176]{0:T(1024)}, u32[]{:S(2)}) copy-start(s32[2176]{0:T(1024)} %param.14) | copy-start | bytes 26116
  48.2 9.5 %copy-start.4 = (s32[16]{0:T(128)S(1)}, s32[16]{0:T(128)}, u32[]{:S(2)}) copy-start(s32[16]{0:T(128)} %param.15) | copy-start | bytes 196
  48.2 9.8 %copy-start.3 = (s32[256]{0:T(256)S(1)}, s32[256]{0:T(256)}, u32[]{:S(2)}) copy-start(s32[256]{0:T(256)} %constant.223) | copy-start | bytes 3076
  49.1 18.4 %all-to-all-start = ((bf16[16,2,272]{2,1,0:T(2,128)(2,1)}), bf16[16,2,272]{2,1,0:T(2,128)(2,1)S(1)}, u32[]{:S(2)}, u32[]{:S(2)}) async-start(bf16[16,2,272]{2,1,0:T(2,128)(2,1)} %reshape.372), calls=%async_computation.1 | async-start | bytes 49152 | tf_op jit(solution)/shard_map/all_to_all | solution.py:104
  55.0 409.7 %reduce-scatter.5.cloned.1.call-start = ((), (), s32[]{:S(2)}) async-start(), calls=%async_computation.4 | async-start | bytes 2654208 | tf_op jit(solution)/shard_map/reduce_scatter | solution.py:136
  125.0 7.7 %collective-permute-start = (bf16[16,2,1350]{2,0,1:T(8,128)(2,1)S(1)}, bf16[16,2,1350]{2,0,1:T(8,128)(2,1)S(1)}, u32[]{:S(2)}, u32[]{:S(2)}) collective-permute-start(bf16[16,2,1350]{2,0,1:T(8,128)(2,1)S(1)} %get-tuple-element.337), channel_id=1, source_target_pairs={{120,0},{0,8},{8,16},{16,24},{24,32},{32,40},{40,48},{48,56},{56,6... | collective-permute-start | bytes 259208 | tf_op jit(solution)/shard_map/while/body/eval_jaxpr/ppermute | solution.py:19
  140.8 9.4 %collective-permute-start = (bf16[16,2,1350]{2,0,1:T(8,128)(2,1)S(1)}, bf16[16,2,1350]{2,0,1:T(8,128)(2,1)S(1)}, u32[]{:S(2)}, u32[]{:S(2)}) collective-permute-start(bf16[16,2,1350]{2,0,1:T(8,128)(2,1)S(1)} %get-tuple-element.337), channel_id=1, source_target_pairs={{120,0},{0,8},{8,16},{16,24},{24,32},{32,40},{40,48},{48,56},{56,6... | collective-permute-start | bytes 259208 | tf_op jit(solution)/shard_map/while/body/eval_jaxpr/ppermute | solution.py:19
  158.2 7.9 %collective-permute-start = (bf16[16,2,1350]{2,0,1:T(8,128)(2,1)S(1)}, bf16[16,2,1350]{2,0,1:T(8,128)(2,1)S(1)}, u32[]{:S(2)}, u32[]{:S(2)}) collective-permute-start(bf16[16,2,1350]{2,0,1:T(8,128)(2,1)S(1)} %get-tuple-element.337), channel_id=1, source_target_pairs={{120,0},{0,8},{8,16},{16,24},{24,32},{32,40},{40,48},{48,56},{56,6... | collective-permute-start | bytes 259208 | tf_op jit(solution)/shard_map/while/body/eval_jaxpr/ppermute | solution.py:19
  174.0 9.3 %collective-permute-start = (bf16[16,2,1350]{2,0,1:T(8,128)(2,1)S(1)}, bf16[16,2,1350]{2,0,1:T(8,128)(2,1)S(1)}, u32[]{:S(2)}, u32[]{:S(2)}) collective-permute-start(bf16[16,2,1350]{2,0,1:T(8,128)(2,1)S(1)} %get-tuple-element.337), channel_id=1, source_target_pairs={{120,0},{0,8},{8,16},{16,24},{24,32},{32,40},{40,48},{48,56},{56,6... | collective-permute-start | bytes 259208 | tf_op jit(solution)/shard_map/while/body/eval_jaxpr/ppermute | solution.py:19
  191.4 7.9 %collective-permute-start = (bf16[16,2,1350]{2,0,1:T(8,128)(2,1)S(1)}, bf16[16,2,1350]{2,0,1:T(8,128)(2,1)S(1)}, u32[]{:S(2)}, u32[]{:S(2)}) collective-permute-start(bf16[16,2,1350]{2,0,1:T(8,128)(2,1)S(1)} %get-tuple-element.337), channel_id=1, source_target_pairs={{120,0},{0,8},{8,16},{16,24},{24,32},{32,40},{40,48},{48,56},{56,6... | collective-permute-start | bytes 259208 | tf_op jit(solution)/shard_map/while/body/eval_jaxpr/ppermute | solution.py:19
  207.2 9.1 %collective-permute-start = (bf16[16,2,1350]{2,0,1:T(8,128)(2,1)S(1)}, bf16[16,2,1350]{2,0,1:T(8,128)(2,1)S(1)}, u32[]{:S(2)}, u32[]{:S(2)}) collective-permute-start(bf16[16,2,1350]{2,0,1:T(8,128)(2,1)S(1)} %get-tuple-element.337), channel_id=1, source_target_pairs={{120,0},{0,8},{8,16},{16,24},{24,32},{32,40},{40,48},{48,56},{56,6... | collective-permute-start | bytes 259208 | tf_op jit(solution)/shard_map/while/body/eval_jaxpr/ppermute | solution.py:19
  224.3 7.9 %collective-permute-start = (bf16[16,2,1350]{2,0,1:T(8,128)(2,1)S(1)}, bf16[16,2,1350]{2,0,1:T(8,128)(2,1)S(1)}, u32[]{:S(2)}, u32[]{:S(2)}) collective-permute-start(bf16[16,2,1350]{2,0,1:T(8,128)(2,1)S(1)} %get-tuple-element.337), channel_id=1, source_target_pairs={{120,0},{0,8},{8,16},{16,24},{24,32},{32,40},{40,48},{48,56},{56,6... | collective-permute-start | bytes 259208 | tf_op jit(solution)/shard_map/while/body/eval_jaxpr/ppermute | solution.py:19
  240.2 8.5 %collective-permute-start = (bf16[16,2,1350]{2,0,1:T(8,128)(2,1)S(1)}, bf16[16,2,1350]{2,0,1:T(8,128)(2,1)S(1)}, u32[]{:S(2)}, u32[]{:S(2)}) collective-permute-start(bf16[16,2,1350]{2,0,1:T(8,128)(2,1)S(1)} %get-tuple-element.337), channel_id=1, source_target_pairs={{120,0},{0,8},{8,16},{16,24},{24,32},{32,40},{40,48},{48,56},{56,6... | collective-permute-start | bytes 259208 | tf_op jit(solution)/shard_map/while/body/eval_jaxpr/ppermute | solution.py:19
  256.7 7.9 %collective-permute-start = (bf16[16,2,1350]{2,0,1:T(8,128)(2,1)S(1)}, bf16[16,2,1350]{2,0,1:T(8,128)(2,1)S(1)}, u32[]{:S(2)}, u32[]{:S(2)}) collective-permute-start(bf16[16,2,1350]{2,0,1:T(8,128)(2,1)S(1)} %get-tuple-element.337), channel_id=1, source_target_pairs={{120,0},{0,8},{8,16},{16,24},{24,32},{32,40},{40,48},{48,56},{56,6... | collective-permute-start | bytes 259208 | tf_op jit(solution)/shard_map/while/body/eval_jaxpr/ppermute | solution.py:19
  272.6 9.3 %collective-permute-start = (bf16[16,2,1350]{2,0,1:T(8,128)(2,1)S(1)}, bf16[16,2,1350]{2,0,1:T(8,128)(2,1)S(1)}, u32[]{:S(2)}, u32[]{:S(2)}) collective-permute-start(bf16[16,2,1350]{2,0,1:T(8,128)(2,1)S(1)} %get-tuple-element.337), channel_id=1, source_target_pairs={{120,0},{0,8},{8,16},{16,24},{24,32},{32,40},{40,48},{48,56},{56,6... | collective-permute-start | bytes 259208 | tf_op jit(solution)/shard_map/while/body/eval_jaxpr/ppermute | solution.py:19
  289.9 7.9 %collective-permute-start = (bf16[16,2,1350]{2,0,1:T(8,128)(2,1)S(1)}, bf16[16,2,1350]{2,0,1:T(8,128)(2,1)S(1)}, u32[]{:S(2)}, u32[]{:S(2)}) collective-permute-start(bf16[16,2,1350]{2,0,1:T(8,128)(2,1)S(1)} %get-tuple-element.337), channel_id=1, source_target_pairs={{120,0},{0,8},{8,16},{16,24},{24,32},{32,40},{40,48},{48,56},{56,6... | collective-permute-start | bytes 259208 | tf_op jit(solution)/shard_map/while/body/eval_jaxpr/ppermute | solution.py:19
  305.8 9.4 %collective-permute-start = (bf16[16,2,1350]{2,0,1:T(8,128)(2,1)S(1)}, bf16[16,2,1350]{2,0,1:T(8,128)(2,1)S(1)}, u32[]{:S(2)}, u32[]{:S(2)}) collective-permute-start(bf16[16,2,1350]{2,0,1:T(8,128)(2,1)S(1)} %get-tuple-element.337), channel_id=1, source_target_pairs={{120,0},{0,8},{8,16},{16,24},{24,32},{32,40},{40,48},{48,56},{56,6... | collective-permute-start | bytes 259208 | tf_op jit(solution)/shard_map/while/body/eval_jaxpr/ppermute | solution.py:19
  323.2 7.9 %collective-permute-start = (bf16[16,2,1350]{2,0,1:T(8,128)(2,1)S(1)}, bf16[16,2,1350]{2,0,1:T(8,128)(2,1)S(1)}, u32[]{:S(2)}, u32[]{:S(2)}) collective-permute-start(bf16[16,2,1350]{2,0,1:T(8,128)(2,1)S(1)} %get-tuple-element.337), channel_id=1, source_target_pairs={{120,0},{0,8},{8,16},{16,24},{24,32},{32,40},{40,48},{48,56},{56,6... | collective-permute-start | bytes 259208 | tf_op jit(solution)/shard_map/while/body/eval_jaxpr/ppermute | solution.py:19
  339.0 9.0 %collective-permute-start = (bf16[16,2,1350]{2,0,1:T(8,128)(2,1)S(1)}, bf16[16,2,1350]{2,0,1:T(8,128)(2,1)S(1)}, u32[]{:S(2)}, u32[]{:S(2)}) collective-permute-start(bf16[16,2,1350]{2,0,1:T(8,128)(2,1)S(1)} %get-tuple-element.337), channel_id=1, source_target_pairs={{120,0},{0,8},{8,16},{16,24},{24,32},{32,40},{40,48},{48,56},{56,6... | collective-permute-start | bytes 259208 | tf_op jit(solution)/shard_map/while/body/eval_jaxpr/ppermute | solution.py:19
  356.1 7.9 %collective-permute-start = (bf16[16,2,1350]{2,0,1:T(8,128)(2,1)S(1)}, bf16[16,2,1350]{2,0,1:T(8,128)(2,1)S(1)}, u32[]{:S(2)}, u32[]{:S(2)}) collective-permute-start(bf16[16,2,1350]{2,0,1:T(8,128)(2,1)S(1)} %get-tuple-element.337), channel_id=1, source_target_pairs={{120,0},{0,8},{8,16},{16,24},{24,32},{32,40},{40,48},{48,56},{56,6... | collective-permute-start | bytes 259208 | tf_op jit(solution)/shard_map/while/body/eval_jaxpr/ppermute | solution.py:19
  384.1 82.7 %copy-start.1 = (bf16[17,2,2176]{2,1,0:T(2,128)(2,1)S(1)}, bf16[17,2,2176]{2,1,0:T(2,128)(2,1)}, u32[]{:S(2)}) copy-start(bf16[17,2,2176]{2,1,0:T(2,128)(2,1)} %param.12) | copy-start | bytes 443908
Sparse Core Ops, SparseCore 0:
  39.3 77.0 reduce-scatter.2
  387.0 77.7 reduce-scatter.4
where the time goes:
time: 483 us; the launch traced here: 474 us
  local copies, waits for them, and re-layouts  169 us (35%)
  matrix products  145 us (30%)
  waiting for transfers between devices  126 us (26%)
  starting transfers between devices  16.7 us (3%)
  between operations  13.9 us (3%)
    gather x32, local copies, waits for them, and re-layouts, gather_terms(): toeplitz = window[offsets]  123 us
    dot_general x16, matrix products, gather_terms(): jnp.einsum('pqk,qck->pck', toeplitz, source, preferred_element_type=jnp.f...  113 us
    reduce_scatter x1, waiting for transfers between devices, per_device(): lax.psum_scatter(grid_terms, 'freq', scatter_dimension=1, tiled=True)  77.9 us
    reduce_scatter x1, waiting for transfers between devices, per_device(): lax.psum_scatter(terms, 'freq', scatter_dimension=0, tiled=True)[0]  48 us
    ppermute x15, local copies, waits for them, and re-layouts, passed_along(): return lax.ppermute(block, axis, route)  13.4 us
    ppermute x15, starting transfers between devices, passed_along(): return lax.ppermute(block, axis, route)  10.7 us
  transfers between devices with their start and end apart: 18, of which 2 were waited for; matrix products, arithmetic and copies ran while one was open for 29% of the time, Pallas kernels for 0%

commit v1 on v0

--- a/solution.py
+++ b/solution.py
@@ -3,6 +3,8 @@
 import numpy as np
 from jax import lax
 from jax.sharding import PartitionSpec as P
+from jax.experimental import pallas as pl
+from jax.experimental.pallas import tpu as pltpu
 
 L = 21600
 PA = 144
@@ -11,12 +13,6 @@
 
 
 highest = lax.Precision.HIGHEST
-
-
-def passed_along(block, axis, distance):
-    devices = range(lax.axis_size(axis))
-    route = [((i - distance) % len(devices), i) for i in devices]
-    return lax.ppermute(block, axis, route)
 
 
 def angle_table(first, second, period):
@@ -87,6 +83,62 @@
     return grid * (2.0 / L) ** 0.5
 
 
+LANE = 128
+
+
+def stokes_body(k_ref, w_ref, o_ref, sh_ref):
+    shifts = sh_ref.shape[0]
+    span = sh_ref.shape[1]
+    steps = w_ref.shape[1] // shifts
+    width = o_ref.shape[1]
+    for r in range(shifts):
+        sh_ref[r] = k_ref[pl.ds(r, span), :]
+
+    def step(a, carry):
+        acc_re, acc_im = carry
+        base = pl.multiple_of(a * shifts, shifts)
+        w_re = w_ref[0, pl.ds(base, shifts), :]
+        w_im = w_ref[1, pl.ds(base, shifts), :]
+        for r in range(shifts):
+            slab = sh_ref[r, pl.ds(base, width), :]
+            acc_re = acc_re + slab * w_re[r : r + 1, :]
+            acc_im = acc_im + slab * w_im[r : r + 1, :]
+        return acc_re, acc_im
+
+    zero = jnp.zeros(o_ref.shape[1:], jnp.float32)
+    acc_re, acc_im = lax.fori_loop(0, steps, step, (zero, zero))
+    o_ref[0] = acc_re
+    o_ref[1] = acc_im
+
+
+def toeplitz_stokes(kernel, weighted, block_self, rows, blocks):
+    total_rows = rows * blocks
+    width = kernel.shape[1]
+    padded = -(-width // LANE) * LANE
+    shifts = 8
+    everyone = lax.all_gather(weighted, "lat", axis=0, tiled=True)
+    first = (blocks - 1 - block_self) * rows
+    used = total_rows + rows - 1
+    window = lax.dynamic_slice_in_dim(kernel, first, used, 0).astype(jnp.float32)
+    window = jnp.pad(window, ((0, -used % shifts), (0, padded - width)))
+    source = jnp.pad(
+        everyone.astype(jnp.float32).transpose(1, 0, 2), ((0, 0), (0, 0), (0, padded - width))
+    )
+    span = total_rows + shifts
+    out = pl.pallas_call(
+        stokes_body,
+        grid=(padded // LANE,),
+        in_specs=[
+            pl.BlockSpec((window.shape[0], LANE), lambda j: (0, j)),
+            pl.BlockSpec((2, total_rows, LANE), lambda j: (0, 0, j)),
+        ],
+        out_specs=pl.BlockSpec((2, rows, LANE), lambda j: (0, 0, j)),
+        out_shape=jax.ShapeDtypeStruct((2, rows, padded), jnp.float32),
+        scratch_shapes=[pltpu.VMEM((shifts, span, LANE), jnp.float32)],
+    )(window, source)
+    return out[:, ::-1, :width].transpose(1, 0, 2)
+
+
 def per_device(gravity, coef, legendre, order_table, band_rows, kernel):
     bands = lax.axis_size("freq")
     blocks = lax.axis_size("lat")
@@ -114,24 +166,7 @@
     model = jnp.einsum("jcr,jt->rct", routed, selector, preferred_element_type=jnp.float32)
     weight = jnp.cos((20.0 + band_rows.astype(jnp.float32) / 60.0) * (np.pi / 180.0))
     weighted = ((observed - model) * weight[:, None, None]).astype(jnp.bfloat16)
-    total_rows = rows * blocks
-    offsets = np.arange(rows)[None, :] - np.arange(rows)[:, None] + rows - 1
-
-    def gather_terms(source, owner):
-        first = (owner - block_self) * rows + total_rows - rows
-        window = lax.dynamic_slice_in_dim(kernel, first, 2 * rows - 1, 0)
-        toeplitz = window[offsets]
-        return jnp.einsum("pqk,qck->pck", toeplitz, source, preferred_element_type=jnp.float32)
-
-    stokes = gather_terms(weighted, block_self)
-
-    def advance(count, carry):
-        total, moving = carry
-        moving = passed_along(moving, "lat", 1)
-        owner = (block_self - count) % blocks
-        return (total + gather_terms(moving, owner), moving)
-
-    stokes, carried = lax.fori_loop(1, blocks, advance, (stokes, weighted))
+    stokes = toeplitz_stokes(kernel, weighted, block_self, rows, blocks)
     grid_terms = inverse_rows(stokes[None], jnp.reshape(band_self, (1,)), bands)
     geoid = lax.psum_scatter(grid_terms, "freq", scatter_dimension=1, tiled=True)
     return geoid.reshape(rows, span * PB)

time: 483 us -> 269 us (0.56); the launches traced: 474 us -> 268 us
  local copies, waits for them, and re-layouts: 169 us -> 32.4 us
  matrix products: 145 us -> 33.5 us
  waiting for transfers between devices: 126 us -> 165 us
  starting transfers between devices: 16.7 us -> 5.95 us
  Pallas kernels: 0 us -> 10 us
  other arithmetic: 2.31 us -> 8.67 us
    gather x32 -> x0, local copies, waits for them, and re-layouts: 123 us -> none  [gather_terms(): toeplitz = window[offsets]]
    dot_general x16 -> x0, matrix products: 113 us -> none  [gather_terms(): jnp.einsum('pqk,qck->pck', toeplitz, source, preferred_element_type=jnp.f...]
    all_gather x0 -> x1, waiting for transfers between devices: none -> 28.3 us  [toeplitz_stokes(): everyone = lax.all_gather(weighted, 'lat', axis=0, tiled=True)]
    ppermute x15 -> x0, local copies, waits for them, and re-layouts: 13.4 us -> none  [passed_along(): return lax.ppermute(block, axis, route)]
    ppermute x15 -> x0, starting transfers between devices: 10.7 us -> none  [passed_along(): return lax.ppermute(block, axis, route)]
    pallas_call x0 -> x1, Pallas kernels: none -> 10 us  [toeplitz_stokes(): pl.pallas_call(stokes_body, grid=(padded // LANE,), in_specs=[pl.BlockSpe...]
    reduce_scatter x1, waiting for transfers between devices: 48 us -> 54.4 us  [per_device(): lax.psum_scatter(terms, 'freq', scatter_dimension=0, tiled=True)[0]]
  transfers between devices with their start and end apart: 18 -> 4, of which waited for: 2 -> 4; matrix products, arithmetic and copies ran while one was open for 29% -> 6% of each run, Pallas kernels for 0% -> 0%
where the time goes in v1:
time: 269 us; the launch traced here: 268 us
  waiting for transfers between devices  165 us (61%)
  matrix products  33.5 us (12%)
  local copies, waits for them, and re-layouts  32.4 us (12%)
  between operations  13.4 us (5%)
  Pallas kernels  10 us (4%)
  other arithmetic  8.67 us (3%)
  starting transfers between devices  5.95 us (2%)
    reduce_scatter x1, waiting for transfers between devices, per_device(): lax.psum_scatter(grid_terms, 'freq', scatter_dimension=1, tiled=True)  78.3 us
    reduce_scatter x1, waiting for transfers between devices, per_device(): lax.psum_scatter(terms, 'freq', scatter_dimension=0, tiled=True)[0]  54.4 us
    all_gather x1, waiting for transfers between devices, toeplitz_stokes(): everyone = lax.all_gather(weighted, 'lat', axis=0, tiled=True)  28.3 us
    pallas_call x1, Pallas kernels, toeplitz_stokes(): pl.pallas_call(stokes_body, grid=(padded // LANE,), in_specs=[pl.BlockSpe...  10 us
    dot_general x1, matrix products, per_device(): jnp.einsum('ocn,onq->ocq', coef, legendre, preferred_element_type=jnp.flo...  8.94 us
    reshape x1, local copies, waits for them, and re-layouts, forward_bands(): return stacked.reshape(bands, rows, 2, PH * span)  8 us
    transpose x1, local copies, waits for them, and re-layouts, forward_bands(): stacked = stacked.reshape(2, rows, span, bands, PH).transpose(3, 1, 0, 4, 2)  7.99 us
    all_to_all x1, starting transfers between devices, per_device(): lax.all_to_all(synth, 'lat', split_axis=2, concat_axis=0, tiled=True)  5.87 us
  transfers between devices with their start and end apart: 4, of which 4 were waited for; matrix products, arithmetic and copies ran while one was open for 6% of the time, Pallas kernels for 0%

profile of v1, /device:TPU:0, one launch (start us, length us, event | category | flops | bytes accessed | tf_op | source)
XLA Modules:
  0.0 268.5 jit_solution(10244089903857552643)
XLA Ops:
  6.5 0.0 copy-start
  6.5 0.0 reduce-scatter.3.cloned.1.call-start
  6.5 1.2 reshape.291
  7.8 2.2 fusion.96
  10.0 2.2 fusion.98
  12.2 0.6 fusion.32
  12.8 2.4 fusion.13
  15.3 2.4 fusion.9
  17.7 2.6 fusion.5
  20.3 2.4 fusion.4
  22.8 1.7 fusion
  24.5 8.0 %copy.29 = f32[8,16,2,75,18]{4,3,1,2,0:T(8,128)} copy(f32[8,16,2,75,18]{3,0,4,1,2:T(8,128)} %fusion) | data formatting | bytes 2764800 | tf_op jit(solution)/shard_map/transpose | solution.py:50
  32.5 0.0 copy-start.2
  32.5 8.0 %reshape.292 = f32[8,16,2,1350]{3,1,2,0:T(8,128)} reshape(f32[8,16,2,75,18]{4,3,1,2,0:T(8,128)} %copy.29) | data formatting | bytes 2764800 | tf_op jit(solution)/shard_map/reshape | solution.py:51
  40.5 0.0 reduce-scatter.3.cloned.1.call-update
  40.5 0.0 copy-done.2
  40.5 0.0 copy-start.1
  40.5 8.9 %convolution_convert_fusion = bf16[17,2,256]{2,1,0:T(2,128)(2,1)S(1)} fusion(bf16[17,2,2176]{2,1,0:T(2,128)(2,1)S(1)} %copy-done.2, bf16[17,2176,256]{2,1,0:T(8,128)(2,1)} %param.8), kind=kOutput, calls=%fused_computation.19 | convolution fusion | flops 37888512 | bytes 19105280 | tf_op jit(solution)/shard_map/ocn,onq->ocq/dot_general | solution.py:153
  49.5 0.0 copy-start.3
  49.5 0.2 copy.30
  49.6 0.8 reshape.316
  50.4 5.9 %all-to-all-start = ((bf16[16,2,272]{2,1,0:T(2,128)(2,1)}), bf16[16,2,272]{2,1,0:T(2,128)(2,1)S(1)}, u32[]{:S(2)}, u32[]{:S(2)}) async-start(bf16[16,2,272]{2,1,0:T(2,128)(2,1)} %reshape.316), calls=%async_computation.1 | async-start | bytes 49152 | tf_op jit(solution)/shard_map/all_to_all | solution.py:156
  56.3 0.0 all-gather.2.cloned.1.call-start
  56.4 0.1 iota_add_fusion
  56.4 0.1 add.204
  56.6 0.0 copy-done.1
  56.6 2.2 gather_fusion
  58.8 0.0 copy-done.3
  58.9 3.5 %all-to-all-done = bf16[16,2,272]{2,1,0:T(2,128)(2,1)S(1)} async-done(((bf16[16,2,272]{2,1,0:T(2,128)(2,1)}), bf16[16,2,272]{2,1,0:T(2,128)(2,1)S(1)}, u32[]{:S(2)}, u32[]{:S(2)}) %all-to-all-start) | async-done | bytes 17440 | tf_op jit(solution)/shard_map/all_to_all | solution.py:156
  62.4 0.2 reshape.317
  62.6 0.1 copy.43
  62.6 0.2 reshape.308
  62.8 0.4 fusion.3
  63.2 54.4 %reduce-scatter.3.cloned.1.call-done = f32[1,16,2,1350]{3,1,2,0:T(8,128)} async-done(((f32[8,16,2,1350]{3,1,2,0:T(8,128)}), f32[1,16,2,1350]{3,1,2,0:T(8,128)}) %reduce-scatter.3.cloned.1.call-update) | async-done | bytes 172816 | tf_op jit(solution)/shard_map/reduce_scatter | solution.py:151
  117.7 1.6 fusion.27
  119.3 0.0 all-gather.2.cloned.1.call-update
  119.3 0.0 reduce-scatter.5.cloned.1.call-start
  119.4 0.0 copy-done
  119.4 0.4 constant_dynamic-slice_fusion
  119.9 1.3 copy.39
  121.2 0.2 fusion.105
  121.4 1.2 pad_convert_fusion.1.k_ref
  122.6 28.3 %all-gather.2.cloned.1.call-done = bf16[256,2,1350]{2,0,1:T(8,128)(2,1)} async-done(((bf16[16,2,1350]{2,0,1:T(8,128)(2,1)}), bf16[256,2,1350]{2,0,1:T(8,128)(2,1)}) %all-gather.2.cloned.1.call-update) | async-done | bytes 1382416 | tf_op jit(solution)/shard_map/all_gather | solution.py:119
  150.9 3.1 %pad_convert_fusion.w_ref = f32[2,256,1408]{2,1,0:T(8,128)} fusion(bf16[2,256,1350]{2,1,0:T(8,128)(2,1)} %bitcast.106), kind=kLoop, calls=%fused_computation.12 | loop fusion | flops 720896 | bytes 4265984 | tf_op jit(solution)/shard_map/jit(_pad)/pad | solution.py:124
  154.0 10.0 %shard_map.64 = f32[2,16,1408]{2,1,0:T(8,128)} custom-call(f32[272,1408]{1,0:T(8,128)} %pad_convert_fusion.1.k_ref, f32[2,256,1408]{2,1,0:T(8,128)} %pad_convert_fusion.w_ref), custom_call_target="tpu_custom_call" | custom-call | tf_op jit(solution)/shard_map/pallas_call | solution.py:128
  164.0 4.3 %rev.3 = f32[2,16,1350]{2,1,0:T(8,128)S(1)} reverse(f32[2,16,1350]{2,1,0:T(8,128)} %bitcast.107), dimensions={1} | reverse | bytes 345600 | tf_op jit(solution)/shard_map/rev | solution.py:139
  168.4 0.7 reshape_broadcast_in_dim.3
  169.0 1.3 fusion.7
  170.3 1.3 fusion.8
  171.6 1.3 convolution_subtract_fusion.1
  172.9 1.3 convolution_add_fusion.1
  174.2 2.2 fusion.18
  176.5 2.4 multiply_bitcast_fusion
  178.9 2.8 %copy.35 = f32[16,144,150]{2,0,1:T(8,128)} copy(f32[16,144,150]{2,1,0:T(8,128)S(1)} %multiply_bitcast_fusion) | data formatting | bytes 2764800 | tf_op jit(solution)/shard_map/mul | solution.py:83
  181.6 0.0 reduce-scatter.5.cloned.1.call-update
  181.7 78.3 %reduce-scatter.5.cloned.1.call-done = f32[16,18,150]{2,0,1:T(8,128)} async-done(((f32[16,144,150]{2,0,1:T(8,128)}), f32[16,18,150]{2,0,1:T(8,128)}) %reduce-scatter.5.cloned.1.call-update) | async-done | bytes 172816 | tf_op jit(solution)/shard_map/reduce_scatter | solution.py:171
  259.9 1.1 copy.36
  261.1 0.8 reshape.295
  (7 shorter events, 0.1 us)
Async XLA Ops:
  6.5 112.9 %copy-start = (bf16[511,1350]{0,1:T(8,128)(2,1)S(1)}, bf16[511,1350]{0,1:T(8,128)(2,1)}, u32[]{:S(2)}) copy-start(bf16[511,1350]{0,1:T(8,128)(2,1)} %param.11) | copy-start | bytes 4139104
  6.5 111.1 %reduce-scatter.3.cloned.1.call-start = ((), (), s32[]{:S(2)}) async-start(), calls=%async_computation.3 | async-start | bytes 1622016 | tf_op jit(solution)/shard_map/reduce_scatter | solution.py:151
  32.5 8.0 %copy-start.2 = (bf16[17,2,2176]{2,1,0:T(2,128)(2,1)S(1)}, bf16[17,2,2176]{2,1,0:T(2,128)(2,1)}, u32[]{:S(2)}) copy-start(bf16[17,2,2176]{2,1,0:T(2,128)(2,1)} %param.7) | copy-start | bytes 443908
  40.5 16.1 %copy-start.1 = (s32[2176]{0:T(1024)S(1)}, s32[2176]{0:T(1024)}, u32[]{:S(2)}) copy-start(s32[2176]{0:T(1024)} %param.9) | copy-start | bytes 26116
  49.5 9.4 %copy-start.3 = (s32[16]{0:T(128)S(1)}, s32[16]{0:T(128)}, u32[]{:S(2)}) copy-start(s32[16]{0:T(128)} %param.10) | copy-start | bytes 196
  50.4 12.0 %all-to-all-start = ((bf16[16,2,272]{2,1,0:T(2,128)(2,1)}), bf16[16,2,272]{2,1,0:T(2,128)(2,1)S(1)}, u32[]{:S(2)}, u32[]{:S(2)}) async-start(bf16[16,2,272]{2,1,0:T(2,128)(2,1)} %reshape.316), calls=%async_computation.1 | async-start | bytes 49152 | tf_op jit(solution)/shard_map/all_to_all | solution.py:156
  56.3 94.6 %all-gather.2.cloned.1.call-start = ((), (), s32[]{:S(2)}) async-start(), calls=%async_computation.4 | async-start | bytes 1531904 | tf_op jit(solution)/shard_map/all_gather | solution.py:119
  119.3 140.6 %reduce-scatter.5.cloned.1.call-start = ((), (), s32[]{:S(2)}) async-start(), calls=%async_computation.5 | async-start | bytes 2654208 | tf_op jit(solution)/shard_map/reduce_scatter | solution.py:171
Sparse Core Ops, SparseCore 0:
  40.6 77.0 reduce-scatter.2
  119.5 31.3 all-gather.1
  181.8 78.1 reduce-scatter.4

commit v2 on v1

--- a/solution.py
+++ b/solution.py
@@ -145,10 +145,9 @@
     band_self = lax.axis_index("freq")
     block_self = lax.axis_index("lat")
     rows = gravity.shape[0]
-    span = PA // bands
-    local_grid = gravity.reshape(rows, span, PB)
-    terms = forward_bands(local_grid, band_self * span, bands)
-    observed = lax.psum_scatter(terms, "freq", scatter_dimension=0, tiled=True)[0]
+    whole_rows = lax.all_to_all(gravity, "freq", split_axis=0, concat_axis=1, tiled=True)
+    terms = forward_bands(whole_rows.reshape(rows // bands, PA, PB), 0, bands)
+    observed = lax.all_to_all(terms, "freq", split_axis=0, concat_axis=1, tiled=True)[0]
     band_width = observed.shape[2]
     synth = jnp.einsum("ocn,onq->ocq", coef, legendre, preferred_element_type=jnp.float32).astype(
         jnp.bfloat16
@@ -167,9 +166,10 @@
     weight = jnp.cos((20.0 + band_rows.astype(jnp.float32) / 60.0) * (np.pi / 180.0))
     weighted = ((observed - model) * weight[:, None, None]).astype(jnp.bfloat16)
     stokes = toeplitz_stokes(kernel, weighted, block_self, rows, blocks)
-    grid_terms = inverse_rows(stokes[None], jnp.reshape(band_self, (1,)), bands)
-    geoid = lax.psum_scatter(grid_terms, "freq", scatter_dimension=1, tiled=True)
-    return geoid.reshape(rows, span * PB)
+    by_band = lax.all_to_all(stokes[None], "freq", split_axis=1, concat_axis=0, tiled=True)
+    grid_rows = inverse_rows(by_band, jnp.arange(bands, dtype=jnp.int32), bands)
+    geoid = lax.all_to_all(grid_rows.reshape(rows // bands, L), "freq", split_axis=1, concat_axis=0, tiled=True)
+    return geoid
 
 
 def solution(mesh):

time: 269 us -> 154 us (0.57)
  waiting for transfers between devices: 165 us -> 50.6 us
  starting transfers between devices: 5.95 us -> 23.6 us
  local copies, waits for them, and re-layouts: 32.4 us -> 15.1 us
  matrix products: 33.5 us -> 22.2 us
  blocking collectives: 0 us -> 10.9 us
    reduce_scatter x2 -> x0, waiting for transfers between devices: 133 us -> none  [the longest x1 78.3 us: per_device(): lax.psum_scatter(grid_terms, 'freq', scatter_dimension=1, tiled=True)]
    all_to_all x0 -> x3, waiting for transfers between devices: none -> 22.4 us  [the longest x1 7.63 us: per_device(): lax.all_to_all(terms, 'freq', split_axis=0, concat_axis=1, tiled=True)[0]]
    all_to_all x0 -> x3, starting transfers between devices: none -> 17.5 us  [the longest x1 7.49 us: per_device(): lax.all_to_all(gravity, 'freq', split_axis=0, concat_axis=1, tiled=True)]
    all_to_all x0 -> x1, blocking collectives: none -> 10.9 us  [per_device(): lax.all_to_all(grid_rows.reshape(rows // bands, L), 'freq', split_axis=1,...]
    transpose x1 -> x0, local copies, waits for them, and re-layouts: 7.99 us -> none  [forward_bands(): stacked = stacked.reshape(2, rows, span, bands, PH).transpose(3, 1, 0, 4, 2)]
    reshape x1 -> x2, local copies, waits for them, and re-layouts: 8 us -> 1.92 us  [forward_bands(): return stacked.reshape(bands, rows, 2, PH * span)]
    all_gather x1, waiting for transfers between devices: 28.3 us -> 25.4 us  [toeplitz_stokes(): everyone = lax.all_gather(weighted, 'lat', axis=0, tiled=True)]
    mul x1 -> x0, local copies, waits for them, and re-layouts: 2.79 us -> none  [inverse_rows(): return grid * (2.0 / L) ** 0.5]
  transfers between devices with their start and end apart: 4 -> 5, of which waited for: 4 -> 5; matrix products, arithmetic and copies ran while one was open for 6% -> 5% of each run, Pallas kernels for 0% -> 0%
where the time goes in v2:
time: 154 us; the launch traced here: 153 us
  waiting for transfers between devices  50.6 us (33%)
  starting transfers between devices  23.6 us (15%)
  matrix products  22.2 us (14%)
  local copies, waits for them, and re-layouts  15.1 us (10%)
  between operations  13.7 us (9%)
  blocking collectives  10.9 us (7%)
  Pallas kernels  10 us (6%)
  other arithmetic  6.79 us (4%)
    all_gather x1, waiting for transfers between devices, toeplitz_stokes(): everyone = lax.all_gather(weighted, 'lat', axis=0, tiled=True)  25.4 us
    all_to_all x1, blocking collectives, per_device(): lax.all_to_all(grid_rows.reshape(rows // bands, L), 'freq', split_axis=1,...  10.9 us
    pallas_call x1, Pallas kernels, toeplitz_stokes(): pl.pallas_call(stokes_body, grid=(padded // LANE,), in_specs=[pl.BlockSpe...  10 us
    dot_general x1, matrix products, per_device(): jnp.einsum('ocn,onq->ocq', coef, legendre, preferred_element_type=jnp.flo...  9.13 us
    all_to_all x1, waiting for transfers between devices, per_device(): lax.all_to_all(terms, 'freq', split_axis=0, concat_axis=1, tiled=True)[0]  7.63 us
    all_to_all x1, starting transfers between devices, per_device(): lax.all_to_all(gravity, 'freq', split_axis=0, concat_axis=1, tiled=True)  7.49 us
    all_to_all x1, waiting for transfers between devices, per_device(): lax.all_to_all(stokes[None], 'freq', split_axis=1, concat_axis=0, tiled=T...  7.47 us
    all_to_all x1, waiting for transfers between devices, per_device(): lax.all_to_all(gravity, 'freq', split_axis=0, concat_axis=1, tiled=True)  7.25 us
  transfers between devices with their start and end apart: 5, of which 5 were waited for; matrix products, arithmetic and copies ran while one was open for 5% of the time, Pallas kernels for 0%

profile of v2, /device:TPU:0, one launch (start us, length us, event | category | flops | bytes accessed | tf_op | source)
XLA Modules:
  0.0 152.8 jit_solution(17359751564203680055)
XLA Ops:
  6.5 0.0 copy-start
  6.5 9.1 %convolution_convert_fusion = bf16[17,2,256]{2,1,0:T(2,128)(2,1)S(1)} fusion(bf16[17,2,2176]{2,1,0:T(2,128)(2,1)} %param.7, bf16[17,2176,256]{2,1,0:T(8,128)(2,1)} %param.8), kind=kOutput, calls=%fused_computation.18 | convolution fusion | flops 37888512 | bytes 19105280 | tf_op jit(solution)/shard_map/ocn,onq->ocq/dot_general | solution.py:152
  15.7 0.0 copy-start.1
  15.7 0.0 copy-start.2
  15.7 0.2 copy.47
  15.8 0.8 reshape.184
  16.6 5.9 %all-to-all-start.2 = ((bf16[16,2,272]{2,1,0:T(2,128)(2,1)}), bf16[16,2,272]{2,1,0:T(2,128)(2,1)S(1)}, u32[]{:S(2)}, u32[]{:S(2)}) async-start(bf16[16,2,272]{2,1,0:T(2,128)(2,1)} %reshape.184), calls=%async_computation.2 | async-start | bytes 49152 | tf_op jit(solution)/shard_map/all_to_all | solution.py:155
  22.5 0.0 copy-start.3
  22.5 0.1 iota_add_fusion
  22.6 0.1 add.215
  22.7 0.0 copy-done.1
  22.7 2.2 %gather_fusion = s32[272]{0:T(512)S(1)} fusion(s32[2176]{0:T(1024)S(1)} %copy-done.1, s32[1024]{0:T(1024)S(1)} %pad_clamp_fusion), kind=kCustom, calls=%fused_computation | custom fusion | bytes 3264 | tf_op jit(solution)/shard_map/gather | solution.py:161
  25.0 0.0 copy-done.2
  25.0 0.8 all_to_all.53
  25.8 2.8 %all-to-all-done.2 = bf16[16,2,272]{2,1,0:T(2,128)(2,1)S(1)} async-done(((bf16[16,2,272]{2,1,0:T(2,128)(2,1)}), bf16[16,2,272]{2,1,0:T(2,128)(2,1)S(1)}, u32[]{:S(2)}, u32[]{:S(2)}) %all-to-all-start.2) | async-done | bytes 17440 | tf_op jit(solution)/shard_map/all_to_all | solution.py:155
  28.6 7.5 %all-to-all-start = ((f32[8,2,2700]{2,1,0:T(2,128)}), f32[8,2,2700]{2,1,0:T(2,128)S(1)}, u32[]{:S(2)}, u32[]{:S(2)}) async-start(f32[8,2,2700]{2,1,0:T(2,128)} %all_to_all.53), calls=%async_computation | async-start | bytes 360448 | tf_op jit(solution)/shard_map/all_to_all | solution.py:148
  36.1 0.0 copy-done.3
  36.1 0.6 fusion.50
  36.8 0.2 reshape.185
  37.0 0.1 copy.77
  37.0 0.2 reshape.172
  37.2 7.3 %all-to-all-done = f32[8,2,2700]{2,1,0:T(2,128)S(1)} async-done(((f32[8,2,2700]{2,1,0:T(2,128)}), f32[8,2,2700]{2,1,0:T(2,128)S(1)}, u32[]{:S(2)}, u32[]{:S(2)}) %all-to-all-start) | async-done | bytes 172832 | tf_op jit(solution)/shard_map/all_to_all | solution.py:148
  44.5 0.1 reshape.157
  44.6 1.0 convolution_bitcast_fusion.2
  45.6 1.0 fusion.1
  46.6 0.7 fusion.77
  47.3 0.7 fusion.79
  48.0 0.7 fusion.5
  48.8 0.7 fusion.6
  49.5 0.5 copy.61
  50.0 1.4 reshape.180
  51.4 3.4 %all-to-all-start.1 = ((f32[8,2,2,1350]{3,2,1,0:T(2,128)}), f32[8,2,2,1350]{3,2,1,0:T(2,128)S(1)}, u32[]{:S(2)}, u32[]{:S(2)}) async-start(f32[8,2,2,1350]{3,2,1,0:T(2,128)} %reshape.180), calls=%async_computation.1 | async-start | bytes 360448 | tf_op jit(solution)/shard_map/all_to_all | solution.py:150
  54.8 0.2 all-gather.2.cloned.1.call-start
  55.0 0.4 fusion
  55.5 7.6 %all-to-all-done.1 = f32[8,2,2,1350]{3,2,1,0:T(2,128)S(1)} async-done(((f32[8,2,2,1350]{3,2,1,0:T(2,128)}), f32[8,2,2,1350]{3,2,1,0:T(2,128)S(1)}, u32[]{:S(2)}, u32[]{:S(2)}) %all-to-all-start.1) | async-done | bytes 172832 | tf_op jit(solution)/shard_map/all_to_all | solution.py:150
  63.1 0.7 fusion.40
  63.8 0.0 all-gather.2.cloned.1.call-update
  63.9 0.0 copy-done
  63.9 0.4 constant_dynamic-slice_fusion
  64.3 1.1 copy.68
  65.4 1.2 pad_convert_fusion.1.k_ref
  66.7 25.4 %all-gather.2.cloned.1.call-done = bf16[256,2,1350]{2,0,1:T(8,128)(2,1)} async-done(((bf16[16,2,1350]{2,0,1:T(8,128)(2,1)}), bf16[256,2,1350]{2,0,1:T(8,128)(2,1)}) %all-gather.2.cloned.1.call-update) | async-done | bytes 1382416 | tf_op jit(solution)/shard_map/all_gather | solution.py:119
  92.1 3.1 %pad_convert_fusion.w_ref = f32[2,256,1408]{2,1,0:T(8,128)} fusion(bf16[2,256,1350]{2,1,0:T(8,128)(2,1)} %bitcast.109), kind=kLoop, calls=%fused_computation.3 | loop fusion | flops 720896 | bytes 4265984 | tf_op jit(solution)/shard_map/jit(_pad)/pad | solution.py:124
  95.2 10.0 %shard_map.64 = f32[2,16,1408]{2,1,0:T(8,128)} custom-call(f32[272,1408]{1,0:T(8,128)} %pad_convert_fusion.1.k_ref, f32[2,256,1408]{2,1,0:T(8,128)} %pad_convert_fusion.w_ref), custom_call_target="tpu_custom_call" | custom-call | tf_op jit(solution)/shard_map/pallas_call | solution.py:128
  105.2 4.3 %rev.3 = f32[2,16,1350]{2,1,0:T(8,128)S(1)} reverse(f32[2,16,1350]{2,1,0:T(8,128)} %bitcast.110), dimensions={1} | reverse | bytes 345600 | tf_op jit(solution)/shard_map/rev | solution.py:139
  109.5 0.8 copy.50
  110.3 6.6 %all-to-all-start.3 = ((f32[1,16,2,1350]{3,2,0,1:T(2,128)}), f32[1,16,2,1350]{3,2,0,1:T(2,128)S(1)}, u32[]{:S(2)}, u32[]{:S(2)}) async-start(f32[1,16,2,1350]{3,2,0,1:T(2,128)} %copy.50), calls=%async_computation.3 | async-start | bytes 360448 | tf_op jit(solution)/shard_map/all_to_all | solution.py:169
  116.9 0.9 fusion.31
  117.8 7.5 %all-to-all-done.3 = f32[1,16,2,1350]{3,2,0,1:T(2,128)S(1)} async-done(((f32[1,16,2,1350]{3,2,0,1:T(2,128)}), f32[1,16,2,1350]{3,2,0,1:T(2,128)S(1)}, u32[]{:S(2)}, u32[]{:S(2)}) %all-to-all-start.3) | async-done | bytes 172832 | tf_op jit(solution)/shard_map/all_to_all | solution.py:169
  125.3 0.9 reshape.182
  126.1 1.3 fusion.8
  127.4 1.3 fusion.9
  128.7 1.3 convolution_subtract_fusion
  130.0 1.3 convolution_add_fusion
  131.3 1.4 convolution_bitcast_fusion
  132.7 1.4 fusion.4
  134.1 0.1 all_to_all.62
  134.2 0.1 copy.56
  134.3 10.9 %all_to_all.71 = f32[2,8,2700]{2,0,1:T(2,128)S(1)} all-to-all(f32[2,8,2700]{2,0,1:T(2,128)S(1)} %copy.56), channel_id=1, replica_groups=mesh['lat'=16,'freq'=8] {'freq'}, dimensions={1} | all-to-all | bytes 345600 | tf_op jit(solution)/shard_map/all_to_all | solution.py:171
  145.2 0.8 all_to_all.65
  (9 shorter events, 0.1 us)
Async XLA Ops:
  6.5 57.3 %copy-start = (bf16[511,1350]{0,1:T(8,128)(2,1)S(1)}, bf16[511,1350]{0,1:T(8,128)(2,1)}, u32[]{:S(2)}) copy-start(bf16[511,1350]{0,1:T(8,128)(2,1)} %param.11) | copy-start | bytes 4139104
  15.7 7.1 %copy-start.1 = (s32[2176]{0:T(1024)S(1)}, s32[2176]{0:T(1024)}, u32[]{:S(2)}) copy-start(s32[2176]{0:T(1024)} %param.9) | copy-start | bytes 26116
  15.7 9.3 %copy-start.2 = (f32[16,2700]{1,0:T(8,128)S(1)}, f32[16,2700]{1,0:T(8,128)}, u32[]{:S(2)}) copy-start(f32[16,2700]{1,0:T(8,128)} %param.6) | copy-start | bytes 518404
  16.6 12.0 %all-to-all-start.2 = ((bf16[16,2,272]{2,1,0:T(2,128)(2,1)}), bf16[16,2,272]{2,1,0:T(2,128)(2,1)S(1)}, u32[]{:S(2)}, u32[]{:S(2)}) async-start(bf16[16,2,272]{2,1,0:T(2,128)(2,1)} %reshape.184), calls=%async_computation.2 | async-start | bytes 49152 | tf_op jit(solution)/shard_map/all_to_all | solution.py:155
  22.5 13.6 %copy-start.3 = (s32[16]{0:T(128)S(1)}, s32[16]{0:T(128)}, u32[]{:S(2)}) copy-start(s32[16]{0:T(128)} %param.10) | copy-start | bytes 196
  28.6 15.8 %all-to-all-start = ((f32[8,2,2700]{2,1,0:T(2,128)}), f32[8,2,2700]{2,1,0:T(2,128)S(1)}, u32[]{:S(2)}, u32[]{:S(2)}) async-start(f32[8,2,2700]{2,1,0:T(2,128)} %all_to_all.53), calls=%async_computation | async-start | bytes 360448 | tf_op jit(solution)/shard_map/all_to_all | solution.py:148
  51.4 11.7 %all-to-all-start.1 = ((f32[8,2,2,1350]{3,2,1,0:T(2,128)}), f32[8,2,2,1350]{3,2,1,0:T(2,128)S(1)}, u32[]{:S(2)}, u32[]{:S(2)}) async-start(f32[8,2,2,1350]{3,2,1,0:T(2,128)} %reshape.180), calls=%async_computation.1 | async-start | bytes 360448 | tf_op jit(solution)/shard_map/all_to_all | solution.py:150
  54.8 37.2 %all-gather.2.cloned.1.call-start = ((), (), s32[]{:S(2)}) async-start(), calls=%async_computation.5 | async-start | bytes 1531904 | tf_op jit(solution)/shard_map/all_gather | solution.py:119
  110.3 14.9 %all-to-all-start.3 = ((f32[1,16,2,1350]{3,2,0,1:T(2,128)}), f32[1,16,2,1350]{3,2,0,1:T(2,128)S(1)}, u32[]{:S(2)}, u32[]{:S(2)}) async-start(f32[1,16,2,1350]{3,2,0,1:T(2,128)} %copy.50), calls=%async_computation.3 | async-start | bytes 360448 | tf_op jit(solution)/shard_map/all_to_all | solution.py:169
Sparse Core Ops, SparseCore 0:
  64.0 28.0 all-gather.1

commit v3 on v0

--- a/solution.py
+++ b/solution.py
@@ -3,6 +3,8 @@
 import numpy as np
 from jax import lax
 from jax.sharding import PartitionSpec as P
+from jax.experimental import pallas as pl
+from jax.experimental.pallas import tpu as pltpu
 
 L = 21600
 PA = 144
@@ -11,12 +13,6 @@
 
 
 highest = lax.Precision.HIGHEST
-
-
-def passed_along(block, axis, distance):
-    devices = range(lax.axis_size(axis))
-    route = [((i - distance) % len(devices), i) for i in devices]
-    return lax.ppermute(block, axis, route)
 
 
 def angle_table(first, second, period):
@@ -87,54 +83,101 @@
     return grid * (2.0 / L) ** 0.5
 
 
+LANE = 128
+SHIFTS = 8
+CHUNK = 64
+
+
+def stokes_body(k_ref, w_ref, o_ref, sh_ref):
+    span = sh_ref.shape[1]
+    total = w_ref.shape[1]
+    steps = total // SHIFTS
+    for s in range(SHIFTS):
+        sh_ref[s] = k_ref[pl.ds(s, span), :]
+    for part in range(total // CHUNK):
+
+        def step(a, carry):
+            acc_re, acc_im = carry
+            base = pl.multiple_of(a * SHIFTS, SHIFTS)
+            w_re = w_ref[0, pl.ds(base, SHIFTS), :]
+            w_im = w_ref[1, pl.ds(base, SHIFTS), :]
+            start = pl.multiple_of(part * CHUNK + total - SHIFTS - base, SHIFTS)
+            for r in range(SHIFTS):
+                slab = sh_ref[SHIFTS - 1 - r, pl.ds(start, CHUNK), :]
+                acc_re = acc_re + slab * w_re[r : r + 1, :]
+                acc_im = acc_im + slab * w_im[r : r + 1, :]
+            return acc_re, acc_im
+
+        zero = jnp.zeros((CHUNK, LANE), jnp.float32)
+        acc_re, acc_im = lax.fori_loop(0, steps, step, (zero, zero))
+        o_ref[0, part * CHUNK : (part + 1) * CHUNK, :] = acc_re
+        o_ref[1, part * CHUNK : (part + 1) * CHUNK, :] = acc_im
+
+
+def toeplitz_stokes(kernel_cols, weighted):
+    taps, width = kernel_cols.shape
+    total = weighted.shape[0]
+    span = 2 * total
+    flipped = jnp.pad(
+        kernel_cols[::-1].astype(jnp.float32), ((0, span + SHIFTS - taps), (0, LANE - width))
+    )
+    source = jnp.pad(weighted.astype(jnp.float32).transpose(1, 0, 2), ((0, 0), (0, 0), (0, LANE - width)))
+    out = pl.pallas_call(
+        stokes_body,
+        out_shape=jax.ShapeDtypeStruct((2, total, LANE), jnp.float32),
+        scratch_shapes=[pltpu.VMEM((SHIFTS, span, LANE), jnp.float32)],
+    )(flipped, source)
+    return out[:, :, :width]
+
+
 def per_device(gravity, coef, legendre, order_table, band_rows, kernel):
     bands = lax.axis_size("freq")
     blocks = lax.axis_size("lat")
     band_self = lax.axis_index("freq")
     block_self = lax.axis_index("lat")
+    everyone = ("lat", "freq")
+    devices = bands * blocks
     rows = gravity.shape[0]
-    span = PA // bands
-    local_grid = gravity.reshape(rows, span, PB)
-    terms = forward_bands(local_grid, band_self * span, bands)
-    observed = lax.psum_scatter(terms, "freq", scatter_dimension=0, tiled=True)[0]
-    band_width = observed.shape[2]
+    total_rows = rows * blocks
+    mine = rows // bands
+    band_width = kernel.shape[1]
+    sub = -(-band_width // blocks)
+    padded = sub * blocks
+    whole_rows = lax.all_to_all(gravity, "freq", split_axis=0, concat_axis=1, tiled=True)
+    terms = forward_bands(whole_rows.reshape(mine, PA, PB), 0, bands)
+    terms = jnp.pad(terms, ((0, 0), (0, 0), (0, 0), (0, padded - band_width)))
+    terms = terms.reshape(bands, mine, 2, blocks, sub).transpose(3, 0, 1, 2, 4)
+    terms = terms.reshape(devices, mine, 2, sub)
+    observed = lax.all_to_all(terms, everyone, split_axis=0, concat_axis=0, tiled=True)
+    observed = observed.reshape(total_rows, 2, sub)
     synth = jnp.einsum("ocn,onq->ocq", coef, legendre, preferred_element_type=jnp.float32).astype(
         jnp.bfloat16
     )
-    routed = lax.all_to_all(synth, "lat", split_axis=2, concat_axis=0, tiled=True)
+    routed = lax.all_gather(synth, "lat", axis=0, tiled=True)
     per_slot = coef.shape[0]
     slot_ids = (
         (jnp.arange(blocks, dtype=jnp.int32)[:, None] * bands + band_self) * per_slot
         + jnp.arange(per_slot, dtype=jnp.int32)[None, :]
     ).reshape(-1)
-    positions = order_table[slot_ids] // bands
-    selector = (positions[:, None] == jnp.arange(band_width, dtype=jnp.int32)[None, :]).astype(
+    positions = order_table[slot_ids] // bands - block_self * sub
+    selector = (positions[:, None] == jnp.arange(sub, dtype=jnp.int32)[None, :]).astype(
         jnp.bfloat16
     )
     model = jnp.einsum("jcr,jt->rct", routed, selector, preferred_element_type=jnp.float32)
-    weight = jnp.cos((20.0 + band_rows.astype(jnp.float32) / 60.0) * (np.pi / 180.0))
+    all_rows = lax.all_gather(band_rows, "lat", axis=0, tiled=True)
+    weight = jnp.cos((20.0 + all_rows.astype(jnp.float32) / 60.0) * (np.pi / 180.0))
     weighted = ((observed - model) * weight[:, None, None]).astype(jnp.bfloat16)
-    total_rows = rows * blocks
-    offsets = np.arange(rows)[None, :] - np.arange(rows)[:, None] + rows - 1
-
-    def gather_terms(source, owner):
-        first = (owner - block_self) * rows + total_rows - rows
-        window = lax.dynamic_slice_in_dim(kernel, first, 2 * rows - 1, 0)
-        toeplitz = window[offsets]
-        return jnp.einsum("pqk,qck->pck", toeplitz, source, preferred_element_type=jnp.float32)
-
-    stokes = gather_terms(weighted, block_self)
-
-    def advance(count, carry):
-        total, moving = carry
-        moving = passed_along(moving, "lat", 1)
-        owner = (block_self - count) % blocks
-        return (total + gather_terms(moving, owner), moving)
-
-    stokes, carried = lax.fori_loop(1, blocks, advance, (stokes, weighted))
-    grid_terms = inverse_rows(stokes[None], jnp.reshape(band_self, (1,)), bands)
-    geoid = lax.psum_scatter(grid_terms, "freq", scatter_dimension=1, tiled=True)
-    return geoid.reshape(rows, span * PB)
+    kernel_cols = lax.dynamic_slice_in_dim(
+        jnp.pad(kernel, ((0, 0), (0, padded - band_width))), block_self * sub, sub, 1
+    )
+    stokes = toeplitz_stokes(kernel_cols, weighted)
+    stokes = stokes.reshape(2, devices, mine, sub).transpose(1, 2, 0, 3)
+    by_source = lax.all_to_all(stokes, everyone, split_axis=0, concat_axis=0, tiled=True)
+    by_band = by_source.reshape(blocks, bands, mine, 2, sub).transpose(1, 2, 3, 0, 4)
+    by_band = by_band.reshape(bands, mine, 2, padded)[..., :band_width]
+    grid_rows = inverse_rows(by_band, jnp.arange(bands, dtype=jnp.int32), bands)
+    geoid = lax.all_to_all(grid_rows.reshape(mine, L), "freq", split_axis=1, concat_axis=0, tiled=True)
+    return geoid
 
 
 def solution(mesh):

time: 483 us -> 122 us (0.25); the launches traced: 474 us -> 122 us
  local copies, waits for them, and re-layouts: 169 us -> 13.4 us
  matrix products: 145 us -> 19.9 us
  waiting for transfers between devices: 126 us -> 9.72 us
  blocking collectives: 0 us -> 43.2 us
  between operations: 13.9 us -> 1.06 us
  starting transfers between devices: 16.7 us -> 24.3 us
  Pallas kernels: 0 us -> 6.85 us
    reduce_scatter x2 -> x0, waiting for transfers between devices: 126 us -> none  [the longest x1 77.9 us: per_device(): lax.psum_scatter(grid_terms, 'freq', scatter_dimension=1, tiled=True)]
    gather x33 -> x1, local copies, waits for them, and re-layouts: 125 us -> 2.23 us  [per_device(): positions = order_table[slot_ids] // bands - block_self * sub]
    dot_general x16 -> x1, matrix products: 113 us -> 0.34 us  [per_device(): jnp.einsum('jcr,jt->rct', routed, selector, preferred_element_type=jnp.fl...]
    all_gather x0 -> x1, blocking collectives: none -> 20.1 us  [per_device(): routed = lax.all_gather(synth, 'lat', axis=0, tiled=True)]
    all_to_all x1 -> x3, starting transfers between devices: 5.87 us -> 24.3 us  [the longest x1 8.7 us: per_device(): lax.all_to_all(terms, everyone, split_axis=0, concat_axis=0, tiled=True)]
    ppermute x15 -> x0, local copies, waits for them, and re-layouts: 13.4 us -> none  [passed_along(): return lax.ppermute(block, axis, route)]
    unnamed x0 -> x1, blocking collectives: none -> 11.8 us
    all_to_all x0 -> x1, blocking collectives: none -> 11.3 us  [per_device(): lax.all_to_all(grid_rows.reshape(mine, L), 'freq', split_axis=1, concat_a...]
  transfers between devices with their start and end apart: 18 -> 3, of which waited for: 2 -> 1; matrix products, arithmetic and copies ran while one was open for 29% -> 13% of each run, Pallas kernels for 0% -> 0%
where the time goes in v3:
time: 122 us
  blocking collectives  43.2 us (35%)
  starting transfers between devices  24.3 us (20%)
  matrix products  19.9 us (16%)
  local copies, waits for them, and re-layouts  13.4 us (11%)
  waiting for transfers between devices  9.72 us (8%)
  Pallas kernels  6.85 us (6%)
  other arithmetic  3.13 us (3%)
    all_gather x1, blocking collectives, per_device(): routed = lax.all_gather(synth, 'lat', axis=0, tiled=True)  20.1 us
    unnamed x1, blocking collectives  11.8 us
    all_to_all x1, blocking collectives, per_device(): lax.all_to_all(grid_rows.reshape(mine, L), 'freq', split_axis=1, concat_a...  11.3 us
    all_to_all x1, waiting for transfers between devices, per_device(): lax.all_to_all(stokes, everyone, split_axis=0, concat_axis=0, tiled=True)  9.72 us
    dot_general x1, matrix products, per_device(): jnp.einsum('ocn,onq->ocq', coef, legendre, preferred_element_type=jnp.flo...  8.94 us
    all_to_all x1, starting transfers between devices, per_device(): lax.all_to_all(terms, everyone, split_axis=0, concat_axis=0, tiled=True)  8.7 us
    all_to_all x1, starting transfers between devices, per_device(): lax.all_to_all(gravity, 'freq', split_axis=0, concat_axis=1, tiled=True)  7.9 us
    all_to_all x1, starting transfers between devices, per_device(): lax.all_to_all(stokes, everyone, split_axis=0, concat_axis=0, tiled=True)  7.68 us
  transfers between devices with their start and end apart: 3, of which 1 were waited for; matrix products, arithmetic and copies ran while one was open for 13% of the time, Pallas kernels for 0%

profile of v3, /device:TPU:0, one launch (start us, length us, event | category | flops | bytes accessed | tf_op | source)
XLA Modules:
  0.0 121.5 jit_solution(18155179757445207213)
XLA Ops:
  0.0 0.0 copy-start
  0.0 0.0 copy-start.4
  0.0 0.0 copy-start.1
  0.0 0.0 copy-start.3
  0.0 0.0 copy-start.2
  0.0 1.8 %all_to_all.32 = f32[8,2,2700]{2,1,0:T(2,128)} reshape(f32[16,2700]{1,0:T(8,128)} %param.6) | data formatting | bytes 345600 | tf_op jit(solution)/shard_map/all_to_all | solution.py:146
  1.8 7.9 %all-to-all-start = ((f32[8,2,2700]{2,1,0:T(2,128)}), f32[8,2,2700]{2,1,0:T(2,128)S(1)}, u32[]{:S(2)}, u32[]{:S(2)}) async-start(f32[8,2,2700]{2,1,0:T(2,128)} %all_to_all.32), calls=%async_computation | async-start | bytes 360448 | tf_op jit(solution)/shard_map/all_to_all | solution.py:146
  9.8 0.1 iota_add_fusion
  9.8 0.1 add.222
  10.0 0.0 copy-done.1
  10.0 2.2 %gather_fusion = s32[272]{0:T(512)S(1)} fusion(s32[2176]{0:T(1024)S(1)} %copy-done.1, s32[1024]{0:T(1024)S(1)} %pad_clamp_fusion), kind=kCustom, calls=%fused_computation | custom fusion | bytes 3264 | tf_op jit(solution)/shard_map/gather | solution.py:162
  12.2 0.0 copy-done.4
  12.3 0.7 dynamic-slice
  13.6 0.0 copy-done.3
  13.6 0.2 dynamic-update-slice
  13.9 11.8 %all-reduce.4 = s32[256]{0:T(256)S(1)} all-reduce(s32[256]{0:T(256)S(1)} %dynamic-update-slice), channel_id=1, replica_groups=mesh['lat'=16,'freq'=8] {'lat'}, use_global_device_ids=true, to_apply=%add.4 | all-reduce | flops 256 | bytes 2048
  25.7 0.0 copy-done.2
  25.8 0.8 copy.38
  26.6 0.0 copy-done
  26.6 8.9 %convolution_convert_fusion = bf16[17,2,256]{2,1,0:T(2,128)(2,1)S(1)} fusion(bf16[17,2,2176]{2,1,0:T(2,128)(2,1)S(1)} %copy-done, bf16[17,2176,256]{2,1,0:T(8,128)(2,1)} %param.8), kind=kOutput, calls=%fused_computation.21 | convolution fusion | flops 37888512 | bytes 19105280 | tf_op jit(solution)/shard_map/ocn,onq->ocq/dot_general | solution.py:153
  35.5 0.2 pad_dynamic-slice_fusion
  35.7 0.4 rev.3
  36.1 0.6 fusion.55
  36.7 0.0 all-to-all-done
  36.7 0.1 reshape.168
  36.9 1.0 convolution_bitcast_fusion.2
  37.9 1.0 fusion
  38.9 0.7 fusion.86
  39.6 0.7 fusion.84
  40.3 0.7 fusion.8
  41.0 0.7 fusion.7
  41.8 0.5 copy.40
  42.3 0.5 reshape.169
  42.8 0.2 reshape.170
  43.1 0.1 copy.68
  43.2 0.9 copy.42
  44.1 8.7 %all-to-all-start.1 = ((f32[128,2,2,85]{3,2,1,0:T(2,128)}), f32[128,2,2,85]{3,2,1,0:T(2,128)S(1)}, u32[]{:S(2)}, u32[]{:S(2)}) async-start(f32[128,2,2,85]{3,2,1,0:T(2,128)} %copy.42), calls=%async_computation.1 | async-start | bytes 524288 | tf_op jit(solution)/shard_map/all_to_all | solution.py:151
  52.8 0.7 pad_convert_fusion.k_ref
  53.5 20.1 %all_gather.6 = bf16[272,2,256]{2,1,0:T(2,128)(2,1)S(1)} all-gather(bf16[17,2,256]{2,1,0:T(2,128)(2,1)S(1)} %convolution_convert_fusion), channel_id=1, replica_groups=mesh['lat'=16,'freq'=8] {'lat'}, dimensions={0}, use_global_device_ids=true | all-gather | bytes 295936 | tf_op jit(solution)/shard_map/all_gather | solution.py:156
  73.6 0.0 all-to-all-done.1
  73.6 0.1 copy.43
  73.7 0.3 fusion.9
  74.1 0.7 pad_convert_fusion.1.w_ref
  74.8 6.9 %shard_map.64 = f32[2,256,128]{2,1,0:T(8,128)} custom-call(f32[520,128]{1,0:T(8,128)} %pad_convert_fusion.k_ref, f32[2,256,128]{2,1,0:T(8,128)} %pad_convert_fusion.1.w_ref), custom_call_target="tpu_custom_call" | custom-call | tf_op jit(solution)/shard_map/pallas_call | solution.py:125
  81.7 1.8 %copy.67 = f32[2,128,2,85]{3,0,2,1:T(2,128)} copy(f32[2,128,2,85]{3,2,1,0:T(2,128)} %bitcast.130) | data formatting | bytes 348160 | tf_op jit(solution)/shard_map/reshape | solution.py:174
  83.5 7.7 %all-to-all-start.2 = ((f32[128,2,2,85]{3,2,1,0:T(2,128)}), f32[128,2,2,85]{3,2,1,0:T(2,128)S(1)}, u32[]{:S(2)}, u32[]{:S(2)}) async-start(f32[128,2,2,85]{3,2,1,0:T(2,128)} %bitcast.126), calls=%async_computation.2 | async-start | bytes 524288 | tf_op jit(solution)/shard_map/all_to_all | solution.py:175
  91.2 0.9 fusion.38
  92.1 9.7 %all-to-all-done.2 = f32[128,2,2,85]{3,2,1,0:T(2,128)S(1)} async-done(((f32[128,2,2,85]{3,2,1,0:T(2,128)}), f32[128,2,2,85]{3,2,1,0:T(2,128)S(1)}, u32[]{:S(2)}, u32[]{:S(2)}) %all-to-all-start.2) | async-done | bytes 174112 | tf_op jit(solution)/shard_map/all_to_all | solution.py:175
  101.9 0.1 reshape.175
  102.0 0.7 reshape.176
  102.7 0.1 fusion.177
  102.8 0.3 copy.59
  103.1 0.8 fusion.28
  103.9 0.3 copy.60
  104.1 0.8 fusion.24
  104.9 0.8 convolution_subtract_fusion
  105.7 0.8 convolution_add_fusion
  106.5 1.4 %convolution_bitcast_fusion = f32[144,2,150]{2,0,1:T(8,128)S(1)} fusion(f32[8,2,18,150]{3,2,1,0:T(8,128)S(1)} %convolution_add_fusion, f32[8,2,18,150]{3,2,1,0:T(8,128)S(1)} %convolution_subtract_fusion, f32[8,18,150]{2,1,0:T(8,128)S(1)} %get-tuple-element.8, f32[8,18,150]{2,1,0:T(8,128)S(1)} %get-tuple-element.7, s32[8,18]{1,0:T(8,128)S(1)} %iota_add_fusion.1), kind=kOutput, calls=%fused_computation.4 | convolution fusion | flops 74965824 | bytes 691776 | tf_op jit(solution)/shard_map/brsn,bsa->ran/dot_general | solution.py:82
  107.8 1.4 %fusion.5 = f32[2,144,150]{2,1,0:T(8,128)S(1)} fusion(f32[144,2,150]{2,0,1:T(8,128)S(1)} %convolution_bitcast_fusion, f32[8,2,18,150]{3,2,1,0:T(8,128)S(1)} %convolution_add_fusion, f32[8,2,18,150]{3,2,1,0:T(8,128)S(1)} %convolution_subtract_fusion, f32[8,18,150]{2,1,0:T(8,128)S(1)} %get-tuple-element.8, f32[8,18,150]{2,1,0:T(8,128)S(1)} %get-tuple-element.7, ...), kind=kOutput, calls=%fused_computation.14 | convolution fusion | flops 75052224 | bytes 864576 | tf_op jit(solution)/shard_map/brsn,bsa->ran/dot_general | solution.py:80
  109.2 0.1 all_to_all.37
  109.4 0.1 copy.53
  109.5 11.3 %all_to_all.45 = f32[2,8,2700]{2,0,1:T(2,128)S(1)} all-to-all(f32[2,8,2700]{2,0,1:T(2,128)S(1)} %copy.53), channel_id=1, replica_groups=mesh['lat'=16,'freq'=8] {'freq'}, dimensions={1} | all-to-all | bytes 345600 | tf_op jit(solution)/shard_map/all_to_all | solution.py:179
  120.7 0.8 all_to_all.40
  (13 shorter events, 0.2 us)
Async XLA Ops:
  0.0 26.6 %copy-start = (bf16[17,2,2176]{2,1,0:T(2,128)(2,1)S(1)}, bf16[17,2,2176]{2,1,0:T(2,128)(2,1)}, u32[]{:S(2)}) copy-start(bf16[17,2,2176]{2,1,0:T(2,128)(2,1)} %param.7) | copy-start | bytes 443908
  0.0 12.2 %copy-start.4 = (u32[128]{0:T(128)S(1)}, u32[128]{0:T(128)}, u32[]{:S(2)}) copy-start(u32[128]{0:T(128)} %constant.127) | copy-start | bytes 1540
  0.0 10.0 %copy-start.1 = (s32[2176]{0:T(1024)S(1)}, s32[2176]{0:T(1024)}, u32[]{:S(2)}) copy-start(s32[2176]{0:T(1024)} %param.9) | copy-start | bytes 26116
  0.0 13.6 %copy-start.3 = (s32[16]{0:T(128)S(1)}, s32[16]{0:T(128)}, u32[]{:S(2)}) copy-start(s32[16]{0:T(128)} %param.10) | copy-start | bytes 196
  0.0 25.7 %copy-start.2 = (bf16[511,1350]{0,1:T(8,128)(2,1)S(1)}, bf16[511,1350]{0,1:T(8,128)(2,1)}, u32[]{:S(2)}) copy-start(bf16[511,1350]{0,1:T(8,128)(2,1)} %param.11) | copy-start | bytes 4139104
  1.8 34.9 %all-to-all-start = ((f32[8,2,2700]{2,1,0:T(2,128)}), f32[8,2,2700]{2,1,0:T(2,128)S(1)}, u32[]{:S(2)}, u32[]{:S(2)}) async-start(f32[8,2,2700]{2,1,0:T(2,128)} %all_to_all.32), calls=%async_computation | async-start | bytes 360448 | tf_op jit(solution)/shard_map/all_to_all | solution.py:146
  44.1 29.5 %all-to-all-start.1 = ((f32[128,2,2,85]{3,2,1,0:T(2,128)}), f32[128,2,2,85]{3,2,1,0:T(2,128)S(1)}, u32[]{:S(2)}, u32[]{:S(2)}) async-start(f32[128,2,2,85]{3,2,1,0:T(2,128)} %copy.42), calls=%async_computation.1 | async-start | bytes 524288 | tf_op jit(solution)/shard_map/all_to_all | solution.py:151
  83.5 18.3 %all-to-all-start.2 = ((f32[128,2,2,85]{3,2,1,0:T(2,128)}), f32[128,2,2,85]{3,2,1,0:T(2,128)S(1)}, u32[]{:S(2)}, u32[]{:S(2)}) async-start(f32[128,2,2,85]{3,2,1,0:T(2,128)} %bitcast.126), calls=%async_computation.2 | async-start | bytes 524288 | tf_op jit(solution)/shard_map/all_to_all | solution.py:175

commit v4 on v3

--- a/solution.py
+++ b/solution.py
@@ -145,28 +145,30 @@
     padded = sub * blocks
     whole_rows = lax.all_to_all(gravity, "freq", split_axis=0, concat_axis=1, tiled=True)
     terms = forward_bands(whole_rows.reshape(mine, PA, PB), 0, bands)
-    terms = jnp.pad(terms, ((0, 0), (0, 0), (0, 0), (0, padded - band_width)))
-    terms = terms.reshape(bands, mine, 2, blocks, sub).transpose(3, 0, 1, 2, 4)
-    terms = terms.reshape(devices, mine, 2, sub)
-    observed = lax.all_to_all(terms, everyone, split_axis=0, concat_axis=0, tiled=True)
-    observed = observed.reshape(total_rows, 2, sub)
     synth = jnp.einsum("ocn,onq->ocq", coef, legendre, preferred_element_type=jnp.float32).astype(
         jnp.bfloat16
     )
-    routed = lax.all_gather(synth, "lat", axis=0, tiled=True)
     per_slot = coef.shape[0]
-    slot_ids = (
-        (jnp.arange(blocks, dtype=jnp.int32)[:, None] * bands + band_self) * per_slot
-        + jnp.arange(per_slot, dtype=jnp.int32)[None, :]
-    ).reshape(-1)
-    positions = order_table[slot_ids] // bands - block_self * sub
-    selector = (positions[:, None] == jnp.arange(sub, dtype=jnp.int32)[None, :]).astype(
-        jnp.bfloat16
+    held = blocks * per_slot
+    routed = lax.all_to_all(
+        synth.reshape(per_slot, 2, devices, mine), everyone, split_axis=2, concat_axis=0, tiled=True
     )
-    model = jnp.einsum("jcr,jt->rct", routed, selector, preferred_element_type=jnp.float32)
-    all_rows = lax.all_gather(band_rows, "lat", axis=0, tiled=True)
-    weight = jnp.cos((20.0 + all_rows.astype(jnp.float32) / 60.0) * (np.pi / 180.0))
-    weighted = ((observed - model) * weight[:, None, None]).astype(jnp.bfloat16)
+    routed = routed.reshape(blocks, bands, per_slot, 2, mine).transpose(1, 0, 2, 3, 4)
+    routed = routed.reshape(bands, held, 2, mine)
+    positions = order_table.reshape(blocks, bands, per_slot).transpose(1, 0, 2).reshape(bands, held)
+    selector = (
+        positions[:, :, None] // bands == jnp.arange(held, dtype=jnp.int32)[None, None, :]
+    ).astype(jnp.bfloat16)
+    model = jnp.einsum("bjcr,bjt->brct", routed, selector, preferred_element_type=jnp.float32)
+    model = jnp.pad(model, ((0, 0), (0, 0), (0, 0), (0, band_width - held)))
+    my_rows = lax.dynamic_slice_in_dim(band_rows, band_self * mine, mine, 0)
+    weight = jnp.cos((20.0 + my_rows.astype(jnp.float32) / 60.0) * (np.pi / 180.0))
+    weighted = ((terms - model) * weight[None, :, None, None]).astype(jnp.bfloat16)
+    weighted = jnp.pad(weighted, ((0, 0), (0, 0), (0, 0), (0, padded - band_width)))
+    weighted = weighted.reshape(bands, mine, 2, blocks, sub).transpose(3, 0, 1, 2, 4)
+    weighted = weighted.reshape(devices, mine, 2, sub)
+    weighted = lax.all_to_all(weighted, everyone, split_axis=0, concat_axis=0, tiled=True)
+    weighted = weighted.reshape(total_rows, 2, sub)
     kernel_cols = lax.dynamic_slice_in_dim(
         jnp.pad(kernel, ((0, 0), (0, padded - band_width))), block_self * sub, sub, 1
     )

time: 122 us -> 110 us (0.902)
  blocking collectives: 43.2 us -> 11.3 us
  waiting for transfers between devices: 9.72 us -> 31.1 us
  local copies, waits for them, and re-layouts: 13.4 us -> 11.9 us
    all_gather x1 -> x0, blocking collectives: 20.1 us -> none  [per_device(): routed = lax.all_gather(synth, 'lat', axis=0, tiled=True)]
    all_to_all x1 -> x2, waiting for transfers between devices: 0.01 us -> 14.3 us  [the longest x1 8.73 us: per_device(): lax.all_to_all(weighted, everyone, split_axis=0, concat_axis=0, tiled=True)]
    unnamed x1 -> x0, blocking collectives: 11.8 us -> none
    all_to_all x1 -> x2, starting transfers between devices: 8.7 us -> 16 us  [the longest x1 11.2 us: per_device(): lax.all_to_all(synth.reshape(per_slot, 2, devices, mine), everyone, split...]
    all_to_all x1, waiting for transfers between devices: 0.01 us -> 7.12 us  [per_device(): lax.all_to_all(gravity, 'freq', split_axis=0, concat_axis=1, tiled=True)]
    all_to_all x1, starting transfers between devices: 7.9 us -> 3.39 us  [per_device(): lax.all_to_all(gravity, 'freq', split_axis=0, concat_axis=1, tiled=True)]
    all_to_all x1, starting transfers between devices: 7.68 us -> 4.59 us  [per_device(): lax.all_to_all(stokes, everyone, split_axis=0, concat_axis=0, tiled=True)]
    gather x1 -> x0, local copies, waits for them, and re-layouts: 2.23 us -> none  [per_device(): positions = order_table[slot_ids] // bands - block_self * sub]
  transfers between devices with their start and end apart: 3 -> 4, of which waited for: 1 -> 4; matrix products, arithmetic and copies ran while one was open for 13% -> 5% of each run, Pallas kernels for 0% -> 0%
where the time goes in v4:
time: 110 us; the launch traced here: 109 us
  waiting for transfers between devices  31.1 us (28%)
  starting transfers between devices  23.9 us (22%)
  matrix products  20.6 us (19%)
  local copies, waits for them, and re-layouts  11.9 us (11%)
  blocking collectives  11.3 us (10%)
  Pallas kernels  6.85 us (6%)
  other arithmetic  3.19 us (3%)
    all_to_all x1, blocking collectives, per_device(): lax.all_to_all(grid_rows.reshape(mine, L), 'freq', split_axis=1, concat_a...  11.3 us
    all_to_all x1, starting transfers between devices, per_device(): lax.all_to_all(synth.reshape(per_slot, 2, devices, mine), everyone, split...  11.2 us
    all_to_all x1, waiting for transfers between devices, per_device(): lax.all_to_all(stokes, everyone, split_axis=0, concat_axis=0, tiled=True)  9.72 us
    dot_general x1, matrix products, per_device(): jnp.einsum('ocn,onq->ocq', coef, legendre, preferred_element_type=jnp.flo...  9.04 us
    all_to_all x1, waiting for transfers between devices, per_device(): lax.all_to_all(weighted, everyone, split_axis=0, concat_axis=0, tiled=True)  8.73 us
    all_to_all x1, waiting for transfers between devices, per_device(): lax.all_to_all(gravity, 'freq', split_axis=0, concat_axis=1, tiled=True)  7.12 us
    pallas_call x1, Pallas kernels, toeplitz_stokes(): pl.pallas_call(stokes_body, out_shape=jax.ShapeDtypeStruct((2, total, LAN...  6.85 us
    all_to_all x1, waiting for transfers between devices, per_device(): lax.all_to_all(synth.reshape(per_slot, 2, devices, mine), everyone, split...  5.55 us
  transfers between devices with their start and end apart: 4, of which 4 were waited for; matrix products, arithmetic and copies ran while one was open for 5% of the time, Pallas kernels for 0%

profile of v4, /device:TPU:0, one launch (start us, length us, event | category | flops | bytes accessed | tf_op | source)
XLA Modules:
  0.0 109.2 jit_solution(5194747051919560084)
XLA Ops:
  0.0 0.0 copy-start
  0.0 0.0 copy-start.3
  0.0 0.9 copy-done
  0.9 9.0 %convolution_convert_fusion = bf16[17,2,256]{2,1,0:T(2,128)(2,1)S(1)} fusion(bf16[17,2,2176]{2,1,0:T(2,128)(2,1)S(1)} %copy-done, bf16[17,2176,256]{2,1,0:T(8,128)(2,1)} %param.8), kind=kOutput, calls=%fused_computation.19 | convolution fusion | flops 37888512 | bytes 19105280 | tf_op jit(solution)/shard_map/ocn,onq->ocq/dot_general | solution.py:148
  10.0 0.2 copy.66
  10.1 0.8 copy.67
  10.9 11.2 %all-to-all-start.1 = ((bf16[17,2,128,2]{0,3,1,2:T(2,128)(2,1)}), bf16[17,2,128,2]{0,3,1,2:T(2,128)(2,1)S(1)}, u32[]{:S(2)}, u32[]{:S(2)}) async-start(bf16[17,2,128,2]{0,3,1,2:T(2,128)(2,1)} %copy.67), calls=%async_computation.1 | async-start | bytes 262144 | tf_op jit(solution)/shard_map/all_to_all | solution.py:153
  22.1 0.6 fusion.54
  22.7 0.0 copy-done.3
  22.7 0.2 reshape.185
  22.9 0.1 broadcast_in_dim_reshape.3
  23.0 0.0 copy-done.1
  23.1 0.8 copy.62
  23.9 0.0 copy-start.4
  23.9 0.0 copy-start.2
  23.9 0.2 pad_dynamic-slice_fusion
  24.1 0.5 copy-done.4
  24.6 0.1 multiply_cosine_fusion
  24.7 0.2 copy-done.2
  24.9 0.8 all_to_all.43
  25.6 0.3 rev.3
  26.0 5.6 %all-to-all-done.1 = bf16[17,2,128,2]{0,3,1,2:T(2,128)(2,1)S(1)} async-done(((bf16[17,2,128,2]{0,3,1,2:T(2,128)(2,1)}), bf16[17,2,128,2]{0,3,1,2:T(2,128)(2,1)S(1)}, u32[]{:S(2)}, u32[]{:S(2)}) %all-to-all-start.1) | async-done | bytes 17440 | tf_op jit(solution)/shard_map/all_to_all | solution.py:153
  31.5 3.4 %all-to-all-start = ((f32[8,2,2700]{2,1,0:T(2,128)}), f32[8,2,2700]{2,1,0:T(2,128)S(1)}, u32[]{:S(2)}, u32[]{:S(2)}) async-start(f32[8,2,2700]{2,1,0:T(2,128)} %all_to_all.43), calls=%async_computation | async-start | bytes 360448 | tf_op jit(solution)/shard_map/all_to_all | solution.py:146
  34.9 0.1 copy.93
  35.0 0.2 reshape.188
  35.2 0.9 fusion.1
  36.1 7.1 %all-to-all-done = f32[8,2,2700]{2,1,0:T(2,128)S(1)} async-done(((f32[8,2,2700]{2,1,0:T(2,128)}), f32[8,2,2700]{2,1,0:T(2,128)S(1)}, u32[]{:S(2)}, u32[]{:S(2)}) %all-to-all-start) | async-done | bytes 172832 | tf_op jit(solution)/shard_map/all_to_all | solution.py:146
  43.2 0.1 reshape.183
  43.4 1.0 convolution_bitcast_fusion.2
  44.4 1.0 fusion.4
  45.4 0.7 fusion.83
  46.1 0.7 fusion.81
  46.8 0.7 fusion.9
  47.5 0.7 fusion.8
  48.2 0.5 copy.64
  48.8 0.5 reshape.184
  49.3 0.1 multiply_convert_fusion
  49.4 0.3 reshape.189
  49.6 0.8 copy.70
  50.4 4.8 %all-to-all-start.2 = ((bf16[128,2,2,85]{3,1,2,0:T(2,128)(2,1)}), bf16[128,2,2,85]{3,1,2,0:T(2,128)(2,1)S(1)}, u32[]{:S(2)}, u32[]{:S(2)}) async-start(bf16[128,2,2,85]{3,1,2,0:T(2,128)(2,1)} %bitcast.21), calls=%async_computation.2 | async-start | bytes 262144 | tf_op jit(solution)/shard_map/all_to_all | solution.py:170
  55.2 0.7 pad_convert_fusion.k_ref
  56.0 8.7 %all-to-all-done.2 = bf16[128,2,2,85]{3,1,2,0:T(2,128)(2,1)S(1)} async-done(((bf16[128,2,2,85]{3,1,2,0:T(2,128)(2,1)}), bf16[128,2,2,85]{3,1,2,0:T(2,128)(2,1)S(1)}, u32[]{:S(2)}, u32[]{:S(2)}) %all-to-all-start.2) | async-done | bytes 87072 | tf_op jit(solution)/shard_map/all_to_all | solution.py:170
  64.7 0.1 copy.71
  64.8 0.7 pad_convert_fusion.1.w_ref
  65.5 6.8 %shard_map.64 = f32[2,256,128]{2,1,0:T(8,128)} custom-call(f32[520,128]{1,0:T(8,128)} %pad_convert_fusion.k_ref, f32[2,256,128]{2,1,0:T(8,128)} %pad_convert_fusion.1.w_ref), custom_call_target="tpu_custom_call" | custom-call | tf_op jit(solution)/shard_map/pallas_call | solution.py:125
  72.4 1.9 %copy.92 = f32[2,128,2,85]{3,0,2,1:T(2,128)} copy(f32[2,128,2,85]{3,2,1,0:T(2,128)} %bitcast.137) | data formatting | bytes 348160 | tf_op jit(solution)/shard_map/reshape | solution.py:176
  74.2 4.6 %all-to-all-start.3 = ((f32[128,2,2,85]{3,2,1,0:T(2,128)}), f32[128,2,2,85]{3,2,1,0:T(2,128)S(1)}, u32[]{:S(2)}, u32[]{:S(2)}) async-start(f32[128,2,2,85]{3,2,1,0:T(2,128)} %bitcast.132), calls=%async_computation.3 | async-start | bytes 524288 | tf_op jit(solution)/shard_map/all_to_all | solution.py:177
  78.8 0.9 fusion.37
  79.7 9.7 %all-to-all-done.3 = f32[128,2,2,85]{3,2,1,0:T(2,128)S(1)} async-done(((f32[128,2,2,85]{3,2,1,0:T(2,128)}), f32[128,2,2,85]{3,2,1,0:T(2,128)S(1)}, u32[]{:S(2)}, u32[]{:S(2)}) %all-to-all-start.3) | async-done | bytes 174112 | tf_op jit(solution)/shard_map/all_to_all | solution.py:177
  89.5 0.1 reshape.193
  89.6 0.7 reshape.194
  90.3 0.1 fusion.171
  90.4 0.3 copy.85
  90.7 0.8 fusion.27
  91.5 0.3 copy.86
  91.8 0.8 fusion.23
  92.6 0.8 convolution_subtract_fusion
  93.3 0.8 convolution_add_fusion
  94.1 1.3 %convolution_bitcast_fusion = f32[144,2,150]{2,0,1:T(8,128)S(1)} fusion(f32[8,2,18,150]{3,2,1,0:T(8,128)S(1)} %convolution_add_fusion, f32[8,2,18,150]{3,2,1,0:T(8,128)S(1)} %convolution_subtract_fusion, f32[8,18,150]{2,1,0:T(8,128)S(1)} %get-tuple-element.8, f32[8,18,150]{2,1,0:T(8,128)S(1)} %get-tuple-element.7, s32[8,18]{1,0:T(8,128)S(1)} %iota_add_fusion), kind=kOutput, calls=%fused_computation.7 | convolution fusion | flops 74965824 | bytes 691776 | tf_op jit(solution)/shard_map/brsn,bsa->ran/dot_general | solution.py:82
  95.5 1.3 %fusion.7 = f32[2,144,150]{2,1,0:T(8,128)S(1)} fusion(f32[144,2,150]{2,0,1:T(8,128)S(1)} %convolution_bitcast_fusion, f32[8,2,18,150]{3,2,1,0:T(8,128)S(1)} %convolution_add_fusion, f32[8,2,18,150]{3,2,1,0:T(8,128)S(1)} %convolution_subtract_fusion, f32[8,18,150]{2,1,0:T(8,128)S(1)} %get-tuple-element.8, f32[8,18,150]{2,1,0:T(8,128)S(1)} %get-tuple-element.7, ...), kind=kOutput, calls=%fused_computation.14 | convolution fusion | flops 75052224 | bytes 864576 | tf_op jit(solution)/shard_map/brsn,bsa->ran/dot_general | solution.py:80
  96.8 0.1 all_to_all.51
  97.0 0.1 copy.79
  97.1 11.3 %all_to_all.60 = f32[2,8,2700]{2,0,1:T(2,128)S(1)} all-to-all(f32[2,8,2700]{2,0,1:T(2,128)S(1)} %copy.79), channel_id=1, replica_groups=mesh['lat'=16,'freq'=8] {'freq'}, dimensions={1} | all-to-all | bytes 345600 | tf_op jit(solution)/shard_map/all_to_all | solution.py:181
  108.4 0.8 all_to_all.54
  (11 shorter events, 0.2 us)
Async XLA Ops:
  0.0 0.9 copy-start
  0.0 22.7 %copy-start.3 = (s32[2176]{0:T(1024)S(1)}, s32[2176]{0:T(1024)}, u32[]{:S(2)}) copy-start(s32[2176]{0:T(1024)} %param.9) | copy-start | bytes 26116
  0.9 22.1 %copy-start.1 = (bf16[511,1350]{0,1:T(8,128)(2,1)S(1)}, bf16[511,1350]{0,1:T(8,128)(2,1)}, u32[]{:S(2)}) copy-start(bf16[511,1350]{0,1:T(8,128)(2,1)} %param.11) | copy-start | bytes 4139104
  10.9 20.6 %all-to-all-start.1 = ((bf16[17,2,128,2]{0,3,1,2:T(2,128)(2,1)}), bf16[17,2,128,2]{0,3,1,2:T(2,128)(2,1)S(1)}, u32[]{:S(2)}, u32[]{:S(2)}) async-start(bf16[17,2,128,2]{0,3,1,2:T(2,128)(2,1)} %copy.67), calls=%async_computation.1 | async-start | bytes 262144 | tf_op jit(solution)/shard_map/all_to_all | solution.py:153
  23.9 0.7 copy-start.4
  23.9 0.9 copy-start.2
  31.5 11.7 %all-to-all-start = ((f32[8,2,2700]{2,1,0:T(2,128)}), f32[8,2,2700]{2,1,0:T(2,128)S(1)}, u32[]{:S(2)}, u32[]{:S(2)}) async-start(f32[8,2,2700]{2,1,0:T(2,128)} %all_to_all.43), calls=%async_computation | async-start | bytes 360448 | tf_op jit(solution)/shard_map/all_to_all | solution.py:146
  50.4 14.3 %all-to-all-start.2 = ((bf16[128,2,2,85]{3,1,2,0:T(2,128)(2,1)}), bf16[128,2,2,85]{3,1,2,0:T(2,128)(2,1)S(1)}, u32[]{:S(2)}, u32[]{:S(2)}) async-start(bf16[128,2,2,85]{3,1,2,0:T(2,128)(2,1)} %bitcast.21), calls=%async_computation.2 | async-start | bytes 262144 | tf_op jit(solution)/shard_map/all_to_all | solution.py:170
  74.2 15.2 %all-to-all-start.3 = ((f32[128,2,2,85]{3,2,1,0:T(2,128)}), f32[128,2,2,85]{3,2,1,0:T(2,128)S(1)}, u32[]{:S(2)}, u32[]{:S(2)}) async-start(f32[128,2,2,85]{3,2,1,0:T(2,128)} %bitcast.132), calls=%async_computation.3 | async-start | bytes 524288 | tf_op jit(solution)/shard_map/all_to_all | solution.py:177

commit v5 on v3

--- a/solution.py
+++ b/solution.py
@@ -141,40 +141,56 @@
     total_rows = rows * blocks
     mine = rows // bands
     band_width = kernel.shape[1]
+    per_slot = coef.shape[0]
+    held = blocks * per_slot
     sub = -(-band_width // blocks)
-    padded = sub * blocks
+    share = sub - per_slot
+    padded = held + share * blocks
+    positions = order_table.reshape(blocks, bands, per_slot).transpose(1, 0, 2).reshape(bands, held) // bands
+    slot_of = jnp.sum(
+        jnp.where(
+            positions[:, :, None] == jnp.arange(held, dtype=jnp.int32)[None, None, :],
+            jnp.arange(held, dtype=jnp.int32)[None, :, None],
+            0,
+        ),
+        axis=1,
+    )
+
     whole_rows = lax.all_to_all(gravity, "freq", split_axis=0, concat_axis=1, tiled=True)
     terms = forward_bands(whole_rows.reshape(mine, PA, PB), 0, bands)
-    terms = jnp.pad(terms, ((0, 0), (0, 0), (0, 0), (0, padded - band_width)))
-    terms = terms.reshape(bands, mine, 2, blocks, sub).transpose(3, 0, 1, 2, 4)
-    terms = terms.reshape(devices, mine, 2, sub)
-    observed = lax.all_to_all(terms, everyone, split_axis=0, concat_axis=0, tiled=True)
-    observed = observed.reshape(total_rows, 2, sub)
+    own = jnp.take_along_axis(terms[..., :held], positions[:, None, None, :], axis=3)
+    own = own.reshape(bands, mine, 2, blocks, per_slot)
+    rest = jnp.pad(terms[..., held:], ((0, 0), (0, 0), (0, 0), (0, padded - band_width)))
+    rest = rest.reshape(bands, mine, 2, blocks, share)
+    my_rows = lax.dynamic_slice_in_dim(band_rows, band_self * mine, mine, 0)
+    weight = jnp.cos((20.0 + my_rows.astype(jnp.float32) / 60.0) * (np.pi / 180.0))
+    carried = jnp.broadcast_to(weight[None, :, None, None, None], (bands, mine, 2, blocks, 1))
+    payload = jnp.concatenate([own, rest, carried], axis=4).transpose(3, 0, 1, 2, 4)
+    payload = payload.reshape(devices, mine, 2, sub + 1)
+    observed = lax.all_to_all(payload, everyone, split_axis=0, concat_axis=0, tiled=True)
+    observed = observed.reshape(total_rows, 2, sub + 1)
+    weight_all = observed[:, 0, sub]
+    observed = observed[:, :, :sub]
+
     synth = jnp.einsum("ocn,onq->ocq", coef, legendre, preferred_element_type=jnp.float32).astype(
         jnp.bfloat16
     )
-    routed = lax.all_gather(synth, "lat", axis=0, tiled=True)
-    per_slot = coef.shape[0]
-    slot_ids = (
-        (jnp.arange(blocks, dtype=jnp.int32)[:, None] * bands + band_self) * per_slot
-        + jnp.arange(per_slot, dtype=jnp.int32)[None, :]
-    ).reshape(-1)
-    positions = order_table[slot_ids] // bands - block_self * sub
-    selector = (positions[:, None] == jnp.arange(sub, dtype=jnp.int32)[None, :]).astype(
-        jnp.bfloat16
-    )
-    model = jnp.einsum("jcr,jt->rct", routed, selector, preferred_element_type=jnp.float32)
-    all_rows = lax.all_gather(band_rows, "lat", axis=0, tiled=True)
-    weight = jnp.cos((20.0 + all_rows.astype(jnp.float32) / 60.0) * (np.pi / 180.0))
-    weighted = ((observed - model) * weight[:, None, None]).astype(jnp.bfloat16)
-    kernel_cols = lax.dynamic_slice_in_dim(
-        jnp.pad(kernel, ((0, 0), (0, padded - band_width))), block_self * sub, sub, 1
-    )
-    stokes = toeplitz_stokes(kernel_cols, weighted)
+    model = jnp.pad(synth.astype(jnp.float32).transpose(2, 1, 0), ((0, 0), (0, 0), (0, share)))
+    weighted = ((observed - model) * weight_all[:, None, None]).astype(jnp.bfloat16)
+
+    own_cols = lax.dynamic_slice_in_dim(positions[band_self], block_self * per_slot, per_slot, 0)
+    kernel_own = jnp.take(kernel, own_cols, axis=1)
+    kernel_rest = lax.dynamic_slice_in_dim(
+        jnp.pad(kernel, ((0, 0), (0, padded - band_width))), held + block_self * share, share, 1
+    )
+    stokes = toeplitz_stokes(jnp.concatenate([kernel_own, kernel_rest], axis=1), weighted)
     stokes = stokes.reshape(2, devices, mine, sub).transpose(1, 2, 0, 3)
     by_source = lax.all_to_all(stokes, everyone, split_axis=0, concat_axis=0, tiled=True)
-    by_band = by_source.reshape(blocks, bands, mine, 2, sub).transpose(1, 2, 3, 0, 4)
-    by_band = by_band.reshape(bands, mine, 2, padded)[..., :band_width]
+    by_source = by_source.reshape(blocks, bands, mine, 2, sub).transpose(1, 2, 3, 0, 4)
+    slots_back = by_source[..., :per_slot].reshape(bands, mine, 2, held)
+    slots_back = jnp.take_along_axis(slots_back, slot_of[:, None, None, :], axis=3)
+    rest_back = by_source[..., per_slot:].reshape(bands, mine, 2, blocks * share)
+    by_band = jnp.concatenate([slots_back, rest_back], axis=3)[..., :band_width]
     grid_rows = inverse_rows(by_band, jnp.arange(bands, dtype=jnp.int32), bands)
     geoid = lax.all_to_all(grid_rows.reshape(mine, L), "freq", split_axis=1, concat_axis=0, tiled=True)
     return geoid

time: 122 us -> 138 us (1.13)
  local copies, waits for them, and re-layouts: 13.4 us -> 51.9 us
  blocking collectives: 43.2 us -> 11.3 us
  waiting for transfers between devices: 9.72 us -> 19.7 us
    gather x1 -> x8, local copies, waits for them, and re-layouts: 2.23 us -> 34.2 us  [the longest x3 16.8 us: per_device(): jnp.take_along_axis(terms[..., :held], positions[:, None, None, :], axis=3)]
    all_gather x1 -> x0, blocking collectives: 20.1 us -> none  [per_device(): routed = lax.all_gather(synth, 'lat', axis=0, tiled=True)]
    unnamed x1 -> x0, blocking collectives: 11.8 us -> none
    all_to_all x1, waiting for transfers between devices: 0.01 us -> 9.12 us  [per_device(): lax.all_to_all(payload, everyone, split_axis=0, concat_axis=0, tiled=True)]
    reshape x3 -> x8, local copies, waits for them, and re-layouts: 1.29 us -> 4.57 us  [the longest x1 2.06 us: per_device(): slots_back = by_source[..., :per_slot].reshape(bands, mine, 2, held)]
    all_to_all x1, starting transfers between devices: 7.68 us -> 4.61 us  [per_device(): lax.all_to_all(stokes, everyone, split_axis=0, concat_axis=0, tiled=True)]
    unnamed x16 -> x10, local copies, waits for them, and re-layouts: 2.27 us -> 5.06 us
    all_to_all x1, starting transfers between devices: 8.7 us -> 10.5 us  [per_device(): lax.all_to_all(payload, everyone, split_axis=0, concat_axis=0, tiled=True)]
  transfers between devices with their start and end apart: 3 -> 3, of which waited for: 1 -> 2; matrix products, arithmetic and copies ran while one was open for 13% -> 12% of each run, Pallas kernels for 0% -> 0%
where the time goes in v5:
time: 138 us; the launch traced here: 137 us
  local copies, waits for them, and re-layouts  51.9 us (38%)
  starting transfers between devices  23 us (17%)
  waiting for transfers between devices  19.7 us (14%)
  matrix products  19.6 us (14%)
  blocking collectives  11.3 us (8%)
  Pallas kernels  6.85 us (5%)
  other arithmetic  4.43 us (3%)
    gather x3, local copies, waits for them, and re-layouts, per_device(): jnp.take_along_axis(terms[..., :held], positions[:, None, None, :], axis=3)  16.8 us
    gather x3, local copies, waits for them, and re-layouts, per_device(): jnp.take_along_axis(slots_back, slot_of[:, None, None, :], axis=3)  16.6 us
    all_to_all x1, blocking collectives, per_device(): lax.all_to_all(grid_rows.reshape(mine, L), 'freq', split_axis=1, concat_a...  11.3 us
    all_to_all x1, waiting for transfers between devices, per_device(): lax.all_to_all(stokes, everyone, split_axis=0, concat_axis=0, tiled=True)  10.6 us
    all_to_all x1, starting transfers between devices, per_device(): lax.all_to_all(payload, everyone, split_axis=0, concat_axis=0, tiled=True)  10.5 us
    all_to_all x1, waiting for transfers between devices, per_device(): lax.all_to_all(payload, everyone, split_axis=0, concat_axis=0, tiled=True)  9.12 us
    dot_general x1, matrix products, per_device(): jnp.einsum('ocn,onq->ocq', coef, legendre, preferred_element_type=jnp.flo...  8.94 us
    all_to_all x1, starting transfers between devices, per_device(): lax.all_to_all(gravity, 'freq', split_axis=0, concat_axis=1, tiled=True)  7.89 us
  transfers between devices with their start and end apart: 3, of which 2 were waited for; matrix products, arithmetic and copies ran while one was open for 12% of the time, Pallas kernels for 0%

profile of v5, /device:TPU:0, one launch (start us, length us, event | category | flops | bytes accessed | tf_op | source)
XLA Modules:
  0.0 137.2 jit_solution(7043333954988301020)
XLA Ops:
  0.0 1.7 %all_to_all.32 = f32[8,2,2700]{2,1,0:T(2,128)} reshape(f32[16,2700]{1,0:T(8,128)} %param.8) | data formatting | bytes 345600 | tf_op jit(solution)/shard_map/all_to_all | solution.py:159
  1.7 7.9 %all-to-all-start = ((f32[8,2,2700]{2,1,0:T(2,128)}), f32[8,2,2700]{2,1,0:T(2,128)S(1)}, u32[]{:S(2)}, u32[]{:S(2)}) async-start(f32[8,2,2700]{2,1,0:T(2,128)} %all_to_all.32), calls=%async_computation | async-start | bytes 360448 | tf_op jit(solution)/shard_map/all_to_all | solution.py:159
  9.6 0.9 reshape.278
  11.0 0.6 select_reduce_fusion
  11.6 1.9 %copy.100 = bf16[511,1350]{1,0:T(8,128)(2,1)S(1)} copy(bf16[511,1350]{0,1:T(8,128)(2,1)} %param.13) | data formatting | bytes 2759400 | tf_op args[5]
  13.5 0.6 gather_fusion
  14.1 0.1 copy.99
  14.3 0.9 fusion.35
  15.2 8.9 %convolution_convert_fusion = bf16[17,2,256]{2,1,0:T(2,128)(2,1)S(1)} fusion(bf16[17,2,2176]{2,1,0:T(2,128)(2,1)S(1)} %copy-done, bf16[17,2176,256]{2,1,0:T(8,128)(2,1)} %param.10), kind=kOutput, calls=%fused_computation.20 | convolution fusion | flops 37888512 | bytes 19105280 | tf_op jit(solution)/shard_map/ocn,onq->ocq/dot_general | solution.py:175
  24.2 0.2 pad_dynamic-slice_fusion
  24.3 0.5 copy-done.2
  24.8 0.1 multiply_cosine_fusion
  25.0 0.6 fusion.52
  25.6 0.1 reshape.280
  25.8 1.0 convolution_bitcast_fusion.2
  26.8 1.0 fusion
  27.8 0.7 fusion.82
  28.5 0.7 fusion.80
  29.2 0.7 fusion.5
  29.9 0.7 fusion.4
  30.7 0.5 copy.103
  31.2 0.5 reshape.281
  31.7 0.1 slice.47
  31.8 2.1 %copy.127 = f32[8,2,2,272]{2,1,3,0:T(2,128)S(1)} copy(f32[8,2,2,272]{3,0,2,1:T(8,128)S(1)} %slice.46) | data formatting | bytes 69632
  34.0 13.7 %gather_fusion.1 = f32[2176,2,2]{2,1,0:T(2,128)} fusion(f32[8,2,2,272]{2,1,3,0:T(2,128)S(1)} %copy.127, s32[2176]{0:T(1024)S(1)} %reshape.324), kind=kCustom, calls=%fused_computation.clone | custom fusion | bytes 87040 | tf_op jit(solution)/shard_map/jit(take_along_axis)/gather | solution.py:161
  47.7 3.0 %copy.105 = f32[8,272,2,2]{1,0,3,2:T(8,128)S(1)} copy(f32[8,272,2,2]{3,2,1,0:T(2,128)} %bitcast.159) | data formatting | bytes 69632 | tf_op jit(solution)/shard_map/jit(take_along_axis)/gather | solution.py:161
  50.7 0.2 reshape.283
  50.9 0.2 reshape.284
  51.2 0.2 maximum_bitcast_fusion
  51.5 0.9 copy.107
  52.4 10.5 %all-to-all-start.1 = ((f32[128,2,2,86]{3,2,1,0:T(2,128)}), f32[128,2,2,86]{3,2,1,0:T(2,128)S(1)}, u32[]{:S(2)}, u32[]{:S(2)}) async-start(f32[128,2,2,86]{3,2,1,0:T(2,128)} %copy.107), calls=%async_computation.1 | async-start | bytes 524288 | tf_op jit(solution)/shard_map/all_to_all | solution.py:170
  62.9 0.1 pad_maximum_fusion.1
  63.0 0.2 copy.109
  63.2 0.4 rev.3
  63.6 0.7 pad_convert_fusion.k_ref
  64.4 9.1 %all-to-all-done.1 = f32[128,2,2,86]{3,2,1,0:T(2,128)S(1)} async-done(((f32[128,2,2,86]{3,2,1,0:T(2,128)}), f32[128,2,2,86]{3,2,1,0:T(2,128)S(1)}, u32[]{:S(2)}, u32[]{:S(2)}) %all-to-all-start.1) | async-done | bytes 176160 | tf_op jit(solution)/shard_map/all_to_all | solution.py:170
  73.5 0.1 copy.108
  73.6 0.2 slice_reduce_fusion
  73.8 0.1 fusion.61
  73.9 0.7 pad_convert_fusion.1.w_ref
  74.6 6.9 %shard_map.64 = f32[2,256,128]{2,1,0:T(8,128)} custom-call(f32[520,128]{1,0:T(8,128)} %pad_convert_fusion.k_ref, f32[2,256,128]{2,1,0:T(8,128)} %pad_convert_fusion.1.w_ref), custom_call_target="tpu_custom_call" | custom-call | tf_op jit(solution)/shard_map/pallas_call | solution.py:125
  81.5 1.9 %copy.134 = f32[2,128,2,85]{3,0,2,1:T(2,128)} copy(f32[2,128,2,85]{3,2,1,0:T(2,128)} %bitcast.163) | data formatting | bytes 348160 | tf_op jit(solution)/shard_map/reshape | solution.py:187
  83.3 4.6 %all-to-all-start.2 = ((f32[128,2,2,85]{3,2,1,0:T(2,128)}), f32[128,2,2,85]{3,2,1,0:T(2,128)S(1)}, u32[]{:S(2)}, u32[]{:S(2)}) async-start(f32[128,2,2,85]{3,2,1,0:T(2,128)} %bitcast.152), calls=%async_computation.2 | async-start | bytes 524288 | tf_op jit(solution)/shard_map/all_to_all | solution.py:188
  88.0 10.6 %all-to-all-done.2 = f32[128,2,2,85]{3,2,1,0:T(2,128)S(1)} async-done(((f32[128,2,2,85]{3,2,1,0:T(2,128)}), f32[128,2,2,85]{3,2,1,0:T(2,128)S(1)}, u32[]{:S(2)}, u32[]{:S(2)}) %all-to-all-start.2) | async-done | bytes 174112 | tf_op jit(solution)/shard_map/all_to_all | solution.py:188
  98.6 0.1 slice.52
  98.7 2.1 %copy.125 = f32[8,2,2,16,17]{2,1,4,3,0:T(2,128)S(1)} copy(f32[8,2,2,16,17]{4,0,3,2,1:T(8,128)S(1)} %bitcast.157) | data formatting | bytes 69632 | tf_op jit(solution)/shard_map/reshape | solution.py:190
  100.8 13.8 %gather_fusion.2 = f32[2176,2,2]{2,1,0:T(2,128)} fusion(f32[8,2,2,272]{2,1,3,0:T(2,128)S(1)} %bitcast.158, s32[2176]{0:T(1024)S(1)} %reshape.329), kind=kCustom, calls=%fused_computation.1.clone | custom fusion | bytes 87040 | tf_op jit(solution)/shard_map/jit(take_along_axis)/gather | solution.py:191
  114.5 2.8 %copy.114 = f32[8,272,2,2]{1,0,3,2:T(8,128)S(1)} copy(f32[8,272,2,2]{3,2,1,0:T(2,128)} %bitcast.160) | data formatting | bytes 69632 | tf_op jit(solution)/shard_map/jit(take_along_axis)/gather | solution.py:191
  117.4 0.1 reshape.290
  117.6 0.1 pad_maximum_fusion
  117.7 0.7 reshape.291
  118.3 0.1 fusion.173
  118.4 0.3 copy.128
  118.7 0.8 fusion.25
  119.5 0.3 copy.129
  119.8 0.8 fusion.21
  120.6 0.8 convolution_subtract_fusion
  121.4 0.8 convolution_add_fusion
  122.1 1.4 convolution_bitcast_fusion
  123.5 1.4 fusion.3
  124.9 0.1 all_to_all.37
  125.0 0.1 copy.120
  125.1 11.3 %all_to_all.45 = f32[2,8,2700]{2,0,1:T(2,128)S(1)} all-to-all(f32[2,8,2700]{2,0,1:T(2,128)S(1)} %copy.120), channel_id=1, replica_groups=mesh['lat'=16,'freq'=8] {'freq'}, dimensions={1} | all-to-all | bytes 345600 | tf_op jit(solution)/shard_map/all_to_all | solution.py:195
  136.4 0.8 all_to_all.40
  (32 shorter events, 1.0 us)
Async XLA Ops:
  0.0 15.2 %copy-start = (bf16[17,2,2176]{2,1,0:T(2,128)(2,1)S(1)}, bf16[17,2,2176]{2,1,0:T(2,128)(2,1)}, u32[]{:S(2)}) copy-start(bf16[17,2,2176]{2,1,0:T(2,128)(2,1)} %param.9) | copy-start | bytes 443908
  1.7 23.9 %all-to-all-start = ((f32[8,2,2700]{2,1,0:T(2,128)}), f32[8,2,2700]{2,1,0:T(2,128)S(1)}, u32[]{:S(2)}, u32[]{:S(2)}) async-start(f32[8,2,2700]{2,1,0:T(2,128)} %all_to_all.32), calls=%async_computation | async-start | bytes 360448 | tf_op jit(solution)/shard_map/all_to_all | solution.py:159
  11.6 1.9 %copy-start.1 = (bf16[511,1350]{0,1:T(8,128)(2,1)S(1)}, bf16[511,1350]{0,1:T(8,128)(2,1)}, u32[]{:S(2)}) copy-start(bf16[511,1350]{0,1:T(8,128)(2,1)} %param.13) | copy-start | bytes 4139104
  24.1 0.7 copy-start.2
  52.4 21.1 %all-to-all-start.1 = ((f32[128,2,2,86]{3,2,1,0:T(2,128)}), f32[128,2,2,86]{3,2,1,0:T(2,128)S(1)}, u32[]{:S(2)}, u32[]{:S(2)}) async-start(f32[128,2,2,86]{3,2,1,0:T(2,128)} %copy.107), calls=%async_computation.1 | async-start | bytes 524288 | tf_op jit(solution)/shard_map/all_to_all | solution.py:170
  83.3 15.2 %all-to-all-start.2 = ((f32[128,2,2,85]{3,2,1,0:T(2,128)}), f32[128,2,2,85]{3,2,1,0:T(2,128)S(1)}, u32[]{:S(2)}, u32[]{:S(2)}) async-start(f32[128,2,2,85]{3,2,1,0:T(2,128)} %bitcast.152), calls=%async_computation.2 | async-start | bytes 524288 | tf_op jit(solution)/shard_map/all_to_all | solution.py:188

commit v6 on v5

--- a/solution.py
+++ b/solution.py
@@ -147,18 +147,13 @@
     share = sub - per_slot
     padded = held + share * blocks
     positions = order_table.reshape(blocks, bands, per_slot).transpose(1, 0, 2).reshape(bands, held) // bands
-    slot_of = jnp.sum(
-        jnp.where(
-            positions[:, :, None] == jnp.arange(held, dtype=jnp.int32)[None, None, :],
-            jnp.arange(held, dtype=jnp.int32)[None, :, None],
-            0,
-        ),
-        axis=1,
-    )
+    selector = (
+        positions[:, None, :] == jnp.arange(held, dtype=jnp.int32)[None, :, None]
+    ).astype(jnp.float32)
 
     whole_rows = lax.all_to_all(gravity, "freq", split_axis=0, concat_axis=1, tiled=True)
     terms = forward_bands(whole_rows.reshape(mine, PA, PB), 0, bands)
-    own = jnp.take_along_axis(terms[..., :held], positions[:, None, None, :], axis=3)
+    own = jnp.einsum("brct,bts->brcs", terms[..., :held], selector, precision=highest)
     own = own.reshape(bands, mine, 2, blocks, per_slot)
     rest = jnp.pad(terms[..., held:], ((0, 0), (0, 0), (0, 0), (0, padded - band_width)))
     rest = rest.reshape(bands, mine, 2, blocks, share)
@@ -188,7 +183,7 @@
     by_source = lax.all_to_all(stokes, everyone, split_axis=0, concat_axis=0, tiled=True)
     by_source = by_source.reshape(blocks, bands, mine, 2, sub).transpose(1, 2, 3, 0, 4)
     slots_back = by_source[..., :per_slot].reshape(bands, mine, 2, held)
-    slots_back = jnp.take_along_axis(slots_back, slot_of[:, None, None, :], axis=3)
+    slots_back = jnp.einsum("brcs,bts->brct", slots_back, selector, precision=highest)
     rest_back = by_source[..., per_slot:].reshape(bands, mine, 2, blocks * share)
     by_band = jnp.concatenate([slots_back, rest_back], axis=3)[..., :band_width]
     grid_rows = inverse_rows(by_band, jnp.arange(bands, dtype=jnp.int32), bands)

time: 138 us -> 102 us (0.74)
  local copies, waits for them, and re-layouts: 51.9 us -> 13.8 us
  matrix products: 19.6 us -> 22.5 us
    gather x6 -> x0, local copies, waits for them, and re-layouts: 33.4 us -> none  [the longest x3 16.8 us: per_device(): jnp.take_along_axis(terms[..., :held], positions[:, None, None, :], axis=3)]
    dot_general x0 -> x2, matrix products: none -> 2.94 us  [the longest x1 1.73 us: per_device(): jnp.einsum('brcs,bts->brct', slots_back, selector, precision=highest)]
    unnamed x10 -> x9, local copies, waits for them, and re-layouts: 5.06 us -> 2.35 us
    reshape x1, local copies, waits for them, and re-layouts: 2.06 us -> 0.19 us  [per_device(): slots_back = by_source[..., :per_slot].reshape(bands, mine, 2, held)]
    all_to_all x1, waiting for transfers between devices: 9.12 us -> 10.6 us  [per_device(): lax.all_to_all(payload, everyone, split_axis=0, concat_axis=0, tiled=True)]
  transfers between devices with their start and end apart: 3 -> 3, of which waited for: 2 -> 2; matrix products, arithmetic and copies ran while one was open for 12% -> 16% of each run, Pallas kernels for 0% -> 0%
where the time goes in v6:
time: 102 us
  starting transfers between devices  23 us (23%)
  matrix products  22.5 us (22%)
  waiting for transfers between devices  20.3 us (20%)
  local copies, waits for them, and re-layouts  13.8 us (14%)
  blocking collectives  11.3 us (11%)
  Pallas kernels  6.86 us (7%)
  other arithmetic  3.81 us (4%)
    all_to_all x1, blocking collectives, per_device(): lax.all_to_all(grid_rows.reshape(mine, L), 'freq', split_axis=1, concat_a...  11.3 us
    all_to_all x1, waiting for transfers between devices, per_device(): lax.all_to_all(payload, everyone, split_axis=0, concat_axis=0, tiled=True)  10.6 us
    all_to_all x1, starting transfers between devices, per_device(): lax.all_to_all(payload, everyone, split_axis=0, concat_axis=0, tiled=True)  10.5 us
    all_to_all x1, waiting for transfers between devices, per_device(): lax.all_to_all(stokes, everyone, split_axis=0, concat_axis=0, tiled=True)  9.72 us
    dot_general x1, matrix products, per_device(): jnp.einsum('ocn,onq->ocq', coef, legendre, preferred_element_type=jnp.flo...  8.95 us
    all_to_all x1, starting transfers between devices, per_device(): lax.all_to_all(gravity, 'freq', split_axis=0, concat_axis=1, tiled=True)  7.89 us
    pallas_call x1, Pallas kernels, toeplitz_stokes(): pl.pallas_call(stokes_body, out_shape=jax.ShapeDtypeStruct((2, total, LAN...  6.86 us
    all_to_all x1, starting transfers between devices, per_device(): lax.all_to_all(stokes, everyone, split_axis=0, concat_axis=0, tiled=True)  4.58 us
  transfers between devices with their start and end apart: 3, of which 2 were waited for; matrix products, arithmetic and copies ran while one was open for 16% of the time, Pallas kernels for 0%

profile of v6, /device:TPU:0, one launch (start us, length us, event | category | flops | bytes accessed | tf_op | source)
XLA Modules:
  0.0 102.0 jit_solution(7478522348862205472)
XLA Ops:
  0.0 1.8 %all_to_all.32 = f32[8,2,2700]{2,1,0:T(2,128)} reshape(f32[16,2700]{1,0:T(8,128)} %param.6) | data formatting | bytes 345600 | tf_op jit(solution)/shard_map/all_to_all | solution.py:154
  1.8 7.9 %all-to-all-start = ((f32[8,2,2700]{2,1,0:T(2,128)}), f32[8,2,2700]{2,1,0:T(2,128)S(1)}, u32[]{:S(2)}, u32[]{:S(2)}) async-start(f32[8,2,2700]{2,1,0:T(2,128)} %all_to_all.32), calls=%async_computation | async-start | bytes 360448 | tf_op jit(solution)/shard_map/all_to_all | solution.py:154
  9.7 0.9 reshape.188
  10.6 0.1 reshape.189
  10.8 0.1 fusion.142
  10.8 0.1 compare_and_fusion
  10.9 1.8 %copy.73 = bf16[511,1350]{1,0:T(8,128)(2,1)S(1)} copy(bf16[511,1350]{0,1:T(8,128)(2,1)} %param.11) | data formatting | bytes 2759400 | tf_op args[5]
  12.8 0.6 gather_fusion
  13.4 0.1 copy.72
  13.5 0.2 pad_dynamic-slice_fusion
  13.7 0.1 pad_maximum_fusion.1
  13.8 0.4 rev.3
  14.2 0.7 pad_convert_fusion.k_ref
  14.9 8.9 %convolution_convert_fusion = bf16[17,2,256]{2,1,0:T(2,128)(2,1)S(1)} fusion(bf16[17,2,2176]{2,1,0:T(2,128)(2,1)S(1)} %copy-done, bf16[17,2176,256]{2,1,0:T(8,128)(2,1)} %param.8), kind=kOutput, calls=%fused_computation.22 | convolution fusion | flops 37888512 | bytes 19105280 | tf_op jit(solution)/shard_map/ocn,onq->ocq/dot_general | solution.py:170
  23.9 0.1 multiply_cosine_fusion
  24.0 0.2 copy.80
  24.2 0.6 fusion.59
  24.8 0.1 reshape.190
  25.0 1.0 convolution_bitcast_fusion.2
  26.0 1.0 fusion.7
  27.0 0.7 fusion.89
  27.7 0.7 fusion.87
  28.4 0.7 fusion.12
  29.1 0.7 fusion.11
  29.9 0.5 copy.75
  30.4 0.5 reshape.191
  30.9 0.1 slice.43
  31.0 1.2 %fusion.3 = f32[8,2,2,272]{3,2,1,0:T(2,128)S(1)} fusion(s32[8,272]{1,0:T(8,128)S(1)} %add_select_fusion.6, f32[8,2,2,272]{3,0,2,1:T(8,128)S(1)} %slice.42), kind=kOutput, calls=%fused_computation.4 | convolution fusion | flops 29001728 | bytes 78336 | tf_op jit(solution)/shard_map/brct,bts->brcs/dot_general | solution.py:156
  32.2 0.2 reshape.192
  32.4 0.2 reshape.193
  32.6 0.1 broadcast_in_dim.11
  32.7 0.2 maximum_bitcast_fusion
  32.9 0.9 copy.78
  33.9 10.5 %all-to-all-start.1 = ((f32[128,2,2,86]{3,1,2,0:T(2,128)}), f32[128,2,2,86]{3,1,2,0:T(2,128)S(1)}, u32[]{:S(2)}, u32[]{:S(2)}) async-start(f32[128,2,2,86]{3,1,2,0:T(2,128)} %bitcast.19), calls=%async_computation.1 | async-start | bytes 524288 | tf_op jit(solution)/shard_map/all_to_all | solution.py:165
  44.4 10.6 %all-to-all-done.1 = f32[128,2,2,86]{3,1,2,0:T(2,128)S(1)} async-done(((f32[128,2,2,86]{3,1,2,0:T(2,128)}), f32[128,2,2,86]{3,1,2,0:T(2,128)S(1)}, u32[]{:S(2)}, u32[]{:S(2)}) %all-to-all-start.1) | async-done | bytes 176160 | tf_op jit(solution)/shard_map/all_to_all | solution.py:165
  54.9 0.1 copy.79
  55.0 0.2 slice_reduce_fusion
  55.2 0.1 fusion.68
  55.3 0.7 pad_convert_fusion.1.w_ref
  56.1 6.9 %shard_map.64 = f32[2,256,128]{2,1,0:T(8,128)} custom-call(f32[520,128]{1,0:T(8,128)} %pad_convert_fusion.k_ref, f32[2,256,128]{2,1,0:T(8,128)} %pad_convert_fusion.1.w_ref), custom_call_target="tpu_custom_call" | custom-call | tf_op jit(solution)/shard_map/pallas_call | solution.py:125
  62.9 1.7 %copy.106 = f32[2,128,2,85]{3,2,0,1:T(2,128)} copy(f32[2,128,2,85]{3,2,1,0:T(2,128)} %bitcast.135) | data formatting | bytes 348160 | tf_op jit(solution)/shard_map/reshape | solution.py:182
  64.6 4.6 %all-to-all-start.2 = ((f32[128,2,2,85]{3,1,2,0:T(2,128)}), f32[128,2,2,85]{3,1,2,0:T(2,128)S(1)}, u32[]{:S(2)}, u32[]{:S(2)}) async-start(f32[128,2,2,85]{3,1,2,0:T(2,128)} %bitcast.128), calls=%async_computation.2 | async-start | bytes 524288 | tf_op jit(solution)/shard_map/all_to_all | solution.py:183
  69.2 0.9 fusion.42
  70.1 9.7 %all-to-all-done.2 = f32[128,2,2,85]{3,1,2,0:T(2,128)S(1)} async-done(((f32[128,2,2,85]{3,1,2,0:T(2,128)}), f32[128,2,2,85]{3,1,2,0:T(2,128)S(1)}, u32[]{:S(2)}, u32[]{:S(2)}) %all-to-all-start.2) | async-done | bytes 174112 | tf_op jit(solution)/shard_map/all_to_all | solution.py:183
  79.8 0.2 copy.105
  80.0 0.1 slice.48
  80.1 0.3 reshape.220
  80.4 0.2 reshape.198
  80.6 1.7 %fusion.1 = f32[8,2,2,272]{3,2,1,0:T(2,128)S(1)} fusion(f32[8,2,2,272]{3,2,1,0:T(2,128)S(1)} %reshape.198, s32[8,272]{1,0:T(8,128)S(1)} %add_select_fusion.6), kind=kOutput, calls=%fused_computation.3 | convolution fusion | flops 29001728 | bytes 78336 | tf_op jit(solution)/shard_map/brcs,bts->brct/dot_general | solution.py:186
  82.4 0.1 pad_maximum_fusion
  82.5 0.7 reshape.200
  83.1 0.1 fusion.179
  83.3 0.3 copy.97
  83.5 0.8 fusion.32
  84.3 0.3 copy.98
  84.6 0.8 fusion.28
  85.4 0.8 convolution_subtract_fusion
  86.2 0.8 convolution_add_fusion
  86.9 1.4 %convolution_bitcast_fusion = f32[144,2,150]{2,0,1:T(8,128)S(1)} fusion(f32[8,2,18,150]{3,2,1,0:T(8,128)S(1)} %convolution_add_fusion, f32[8,2,18,150]{3,2,1,0:T(8,128)S(1)} %convolution_subtract_fusion, f32[8,18,150]{2,1,0:T(8,128)S(1)} %get-tuple-element.8, f32[8,18,150]{2,1,0:T(8,128)S(1)} %get-tuple-element.7, s32[8,18]{1,0:T(8,128)S(1)} %iota_add_fusion), kind=kOutput, calls=%fused_computation.10 | convolution fusion | flops 74965824 | bytes 691776 | tf_op jit(solution)/shard_map/brsn,bsa->ran/dot_general | solution.py:82
  88.3 1.4 %fusion.10 = f32[2,144,150]{2,1,0:T(8,128)S(1)} fusion(f32[144,2,150]{2,0,1:T(8,128)S(1)} %convolution_bitcast_fusion, f32[8,2,18,150]{3,2,1,0:T(8,128)S(1)} %convolution_add_fusion, f32[8,2,18,150]{3,2,1,0:T(8,128)S(1)} %convolution_subtract_fusion, f32[8,18,150]{2,1,0:T(8,128)S(1)} %get-tuple-element.8, f32[8,18,150]{2,1,0:T(8,128)S(1)} %get-tuple-element.7, ...), kind=kOutput, calls=%fused_computation.17 | convolution fusion | flops 75052224 | bytes 864576 | tf_op jit(solution)/shard_map/brsn,bsa->ran/dot_general | solution.py:80
  89.7 0.1 all_to_all.37
  89.8 0.1 copy.89
  89.9 11.3 %all_to_all.45 = f32[2,8,2700]{2,0,1:T(2,128)S(1)} all-to-all(f32[2,8,2700]{2,0,1:T(2,128)S(1)} %copy.89), channel_id=1, replica_groups=mesh['lat'=16,'freq'=8] {'freq'}, dimensions={1} | all-to-all | bytes 345600 | tf_op jit(solution)/shard_map/all_to_all | solution.py:190
  101.2 0.8 all_to_all.40
  (19 shorter events, 0.2 us)
Async XLA Ops:
  0.0 14.9 %copy-start = (bf16[17,2,2176]{2,1,0:T(2,128)(2,1)S(1)}, bf16[17,2,2176]{2,1,0:T(2,128)(2,1)}, u32[]{:S(2)}) copy-start(bf16[17,2,2176]{2,1,0:T(2,128)(2,1)} %param.7) | copy-start | bytes 443908
  0.0 12.7 %copy-start.1 = (bf16[511,1350]{0,1:T(8,128)(2,1)S(1)}, bf16[511,1350]{0,1:T(8,128)(2,1)}, u32[]{:S(2)}) copy-start(bf16[511,1350]{0,1:T(8,128)(2,1)} %param.11) | copy-start | bytes 4139104
  1.8 23.0 %all-to-all-start = ((f32[8,2,2700]{2,1,0:T(2,128)}), f32[8,2,2700]{2,1,0:T(2,128)S(1)}, u32[]{:S(2)}, u32[]{:S(2)}) async-start(f32[8,2,2700]{2,1,0:T(2,128)} %all_to_all.32), calls=%async_computation | async-start | bytes 360448 | tf_op jit(solution)/shard_map/all_to_all | solution.py:154
  14.9 9.0 %copy-start.2 = (s32[16]{0:T(128)S(1)}, s32[16]{0:T(128)}, u32[]{:S(2)}) copy-start(s32[16]{0:T(128)} %param.10) | copy-start | bytes 196
  33.9 21.1 %all-to-all-start.1 = ((f32[128,2,2,86]{3,1,2,0:T(2,128)}), f32[128,2,2,86]{3,1,2,0:T(2,128)S(1)}, u32[]{:S(2)}, u32[]{:S(2)}) async-start(f32[128,2,2,86]{3,1,2,0:T(2,128)} %bitcast.19), calls=%async_computation.1 | async-start | bytes 524288 | tf_op jit(solution)/shard_map/all_to_all | solution.py:165
  64.6 15.2 %all-to-all-start.2 = ((f32[128,2,2,85]{3,1,2,0:T(2,128)}), f32[128,2,2,85]{3,1,2,0:T(2,128)S(1)}, u32[]{:S(2)}, u32[]{:S(2)}) async-start(f32[128,2,2,85]{3,1,2,0:T(2,128)} %bitcast.128), calls=%async_computation.2 | async-start | bytes 524288 | tf_op jit(solution)/shard_map/all_to_all | solution.py:183

commit v7 on v6

--- a/solution.py
+++ b/solution.py
@@ -162,6 +162,7 @@
     carried = jnp.broadcast_to(weight[None, :, None, None, None], (bands, mine, 2, blocks, 1))
     payload = jnp.concatenate([own, rest, carried], axis=4).transpose(3, 0, 1, 2, 4)
     payload = payload.reshape(devices, mine, 2, sub + 1)
+    payload, coef, legendre = lax.optimization_barrier((payload, coef, legendre))
     observed = lax.all_to_all(payload, everyone, split_axis=0, concat_axis=0, tiled=True)
     observed = observed.reshape(total_rows, 2, sub + 1)
     weight_all = observed[:, 0, sub]

time: 102 us -> 97.1 us (0.952)
  waiting for transfers between devices: 20.3 us -> 13.4 us
  starting transfers between devices: 23 us -> 24.5 us
    all_to_all x1, waiting for transfers between devices: 10.6 us -> 1.3 us  [per_device(): lax.all_to_all(payload, everyone, split_axis=0, concat_axis=0, tiled=True)]
    all_to_all x1, starting transfers between devices: 4.58 us -> 8.3 us  [per_device(): lax.all_to_all(stokes, everyone, split_axis=0, concat_axis=0, tiled=True)]
    all_to_all x1, waiting for transfers between devices: 0.01 us -> 2.4 us  [per_device(): lax.all_to_all(gravity, 'freq', split_axis=0, concat_axis=1, tiled=True)]
    all_to_all x1, starting transfers between devices: 10.5 us -> 8.28 us  [per_device(): lax.all_to_all(payload, everyone, split_axis=0, concat_axis=0, tiled=True)]
  transfers between devices with their start and end apart: 3 -> 3, of which waited for: 2 -> 3; matrix products, arithmetic and copies ran while one was open for 16% -> 16% of each run, Pallas kernels for 0% -> 0%
where the time goes in v7:
time: 97.1 us; the launch traced here: 96.6 us
  starting transfers between devices  24.5 us (25%)
  matrix products  22.5 us (23%)
  local copies, waits for them, and re-layouts  13.9 us (14%)
  waiting for transfers between devices  13.4 us (14%)
  blocking collectives  11.3 us (12%)
  Pallas kernels  6.86 us (7%)
  other arithmetic  3.8 us (4%)
    all_to_all x1, blocking collectives, per_device(): lax.all_to_all(grid_rows.reshape(mine, L), 'freq', split_axis=1, concat_a...  11.3 us
    all_to_all x1, waiting for transfers between devices, per_device(): lax.all_to_all(stokes, everyone, split_axis=0, concat_axis=0, tiled=True)  9.72 us
    dot_general x1, matrix products, per_device(): jnp.einsum('ocn,onq->ocq', coef, legendre, preferred_element_type=jnp.flo...  8.94 us
    all_to_all x1, starting transfers between devices, per_device(): lax.all_to_all(stokes, everyone, split_axis=0, concat_axis=0, tiled=True)  8.3 us
    all_to_all x1, starting transfers between devices, per_device(): lax.all_to_all(payload, everyone, split_axis=0, concat_axis=0, tiled=True)  8.28 us
    all_to_all x1, starting transfers between devices, per_device(): lax.all_to_all(gravity, 'freq', split_axis=0, concat_axis=1, tiled=True)  7.89 us
    pallas_call x1, Pallas kernels, toeplitz_stokes(): pl.pallas_call(stokes_body, out_shape=jax.ShapeDtypeStruct((2, total, LAN...  6.86 us
    all_to_all x1, waiting for transfers between devices, per_device(): lax.all_to_all(gravity, 'freq', split_axis=0, concat_axis=1, tiled=True)  2.4 us
  transfers between devices with their start and end apart: 3, of which 3 were waited for; matrix products, arithmetic and copies ran while one was open for 16% of the time, Pallas kernels for 0%

profile of v7, /device:TPU:0, one launch (start us, length us, event | category | flops | bytes accessed | tf_op | source)
XLA Modules:
  0.0 96.6 jit_solution(6146844216655746444)
XLA Ops:
  0.0 1.8 %all_to_all.32 = f32[8,2,2700]{2,1,0:T(2,128)} reshape(f32[16,2700]{1,0:T(8,128)} %param.6) | data formatting | bytes 345600 | tf_op jit(solution)/shard_map/all_to_all | solution.py:154
  1.8 7.9 %all-to-all-start = ((f32[8,2,2700]{2,1,0:T(2,128)}), f32[8,2,2700]{2,1,0:T(2,128)S(1)}, u32[]{:S(2)}, u32[]{:S(2)}) async-start(f32[8,2,2700]{2,1,0:T(2,128)} %all_to_all.32), calls=%async_computation | async-start | bytes 360448 | tf_op jit(solution)/shard_map/all_to_all | solution.py:154
  9.7 0.9 reshape.188
  10.6 0.1 reshape.189
  10.8 0.1 fusion.142
  10.9 1.8 %copy.73 = bf16[511,1350]{1,0:T(8,128)(2,1)S(1)} copy(bf16[511,1350]{0,1:T(8,128)(2,1)} %param.11) | data formatting | bytes 2759400 | tf_op args[5]
  12.8 0.6 gather_fusion
  13.4 0.1 copy.72
  13.5 0.2 pad_dynamic-slice_fusion
  13.7 0.1 pad_maximum_fusion.1
  13.8 0.4 rev.3
  14.2 0.7 pad_convert_fusion.k_ref
  14.9 0.1 multiply_cosine_fusion
  15.0 0.6 fusion.59
  15.7 2.4 %all-to-all-done = f32[8,2,2700]{2,1,0:T(2,128)S(1)} async-done(((f32[8,2,2700]{2,1,0:T(2,128)}), f32[8,2,2700]{2,1,0:T(2,128)S(1)}, u32[]{:S(2)}, u32[]{:S(2)}) %all-to-all-start) | async-done | bytes 172832 | tf_op jit(solution)/shard_map/all_to_all | solution.py:154
  18.1 0.1 reshape.190
  18.2 1.0 %convolution_bitcast_fusion.2 = f32[2,150,144]{1,2,0:T(8,128)S(1)} fusion(f32[2,144,150]{2,1,0:T(8,128)S(1)} %reshape.190), kind=kOutput, calls=%fused_computation.14 | convolution fusion | flops 74836224 | bytes 345600 | tf_op jit(solution)/shard_map/rab,ak->rbk/dot_general | solution.py:29
  19.2 1.0 %fusion.7 = f32[2,150,144]{1,2,0:T(8,128)S(1)} fusion(f32[2,144,150]{2,1,0:T(8,128)S(1)} %reshape.190), kind=kOutput, calls=%fused_computation.13 | convolution fusion | flops 74879424 | bytes 345600 | tf_op jit(solution)/shard_map/rab,ak->rbk/dot_general | solution.py:30
  20.2 0.7 fusion.89
  21.0 0.7 fusion.87
  21.7 0.7 fusion.12
  22.4 0.7 fusion.11
  23.1 0.5 copy.75
  23.7 0.5 reshape.191
  24.2 0.1 slice.43
  24.3 1.2 %fusion.3 = f32[8,2,2,272]{3,2,1,0:T(2,128)S(1)} fusion(s32[8,272]{1,0:T(8,128)S(1)} %add_select_fusion.6, f32[8,2,2,272]{3,0,2,1:T(8,128)S(1)} %slice.42), kind=kOutput, calls=%fused_computation.4 | convolution fusion | flops 29001728 | bytes 78336 | tf_op jit(solution)/shard_map/brct,bts->brcs/dot_general | solution.py:156
  25.5 0.2 reshape.192
  25.7 0.2 reshape.193
  25.9 0.1 broadcast_in_dim.11
  26.0 0.2 maximum_bitcast_fusion
  26.2 0.9 copy.78
  27.1 8.3 %all-to-all-start.1 = ((f32[128,2,2,86]{3,1,2,0:T(2,128)}), f32[128,2,2,86]{3,1,2,0:T(2,128)S(1)}, u32[]{:S(2)}, u32[]{:S(2)}) async-start(f32[128,2,2,86]{3,1,2,0:T(2,128)} %bitcast.19), calls=%async_computation.1 | async-start | bytes 524288 | tf_op jit(solution)/shard_map/all_to_all | solution.py:166
  35.4 8.9 %convolution_convert_fusion = bf16[17,2,256]{2,1,0:T(2,128)(2,1)S(1)} fusion(bf16[17,2,2176]{2,1,0:T(2,128)(2,1)S(1)} %copy-done, bf16[17,2176,256]{2,1,0:T(8,128)(2,1)} %param.8), kind=kOutput, calls=%fused_computation.22 | convolution fusion | flops 37888512 | bytes 19105280 | tf_op jit(solution)/shard_map/ocn,onq->ocq/dot_general | solution.py:171
  44.4 0.2 copy.80
  44.5 1.3 %all-to-all-done.1 = f32[128,2,2,86]{3,1,2,0:T(2,128)S(1)} async-done(((f32[128,2,2,86]{3,1,2,0:T(2,128)}), f32[128,2,2,86]{3,1,2,0:T(2,128)S(1)}, u32[]{:S(2)}, u32[]{:S(2)}) %all-to-all-start.1) | async-done | bytes 176160 | tf_op jit(solution)/shard_map/all_to_all | solution.py:166
  45.8 0.1 copy.79
  45.9 0.2 slice_reduce_fusion
  46.1 0.1 fusion.68
  46.2 0.7 pad_convert_fusion.1.w_ref
  47.0 6.9 %shard_map.64 = f32[2,256,128]{2,1,0:T(8,128)} custom-call(f32[520,128]{1,0:T(8,128)} %pad_convert_fusion.k_ref, f32[2,256,128]{2,1,0:T(8,128)} %pad_convert_fusion.1.w_ref), custom_call_target="tpu_custom_call" | custom-call | tf_op jit(solution)/shard_map/pallas_call | solution.py:125
  53.8 1.7 %copy.106 = f32[2,128,2,85]{3,2,0,1:T(2,128)} copy(f32[2,128,2,85]{3,2,1,0:T(2,128)} %bitcast.135) | data formatting | bytes 348160 | tf_op jit(solution)/shard_map/reshape | solution.py:183
  55.5 8.3 %all-to-all-start.2 = ((f32[128,2,2,85]{3,1,2,0:T(2,128)}), f32[128,2,2,85]{3,1,2,0:T(2,128)S(1)}, u32[]{:S(2)}, u32[]{:S(2)}) async-start(f32[128,2,2,85]{3,1,2,0:T(2,128)} %bitcast.128), calls=%async_computation.2 | async-start | bytes 524288 | tf_op jit(solution)/shard_map/all_to_all | solution.py:184
  63.9 0.9 fusion.42
  64.7 9.7 %all-to-all-done.2 = f32[128,2,2,85]{3,1,2,0:T(2,128)S(1)} async-done(((f32[128,2,2,85]{3,1,2,0:T(2,128)}), f32[128,2,2,85]{3,1,2,0:T(2,128)S(1)}, u32[]{:S(2)}, u32[]{:S(2)}) %all-to-all-start.2) | async-done | bytes 174112 | tf_op jit(solution)/shard_map/all_to_all | solution.py:184
  74.5 0.2 copy.105
  74.6 0.1 slice.48
  74.7 0.3 reshape.220
  75.0 0.2 reshape.198
  75.2 1.7 %fusion.1 = f32[8,2,2,272]{3,2,1,0:T(2,128)S(1)} fusion(f32[8,2,2,272]{3,2,1,0:T(2,128)S(1)} %reshape.198, s32[8,272]{1,0:T(8,128)S(1)} %add_select_fusion.6), kind=kOutput, calls=%fused_computation.3 | convolution fusion | flops 29001728 | bytes 78336 | tf_op jit(solution)/shard_map/brcs,bts->brct/dot_general | solution.py:187
  77.0 0.1 pad_maximum_fusion
  77.1 0.7 reshape.200
  77.8 0.1 fusion.179
  77.9 0.3 copy.97
  78.1 0.8 fusion.32
  78.9 0.3 copy.98
  79.2 0.8 fusion.28
  80.0 0.8 convolution_subtract_fusion
  80.8 0.8 convolution_add_fusion
  81.6 1.4 %convolution_bitcast_fusion = f32[144,2,150]{2,0,1:T(8,128)S(1)} fusion(f32[8,2,18,150]{3,2,1,0:T(8,128)S(1)} %convolution_add_fusion, f32[8,2,18,150]{3,2,1,0:T(8,128)S(1)} %convolution_subtract_fusion, f32[8,18,150]{2,1,0:T(8,128)S(1)} %get-tuple-element.14, f32[8,18,150]{2,1,0:T(8,128)S(1)} %get-tuple-element.13, s32[8,18]{1,0:T(8,128)S(1)} %iota_add_fusion), kind=kOutput, calls=%fused_computation.10 | convolution fusion | flops 74965824 | bytes 691776 | tf_op jit(solution)/shard_map/brsn,bsa->ran/dot_general | solution.py:82
  82.9 1.4 %fusion.10 = f32[2,144,150]{2,1,0:T(8,128)S(1)} fusion(f32[144,2,150]{2,0,1:T(8,128)S(1)} %convolution_bitcast_fusion, f32[8,2,18,150]{3,2,1,0:T(8,128)S(1)} %convolution_add_fusion, f32[8,2,18,150]{3,2,1,0:T(8,128)S(1)} %convolution_subtract_fusion, f32[8,18,150]{2,1,0:T(8,128)S(1)} %get-tuple-element.14, f32[8,18,150]{2,1,0:T(8,128)S(1)} %get-tuple-element.13, ...), kind=kOutput, calls=%fused_computation.17 | convolution fusion | flops 75052224 | bytes 864576 | tf_op jit(solution)/shard_map/brsn,bsa->ran/dot_general | solution.py:80
  84.3 0.1 all_to_all.37
  84.4 0.1 copy.89
  84.5 11.3 %all_to_all.45 = f32[2,8,2700]{2,0,1:T(2,128)S(1)} all-to-all(f32[2,8,2700]{2,0,1:T(2,128)S(1)} %copy.89), channel_id=1, replica_groups=mesh['lat'=16,'freq'=8] {'freq'}, dimensions={1} | all-to-all | bytes 345600 | tf_op jit(solution)/shard_map/all_to_all | solution.py:191
  95.8 0.8 all_to_all.40
  (19 shorter events, 0.2 us)
Async XLA Ops:
  0.0 35.4 %copy-start = (bf16[17,2,2176]{2,1,0:T(2,128)(2,1)S(1)}, bf16[17,2,2176]{2,1,0:T(2,128)(2,1)}, u32[]{:S(2)}) copy-start(bf16[17,2,2176]{2,1,0:T(2,128)(2,1)} %param.7) | copy-start | bytes 443908
  0.0 12.8 %copy-start.1 = (bf16[511,1350]{0,1:T(8,128)(2,1)S(1)}, bf16[511,1350]{0,1:T(8,128)(2,1)}, u32[]{:S(2)}) copy-start(bf16[511,1350]{0,1:T(8,128)(2,1)} %param.11) | copy-start | bytes 4139104
  1.8 16.2 %all-to-all-start = ((f32[8,2,2700]{2,1,0:T(2,128)}), f32[8,2,2700]{2,1,0:T(2,128)S(1)}, u32[]{:S(2)}, u32[]{:S(2)}) async-start(f32[8,2,2700]{2,1,0:T(2,128)} %all_to_all.32), calls=%async_computation | async-start | bytes 360448 | tf_op jit(solution)/shard_map/all_to_all | solution.py:154
  10.9 4.0 %copy-start.2 = (s32[16]{0:T(128)S(1)}, s32[16]{0:T(128)}, u32[]{:S(2)}) copy-start(s32[16]{0:T(128)} %param.10) | copy-start | bytes 196
  27.1 18.7 %all-to-all-start.1 = ((f32[128,2,2,86]{3,1,2,0:T(2,128)}), f32[128,2,2,86]{3,1,2,0:T(2,128)S(1)}, u32[]{:S(2)}, u32[]{:S(2)}) async-start(f32[128,2,2,86]{3,1,2,0:T(2,128)} %bitcast.19), calls=%async_computation.1 | async-start | bytes 524288 | tf_op jit(solution)/shard_map/all_to_all | solution.py:166
  55.5 18.9 %all-to-all-start.2 = ((f32[128,2,2,85]{3,1,2,0:T(2,128)}), f32[128,2,2,85]{3,1,2,0:T(2,128)S(1)}, u32[]{:S(2)}, u32[]{:S(2)}) async-start(f32[128,2,2,85]{3,1,2,0:T(2,128)} %bitcast.128), calls=%async_computation.2 | async-start | bytes 524288 | tf_op jit(solution)/shard_map/all_to_all | solution.py:184

commit v8 on v7

--- a/solution.py
+++ b/solution.py
@@ -20,66 +20,64 @@
     return phase.astype(jnp.float32) * (2.0 * np.pi / period)
 
 
-def forward_bands(grid, first_start, bands):
+def forward_bands(grid, bands):
     rows = grid.shape[0]
-    count_one = grid.shape[1]
-    first_index = first_start + jnp.arange(count_one, dtype=jnp.int32)
-    freq_one = jnp.arange(PA, dtype=jnp.int32)
-    theta_one = angle_table(first_index[:, None], freq_one[None, :], PA)
-    section_re = jnp.einsum("rab,ak->rbk", grid, jnp.cos(theta_one), precision=highest)
-    section_im = -jnp.einsum("rab,ak->rbk", grid, jnp.sin(theta_one), precision=highest)
+    first_index = jnp.arange(PA, dtype=jnp.int32)
+    theta_one = angle_table(first_index[:, None], first_index[None, :], PA)
+    stage_one = jnp.concatenate([jnp.cos(theta_one), -jnp.sin(theta_one)], axis=1)
+    section = jnp.einsum("rab,ak->rbk", grid, stage_one, precision=highest)
+    section_re = section[..., :PA]
+    section_im = section[..., PA:]
     second_index = jnp.arange(PB, dtype=jnp.int32)
-    twist = angle_table(second_index[:, None], freq_one[None, :], L)
+    twist = angle_table(second_index[:, None], first_index[None, :], L)
     twist_cos = jnp.cos(twist)
     twist_sin = jnp.sin(twist)
-    turned_re = section_re * twist_cos + section_im * twist_sin
-    turned_im = section_im * twist_cos - section_re * twist_sin
+    turned = jnp.concatenate(
+        [section_re * twist_cos + section_im * twist_sin, section_im * twist_cos - section_re * twist_sin],
+        axis=1,
+    )
     freq_two = jnp.arange(PH, dtype=jnp.int32)
     theta_two = angle_table(second_index[:, None], freq_two[None, :], PB)
     cos_two = jnp.cos(theta_two)
     sin_two = jnp.sin(theta_two)
-    spec_re = jnp.einsum("rbk,bm->rkm", turned_re, cos_two, precision=highest) + jnp.einsum(
-        "rbk,bm->rkm", turned_im, sin_two, precision=highest
-    )
-    spec_im = jnp.einsum("rbk,bm->rkm", turned_im, cos_two, precision=highest) - jnp.einsum(
-        "rbk,bm->rkm", turned_re, sin_two, precision=highest
-    )
+    stage_two = jnp.concatenate(
+        [jnp.concatenate([cos_two, -sin_two], axis=1), jnp.concatenate([sin_two, cos_two], axis=1)], axis=0
+    )
+    spec = jnp.einsum("rbk,bm->rkm", turned, stage_two, precision=highest)
     scale = (2.0 / L) ** 0.5
-    stacked = jnp.stack([spec_re, spec_im]) * scale
+    stacked = spec.reshape(rows, PA, 2, PH).transpose(2, 0, 1, 3) * scale
     span = PA // bands
     stacked = stacked.reshape(2, rows, span, bands, PH).transpose(3, 1, 0, 4, 2)
     return stacked.reshape(bands, rows, 2, PH * span)
 
 
-def inverse_rows(spectra, band_ids, bands):
-    count = spectra.shape[0]
+def inverse_rows(spectra, bands):
     rows = spectra.shape[1]
     span = PA // bands
-    parts = spectra.reshape(count, rows, 2, PH, span)
-    part_re = parts[:, :, 0]
-    part_im = parts[:, :, 1]
+    parts = spectra.reshape(bands, rows, 2 * PH, span)
     freq_two = jnp.arange(PH, dtype=jnp.int32)
     second_index = jnp.arange(PB, dtype=jnp.int32)
     theta_two = angle_table(freq_two[:, None], second_index[None, :], PB)
     cos_two = jnp.cos(theta_two)
     sin_two = jnp.sin(theta_two)
-    middle_re = jnp.einsum("brms,mn->brsn", part_re, cos_two, precision=highest) - jnp.einsum(
-        "brms,mn->brsn", part_im, sin_two, precision=highest
-    )
-    middle_im = jnp.einsum("brms,mn->brsn", part_im, cos_two, precision=highest) + jnp.einsum(
-        "brms,mn->brsn", part_re, sin_two, precision=highest
-    )
+    stage_two = jnp.concatenate(
+        [jnp.concatenate([cos_two, sin_two], axis=1), jnp.concatenate([-sin_two, cos_two], axis=1)], axis=0
+    )
+    middle = jnp.einsum("brms,mn->brsn", parts, stage_two, precision=highest)
+    middle_re = middle[..., :PB]
+    middle_im = middle[..., PB:]
+    band_ids = jnp.arange(bands, dtype=jnp.int32)
     freq_one = jnp.arange(span, dtype=jnp.int32)[None, :] * bands + band_ids[:, None]
     twist = angle_table(freq_one[:, :, None], second_index[None, None, :], L)
     twist_cos = jnp.cos(twist)[:, None]
     twist_sin = jnp.sin(twist)[:, None]
-    turned_re = middle_re * twist_cos - middle_im * twist_sin
-    turned_im = middle_re * twist_sin + middle_im * twist_cos
+    turned = jnp.stack(
+        [middle_re * twist_cos - middle_im * twist_sin, middle_re * twist_sin + middle_im * twist_cos]
+    )
     first_index = jnp.arange(PA, dtype=jnp.int32)
     theta_one = angle_table(freq_one[:, :, None], first_index[None, None, :], PA)
-    grid = jnp.einsum(
-        "brsn,bsa->ran", turned_re, jnp.cos(theta_one), precision=highest
-    ) - jnp.einsum("brsn,bsa->ran", turned_im, jnp.sin(theta_one), precision=highest)
+    stage_one = jnp.stack([jnp.cos(theta_one), -jnp.sin(theta_one)])
+    grid = jnp.einsum("pbrsn,pbsa->ran", turned, stage_one, precision=highest)
     return grid * (2.0 / L) ** 0.5
 
 
@@ -152,7 +150,7 @@
     ).astype(jnp.float32)
 
     whole_rows = lax.all_to_all(gravity, "freq", split_axis=0, concat_axis=1, tiled=True)
-    terms = forward_bands(whole_rows.reshape(mine, PA, PB), 0, bands)
+    terms = forward_bands(whole_rows.reshape(mine, PA, PB), bands)
     own = jnp.einsum("brct,bts->brcs", terms[..., :held], selector, precision=highest)
     own = own.reshape(bands, mine, 2, blocks, per_slot)
     rest = jnp.pad(terms[..., held:], ((0, 0), (0, 0), (0, 0), (0, padded - band_width)))
@@ -187,7 +185,7 @@
     slots_back = jnp.einsum("brcs,bts->brct", slots_back, selector, precision=highest)
     rest_back = by_source[..., per_slot:].reshape(bands, mine, 2, blocks * share)
     by_band = jnp.concatenate([slots_back, rest_back], axis=3)[..., :band_width]
-    grid_rows = inverse_rows(by_band, jnp.arange(bands, dtype=jnp.int32), bands)
+    grid_rows = inverse_rows(by_band, bands)
     geoid = lax.all_to_all(grid_rows.reshape(mine, L), "freq", split_axis=1, concat_axis=0, tiled=True)
     return geoid
 

time: 97.1 us -> 101 us (1.040)
  other arithmetic: 3.8 us -> 11.7 us
  matrix products: 22.5 us -> 17.5 us
  starting transfers between devices: 24.5 us -> 26.9 us
  waiting for transfers between devices: 13.4 us -> 11.2 us
    dot_general x12 -> x4, matrix products: 10.7 us -> 5.57 us  [the longest x1 2.31 us: inverse_rows(): middle = jnp.einsum('brms,mn->brsn', parts, stage_two, precision=highest)]
    neg x0 -> x3, other arithmetic: none -> 2.58 us  [the longest x1 1.28 us: forward_bands(): -jnp.sin(theta_one)]
    all_to_all x1, waiting for transfers between devices: 2.4 us -> 0.01 us  [per_device(): lax.all_to_all(gravity, 'freq', split_axis=0, concat_axis=1, tiled=True)]
    all_to_all x1, starting transfers between devices: 8.28 us -> 10.7 us  [per_device(): lax.all_to_all(payload, everyone, split_axis=0, concat_axis=0, tiled=True)]
    cos x0 -> x1, other arithmetic: none -> 1.64 us  [inverse_rows(): stage_one = jnp.stack([jnp.cos(theta_one), -jnp.sin(theta_one)])]
    sin x0 -> x2, other arithmetic: none -> 1.36 us  [the longest x1 1.01 us: forward_bands(): sin_two = jnp.sin(theta_two)]
    unnamed x9 -> x19, local copies, waits for them, and re-layouts: 2.36 us -> 1.62 us
  transfers between devices with their start and end apart: 3 -> 3, of which waited for: 3 -> 2; matrix products, arithmetic and copies ran while one was open for 16% -> 22% of each run, Pallas kernels for 0% -> 0%
where the time goes in v8:
time: 101 us; the launch traced here: 100 us
  starting transfers between devices  26.9 us (27%)
  matrix products  17.5 us (17%)
  local copies, waits for them, and re-layouts  14.4 us (14%)
  other arithmetic  11.7 us (12%)
  blocking collectives  11.3 us (11%)
  waiting for transfers between devices  11.2 us (11%)
  Pallas kernels  6.84 us (7%)
    all_to_all x1, blocking collectives, per_device(): lax.all_to_all(grid_rows.reshape(mine, L), 'freq', split_axis=1, concat_a...  11.3 us
    all_to_all x1, starting transfers between devices, per_device(): lax.all_to_all(payload, everyone, split_axis=0, concat_axis=0, tiled=True)  10.7 us
    all_to_all x1, waiting for transfers between devices, per_device(): lax.all_to_all(stokes, everyone, split_axis=0, concat_axis=0, tiled=True)  9.91 us
    dot_general x1, matrix products, per_device(): jnp.einsum('ocn,onq->ocq', coef, legendre, preferred_element_type=jnp.flo...  8.94 us
    all_to_all x1, starting transfers between devices, per_device(): lax.all_to_all(stokes, everyone, split_axis=0, concat_axis=0, tiled=True)  8.3 us
    all_to_all x1, starting transfers between devices, per_device(): lax.all_to_all(gravity, 'freq', split_axis=0, concat_axis=1, tiled=True)  7.89 us
    pallas_call x1, Pallas kernels, toeplitz_stokes(): pl.pallas_call(stokes_body, out_shape=jax.ShapeDtypeStruct((2, total, LAN...  6.84 us
    all_to_all x2, local copies, waits for them, and re-layouts, per_device(): lax.all_to_all(gravity, 'freq', split_axis=0, concat_axis=1, tiled=True)  2.75 us
  transfers between devices with their start and end apart: 3, of which 2 were waited for; matrix products, arithmetic and copies ran while one was open for 22% of the time, Pallas kernels for 0%

profile of v8, /device:TPU:0, one launch (start us, length us, event | category | flops | bytes accessed | tf_op | source)
XLA Modules:
  0.0 100.2 jit_solution(6775240789866022275)
XLA Ops:
  0.0 1.8 %all_to_all.32 = f32[8,2,2700]{2,1,0:T(2,128)} reshape(f32[16,2700]{1,0:T(8,128)} %param.6) | data formatting | bytes 345600 | tf_op jit(solution)/shard_map/all_to_all | solution.py:152
  1.8 7.9 %all-to-all-start = ((f32[8,2,2700]{2,1,0:T(2,128)}), f32[8,2,2700]{2,1,0:T(2,128)}, u32[]{:S(2)}, u32[]{:S(2)}) async-start(f32[8,2,2700]{2,1,0:T(2,128)} %all_to_all.32), calls=%async_computation | async-start | bytes 360448 | tf_op jit(solution)/shard_map/all_to_all | solution.py:152
  9.7 1.3 %sine_negate_fusion.1 = (f32[144,144]{1,0:T(8,128)S(1)}, f32[144,144]{1,0:T(8,128)}) fusion(), kind=kLoop, calls=%fused_computation.82 | loop fusion | flops 207360 | bytes 165888 | tf_op jit(solution)/shard_map/neg | solution.py:27
  11.0 1.0 %fusion.69 = (f32[150,75]{0,1:T(8,128)}, f32[150,75]{0,1:T(8,128)}) fusion(), kind=kLoop, calls=%fused_computation.108 | loop fusion | flops 101250 | bytes 90000 | tf_op jit(solution)/shard_map/sin | solution.py:42
  12.0 1.0 fusion.74
  13.0 0.9 reshape.228
  13.9 0.1 reshape.229
  14.1 0.6 compare_and_fusion
  14.7 0.9 fusion.39
  15.6 1.6 %fusion.42 = (f32[1,8,18,144]{3,2,0,1:T(8,128)}, f32[1,8,18,144]{3,2,0,1:T(8,128)}) fusion(s32[8,18]{1,0:T(8,128)S(1)} %iota_add_fusion), kind=kLoop, calls=%fused_computation.68 | loop fusion | flops 207360 | bytes 166464 | tf_op jit(solution)/shard_map/cos | solution.py:79
  17.3 0.6 pad_clamp_fusion
  17.9 0.8 copy.63
  18.7 0.7 gather_fusion
  19.4 0.1 copy.62
  19.5 0.7 select_bitcast_fusion
  20.2 0.2 pad_dynamic-slice_fusion
  20.4 0.1 pad_maximum_fusion.2
  20.5 0.4 rev.3
  20.9 0.7 pad_convert_fusion.k_ref
  21.6 0.1 multiply_cosine_fusion
  21.7 0.6 fusion.49
  22.4 0.9 copy.64
  23.4 0.1 reshape.230
  23.5 1.0 convolution_bitcast_fusion
  24.5 0.2 multiply_add_fusion
  24.7 1.4 %convolution_multiply_fusion = f32[2,144,150]{2,1,0:T(8,128)S(1)} fusion(f32[2,150,144]{2,1,0:T(8,128)S(1)} %get-tuple-element.14, f32[2,150,144]{2,1,0:T(8,128)S(1)} %get-tuple-element.13, f32[150,75]{0,1:T(8,128)S(1)} %copy-done.4, f32[150,75]{0,1:T(8,128)S(1)} %copy-done.3, f32[150,75]{0,1:T(8,128)S(1)} %copy-done.5), kind=kOutput, calls=%fused_computation.11 | convolution fusion | flops 155784608 | bytes 653400 | tf_op jit(solution)/shard_map/rbk,bm->rkm/dot_general | solution.py:46
  26.1 0.2 mul.432
  26.4 0.5 copy.67
  26.9 0.5 reshape.232
  27.4 0.1 slice.53
  27.5 1.2 %fusion.3 = f32[8,2,2,272]{3,2,1,0:T(2,128)S(1)} fusion(s32[8,272]{1,0:T(8,128)S(1)} %add_select_fusion.6, f32[8,2,2,272]{3,0,2,1:T(8,128)S(1)} %slice.52), kind=kOutput, calls=%fused_computation.4 | convolution fusion | flops 29001728 | bytes 78336 | tf_op jit(solution)/shard_map/brct,bts->brcs/dot_general | solution.py:154
  28.7 0.2 reshape.233
  29.0 0.2 reshape.234
  29.3 0.2 maximum_bitcast_fusion.2
  29.5 0.9 copy.70
  30.4 10.7 %all-to-all-start.1 = ((f32[128,2,2,86]{3,1,2,0:T(2,128)}), f32[128,2,2,86]{3,1,2,0:T(2,128)S(1)}, u32[]{:S(2)}, u32[]{:S(2)}) async-start(f32[128,2,2,86]{3,1,2,0:T(2,128)} %bitcast.17), calls=%async_computation.1 | async-start | bytes 524288 | tf_op jit(solution)/shard_map/all_to_all | solution.py:164
  41.1 8.9 %convolution_convert_fusion = bf16[17,2,256]{2,1,0:T(2,128)(2,1)S(1)} fusion(bf16[17,2,2176]{2,1,0:T(2,128)(2,1)S(1)} %copy-done, bf16[17,2176,256]{2,1,0:T(8,128)(2,1)} %param.8), kind=kOutput, calls=%fused_computation.13 | convolution fusion | flops 37888512 | bytes 19105280 | tf_op jit(solution)/shard_map/ocn,onq->ocq/dot_general | solution.py:169
  50.0 0.2 copy.72
  50.2 1.3 %all-to-all-done.1 = f32[128,2,2,86]{3,1,2,0:T(2,128)S(1)} async-done(((f32[128,2,2,86]{3,1,2,0:T(2,128)}), f32[128,2,2,86]{3,1,2,0:T(2,128)S(1)}, u32[]{:S(2)}, u32[]{:S(2)}) %all-to-all-start.1) | async-done | bytes 176160 | tf_op jit(solution)/shard_map/all_to_all | solution.py:164
  51.6 0.2 slice_reduce_fusion
  51.7 0.1 fusion.58
  51.9 0.7 pad_convert_fusion.1.w_ref
  52.6 6.8 %shard_map.64 = f32[2,256,128]{2,1,0:T(8,128)} custom-call(f32[520,128]{1,0:T(8,128)} %pad_convert_fusion.k_ref, f32[2,256,128]{2,1,0:T(8,128)} %pad_convert_fusion.1.w_ref), custom_call_target="tpu_custom_call" | custom-call | tf_op jit(solution)/shard_map/pallas_call | solution.py:123
  59.4 1.8 %copy.96 = f32[2,128,2,85]{3,2,0,1:T(2,128)} copy(f32[2,128,2,85]{3,2,1,0:T(2,128)} %bitcast.93) | data formatting | bytes 348160 | tf_op jit(solution)/shard_map/reshape | solution.py:181
  61.2 8.3 %all-to-all-start.2 = ((f32[128,2,2,85]{3,1,2,0:T(2,128)}), f32[128,2,2,85]{3,1,2,0:T(2,128)S(1)}, u32[]{:S(2)}, u32[]{:S(2)}) async-start(f32[128,2,2,85]{3,1,2,0:T(2,128)} %bitcast.85), calls=%async_computation.2 | async-start | bytes 524288 | tf_op jit(solution)/shard_map/all_to_all | solution.py:182
  69.5 0.3 fusion.75
  69.8 0.3 fusion.65
  70.2 9.9 %all-to-all-done.2 = f32[128,2,2,85]{3,1,2,0:T(2,128)S(1)} async-done(((f32[128,2,2,85]{3,1,2,0:T(2,128)}), f32[128,2,2,85]{3,1,2,0:T(2,128)S(1)}, u32[]{:S(2)}, u32[]{:S(2)}) %all-to-all-start.2) | async-done | bytes 174112 | tf_op jit(solution)/shard_map/all_to_all | solution.py:182
  80.1 0.2 copy.95
  80.3 0.1 slice.58
  80.4 0.3 reshape.240
  80.7 0.2 reshape.239
  80.8 1.7 %fusion.1 = f32[8,2,2,272]{3,2,1,0:T(2,128)S(1)} fusion(f32[8,2,2,272]{3,2,1,0:T(2,128)S(1)} %reshape.239, s32[8,272]{1,0:T(8,128)S(1)} %add_select_fusion.6), kind=kOutput, calls=%fused_computation.3 | convolution fusion | flops 29001728 | bytes 78336 | tf_op jit(solution)/shard_map/brcs,bts->brct/dot_general | solution.py:185
  82.6 0.2 pad_maximum_fusion.1
  82.8 0.8 reshape.241
  83.6 2.3 %fusion.23 = f32[8,2,18,300]{3,2,1,0:T(8,128)S(1)} fusion(f32[8,2,150,18]{3,2,1,0:T(8,128)S(1)} %reshape.241, f32[75,150]{1,0:T(8,128)S(1)} %get-tuple-element.26, f32[75,150]{1,0:T(8,128)S(1)} %fusion.75, f32[75,150]{1,0:T(8,128)S(1)} %get-tuple-element.25), kind=kOutput, calls=%fused_computation.43 | convolution fusion | flops 155655008 | bytes 653400 | tf_op jit(solution)/shard_map/brms,mn->brsn/dot_general | solution.py:66
  86.0 0.2 subtract_bitcast_fusion
  86.2 0.7 copy-done.6
  86.9 0.1 copy-done.7
  87.0 0.9 fusion.8
  87.9 0.1 all_to_all.37
  88.0 0.1 copy.77
  88.1 11.3 %all_to_all.45 = f32[2,8,2700]{2,0,1:T(2,128)S(1)} all-to-all(f32[2,8,2700]{2,0,1:T(2,128)S(1)} %copy.77), channel_id=1, replica_groups=mesh['lat'=16,'freq'=8] {'freq'}, dimensions={1} | all-to-all | bytes 345600 | tf_op jit(solution)/shard_map/all_to_all | solution.py:189
  99.4 0.8 all_to_all.40
  (27 shorter events, 0.4 us)
Async XLA Ops:
  0.0 41.0 %copy-start = (bf16[17,2,2176]{2,1,0:T(2,128)(2,1)S(1)}, bf16[17,2,2176]{2,1,0:T(2,128)(2,1)}, u32[]{:S(2)}) copy-start(bf16[17,2,2176]{2,1,0:T(2,128)(2,1)} %param.7) | copy-start | bytes 443908
  0.0 17.9 %copy-start.1 = (bf16[511,1350]{0,1:T(8,128)(2,1)S(1)}, bf16[511,1350]{0,1:T(8,128)(2,1)}, u32[]{:S(2)}) copy-start(bf16[511,1350]{0,1:T(8,128)(2,1)} %param.11) | copy-start | bytes 4139104
  1.8 20.6 %all-to-all-start = ((f32[8,2,2700]{2,1,0:T(2,128)}), f32[8,2,2700]{2,1,0:T(2,128)}, u32[]{:S(2)}, u32[]{:S(2)}) async-start(f32[8,2,2700]{2,1,0:T(2,128)} %all_to_all.32), calls=%async_computation | async-start | bytes 360448 | tf_op jit(solution)/shard_map/all_to_all | solution.py:152
  19.5 2.1 %copy-start.8 = (s32[16]{0:T(128)S(1)}, s32[16]{0:T(128)}, u32[]{:S(2)}) copy-start(s32[16]{0:T(128)} %param.10) | copy-start | bytes 196
  20.4 3.2 %copy-start.2 = (f32[144,144]{1,0:T(8,128)S(1)}, f32[144,144]{1,0:T(8,128)}, u32[]{:S(2)}) copy-start(f32[144,144]{1,0:T(8,128)} %get-tuple-element.20) | copy-start | bytes 248836
  23.3 1.4 %copy-start.3 = (f32[150,75]{0,1:T(8,128)S(1)}, f32[150,75]{0,1:T(8,128)}, u32[]{:S(2)}) copy-start(f32[150,75]{0,1:T(8,128)} %get-tuple-element.23) | copy-start | bytes 135004
  23.3 1.4 %copy-start.4 = (f32[150,75]{0,1:T(8,128)S(1)}, f32[150,75]{0,1:T(8,128)}, u32[]{:S(2)}) copy-start(f32[150,75]{0,1:T(8,128)} %get-tuple-element.24) | copy-start | bytes 135004
  23.4 1.4 %copy-start.5 = (f32[150,75]{0,1:T(8,128)S(1)}, f32[150,75]{0,1:T(8,128)}, u32[]{:S(2)}) copy-start(f32[150,75]{0,1:T(8,128)} %fusion.74) | copy-start | bytes 135004
  30.4 21.1 %all-to-all-start.1 = ((f32[128,2,2,86]{3,1,2,0:T(2,128)}), f32[128,2,2,86]{3,1,2,0:T(2,128)S(1)}, u32[]{:S(2)}, u32[]{:S(2)}) async-start(f32[128,2,2,86]{3,1,2,0:T(2,128)} %bitcast.17), calls=%async_computation.1 | async-start | bytes 524288 | tf_op jit(solution)/shard_map/all_to_all | solution.py:164
  61.2 18.9 %all-to-all-start.2 = ((f32[128,2,2,85]{3,1,2,0:T(2,128)}), f32[128,2,2,85]{3,1,2,0:T(2,128)S(1)}, u32[]{:S(2)}, u32[]{:S(2)}) async-start(f32[128,2,2,85]{3,1,2,0:T(2,128)} %bitcast.85), calls=%async_computation.2 | async-start | bytes 524288 | tf_op jit(solution)/shard_map/all_to_all | solution.py:182
  85.9 0.9 copy-start.6
  85.9 1.0 %copy-start.7 = (f32[1,8,18,144]{3,2,0,1:T(8,128)S(1)}, f32[1,8,18,144]{3,2,0,1:T(8,128)}, u32[]{:S(2)}) copy-start(f32[1,8,18,144]{3,2,0,1:T(8,128)} %get-tuple-element.16) | copy-start | bytes 248836

commit v9 on v8

--- a/solution.py
+++ b/solution.py
@@ -16,32 +16,36 @@
 
 
 def angle_table(first, second, period):
-    phase = first * second % period
-    return phase.astype(jnp.float32) * (2.0 * np.pi / period)
+    phase = (first * second) % period
+    return phase.astype(np.float64) * (2.0 * np.pi / period)
+
+
+def constant(values):
+    return jnp.asarray(np.asarray(values, dtype=np.float32))
 
 
 def forward_bands(grid, bands):
     rows = grid.shape[0]
-    first_index = jnp.arange(PA, dtype=jnp.int32)
+    first_index = np.arange(PA)
     theta_one = angle_table(first_index[:, None], first_index[None, :], PA)
-    stage_one = jnp.concatenate([jnp.cos(theta_one), -jnp.sin(theta_one)], axis=1)
+    stage_one = constant(np.concatenate([np.cos(theta_one), -np.sin(theta_one)], axis=1))
     section = jnp.einsum("rab,ak->rbk", grid, stage_one, precision=highest)
     section_re = section[..., :PA]
     section_im = section[..., PA:]
-    second_index = jnp.arange(PB, dtype=jnp.int32)
+    second_index = np.arange(PB)
     twist = angle_table(second_index[:, None], first_index[None, :], L)
-    twist_cos = jnp.cos(twist)
-    twist_sin = jnp.sin(twist)
+    twist_cos = constant(np.cos(twist))
+    twist_sin = constant(np.sin(twist))
     turned = jnp.concatenate(
         [section_re * twist_cos + section_im * twist_sin, section_im * twist_cos - section_re * twist_sin],
         axis=1,
     )
-    freq_two = jnp.arange(PH, dtype=jnp.int32)
+    freq_two = np.arange(PH)
     theta_two = angle_table(second_index[:, None], freq_two[None, :], PB)
-    cos_two = jnp.cos(theta_two)
-    sin_two = jnp.sin(theta_two)
-    stage_two = jnp.concatenate(
-        [jnp.concatenate([cos_two, -sin_two], axis=1), jnp.concatenate([sin_two, cos_two], axis=1)], axis=0
+    cos_two = np.cos(theta_two)
+    sin_two = np.sin(theta_two)
+    stage_two = constant(
+        np.concatenate([np.concatenate([cos_two, -sin_two], axis=1), np.concatenate([sin_two, cos_two], axis=1)])
     )
     spec = jnp.einsum("rbk,bm->rkm", turned, stage_two, precision=highest)
     scale = (2.0 / L) ** 0.5
@@ -55,28 +59,28 @@
     rows = spectra.shape[1]
     span = PA // bands
     parts = spectra.reshape(bands, rows, 2 * PH, span)
-    freq_two = jnp.arange(PH, dtype=jnp.int32)
-    second_index = jnp.arange(PB, dtype=jnp.int32)
+    freq_two = np.arange(PH)
+    second_index = np.arange(PB)
     theta_two = angle_table(freq_two[:, None], second_index[None, :], PB)
-    cos_two = jnp.cos(theta_two)
-    sin_two = jnp.sin(theta_two)
-    stage_two = jnp.concatenate(
-        [jnp.concatenate([cos_two, sin_two], axis=1), jnp.concatenate([-sin_two, cos_two], axis=1)], axis=0
+    cos_two = np.cos(theta_two)
+    sin_two = np.sin(theta_two)
+    stage_two = constant(
+        np.concatenate([np.concatenate([cos_two, sin_two], axis=1), np.concatenate([-sin_two, cos_two], axis=1)])
     )
     middle = jnp.einsum("brms,mn->brsn", parts, stage_two, precision=highest)
     middle_re = middle[..., :PB]
     middle_im = middle[..., PB:]
-    band_ids = jnp.arange(bands, dtype=jnp.int32)
-    freq_one = jnp.arange(span, dtype=jnp.int32)[None, :] * bands + band_ids[:, None]
+    band_ids = np.arange(bands)
+    freq_one = np.arange(span)[None, :] * bands + band_ids[:, None]
     twist = angle_table(freq_one[:, :, None], second_index[None, None, :], L)
-    twist_cos = jnp.cos(twist)[:, None]
-    twist_sin = jnp.sin(twist)[:, None]
+    twist_cos = constant(np.cos(twist))[:, None]
+    twist_sin = constant(np.sin(twist))[:, None]
     turned = jnp.stack(
         [middle_re * twist_cos - middle_im * twist_sin, middle_re * twist_sin + middle_im * twist_cos]
     )
-    first_index = jnp.arange(PA, dtype=jnp.int32)
+    first_index = np.arange(PA)
     theta_one = angle_table(freq_one[:, :, None], first_index[None, None, :], PA)
-    stage_one = jnp.stack([jnp.cos(theta_one), -jnp.sin(theta_one)])
+    stage_one = constant(np.stack([np.cos(theta_one), -np.sin(theta_one)]))
     grid = jnp.einsum("pbrsn,pbsa->ran", turned, stage_one, precision=highest)
     return grid * (2.0 / L) ** 0.5
 

time: 101 us -> 91.8 us (0.909)
  blocking collectives: 11.3 us -> 30 us
  starting transfers between devices: 26.9 us -> 15.7 us
  other arithmetic: 11.7 us -> 2.85 us
  waiting for transfers between devices: 11.2 us -> 4.17 us
    all_to_all x0 -> x1, blocking collectives: none -> 18.7 us  [per_device(): lax.all_to_all(stokes, everyone, split_axis=0, concat_axis=0, tiled=True)]
    all_to_all x1 -> x0, waiting for transfers between devices: 9.91 us -> none  [per_device(): lax.all_to_all(stokes, everyone, split_axis=0, concat_axis=0, tiled=True)]
    all_to_all x1 -> x0, starting transfers between devices: 8.3 us -> none  [per_device(): lax.all_to_all(stokes, everyone, split_axis=0, concat_axis=0, tiled=True)]
    all_to_all x1, starting transfers between devices: 10.7 us -> 7.8 us  [per_device(): lax.all_to_all(payload, everyone, split_axis=0, concat_axis=0, tiled=True)]
    all_to_all x1, waiting for transfers between devices: 0.01 us -> 2.69 us  [per_device(): lax.all_to_all(gravity, 'freq', split_axis=0, concat_axis=1, tiled=True)]
    neg x3 -> x0, other arithmetic: 2.58 us -> none  [the longest x1 1.28 us: forward_bands(): -jnp.sin(theta_one)]
    cos x2 -> x0, other arithmetic: 2.52 us -> none  [the longest x1 1.64 us: inverse_rows(): stage_one = jnp.stack([jnp.cos(theta_one), -jnp.sin(theta_one)])]
    sin x3 -> x0, other arithmetic: 2 us -> none  [the longest x1 1.01 us: forward_bands(): sin_two = jnp.sin(theta_two)]
  transfers between devices with their start and end apart: 3 -> 2, of which waited for: 2 -> 2; matrix products, arithmetic and copies ran while one was open for 22% -> 16% of each run, Pallas kernels for 0% -> 0%
where the time goes in v9:
time: 91.8 us; the launch traced here: 91.3 us
  blocking collectives  30 us (33%)
  matrix products  17.4 us (19%)
  starting transfers between devices  15.7 us (17%)
  local copies, waits for them, and re-layouts  13.9 us (15%)
  Pallas kernels  6.86 us (7%)
  waiting for transfers between devices  4.17 us (5%)
  other arithmetic  2.85 us (3%)
    all_to_all x1, blocking collectives, per_device(): lax.all_to_all(stokes, everyone, split_axis=0, concat_axis=0, tiled=True)  18.7 us
    all_to_all x1, blocking collectives, per_device(): lax.all_to_all(grid_rows.reshape(mine, L), 'freq', split_axis=1, concat_a...  11.3 us
    dot_general x1, matrix products, per_device(): jnp.einsum('ocn,onq->ocq', coef, legendre, preferred_element_type=jnp.flo...  8.94 us
    all_to_all x1, starting transfers between devices, per_device(): lax.all_to_all(gravity, 'freq', split_axis=0, concat_axis=1, tiled=True)  7.89 us
    all_to_all x1, starting transfers between devices, per_device(): lax.all_to_all(payload, everyone, split_axis=0, concat_axis=0, tiled=True)  7.8 us
    pallas_call x1, Pallas kernels, toeplitz_stokes(): pl.pallas_call(stokes_body, out_shape=jax.ShapeDtypeStruct((2, total, LAN...  6.86 us
    unnamed x23, local copies, waits for them, and re-layouts  2.9 us
    all_to_all x1, waiting for transfers between devices, per_device(): lax.all_to_all(gravity, 'freq', split_axis=0, concat_axis=1, tiled=True)  2.69 us
  transfers between devices with their start and end apart: 2, of which 2 were waited for; matrix products, arithmetic and copies ran while one was open for 16% of the time, Pallas kernels for 0%

profile of v9, /device:TPU:0, one launch (start us, length us, event | category | flops | bytes accessed | tf_op | source)
XLA Modules:
  0.0 91.3 jit_solution(12111464295036128841)
XLA Ops:
  0.0 1.7 %all_to_all.32 = f32[8,2,2700]{2,1,0:T(2,128)} reshape(f32[16,2700]{1,0:T(8,128)} %param.14) | data formatting | bytes 345600 | tf_op jit(solution)/shard_map/all_to_all | solution.py:156
  1.7 7.9 %all-to-all-start = ((f32[8,2,2700]{2,1,0:T(2,128)}), f32[8,2,2700]{2,1,0:T(2,128)S(1)}, u32[]{:S(2)}, u32[]{:S(2)}) async-start(f32[8,2,2700]{2,1,0:T(2,128)} %all_to_all.32), calls=%async_computation | async-start | bytes 360448 | tf_op jit(solution)/shard_map/all_to_all | solution.py:156
  9.6 0.9 reshape.124
  10.6 0.1 reshape.125
  10.6 0.0 copy-start.1
  10.7 0.1 fusion.19
  10.8 0.1 compare_and_fusion
  10.9 1.9 %copy.71 = bf16[511,1350]{1,0:T(8,128)(2,1)S(1)} copy(bf16[511,1350]{0,1:T(8,128)(2,1)} %param.19) | data formatting | bytes 2759400 | tf_op args[5]
  12.8 0.6 gather_fusion
  13.4 0.0 copy-start.10
  13.4 0.1 copy.70
  13.6 0.0 copy-start.5
  13.6 0.2 pad_dynamic-slice_fusion
  13.8 0.0 copy-start.9
  13.8 0.1 pad_maximum_fusion.2
  13.9 0.2 copy-done.10
  14.1 0.1 multiply_cosine_fusion
  14.2 0.4 rev.3
  14.6 0.7 pad_convert_fusion.k_ref
  15.3 2.7 %all-to-all-done = f32[8,2,2700]{2,1,0:T(2,128)S(1)} async-done(((f32[8,2,2700]{2,1,0:T(2,128)}), f32[8,2,2700]{2,1,0:T(2,128)S(1)}, u32[]{:S(2)}, u32[]{:S(2)}) %all-to-all-start) | async-done | bytes 172832 | tf_op jit(solution)/shard_map/all_to_all | solution.py:156
  18.0 0.0 copy-start.4
  18.0 0.1 reshape.126
  18.2 1.0 %convolution_bitcast_fusion = f32[2,150,288]{2,1,0:T(8,128)S(1)} fusion(f32[144,288,1]{1,0,2:T(8,128)S(1)} %copy-done.5, f32[2,144,150]{2,1,0:T(8,128)S(1)} %reshape.126), kind=kOutput, calls=%fused_computation.8 | convolution fusion | flops 149299200 | bytes 684288 | tf_op jit(solution)/shard_map/rab,ak->rbk/dot_general | solution.py:32
  19.2 0.2 multiply_add_fusion
  19.4 1.3 %convolution_multiply_fusion = f32[2,144,150]{2,1,0:T(8,128)S(1)} fusion(f32[300,150,1]{0,1,2:T(8,128)S(1)} %copy-done.4, f32[2,150,144]{2,1,0:T(8,128)S(1)} %get-tuple-element.14, f32[2,150,144]{2,1,0:T(8,128)S(1)} %get-tuple-element.13), kind=kOutput, calls=%fused_computation.11 | convolution fusion | flops 155649600 | bytes 698400 | tf_op jit(solution)/shard_map/rbk,bm->rkm/dot_general | solution.py:50
  20.7 0.2 mul.109
  21.0 0.5 copy.75
  21.5 0.5 reshape.128
  22.0 0.1 slice.53
  22.1 1.2 %fusion.3 = f32[8,2,2,272]{3,2,1,0:T(2,128)S(1)} fusion(s32[8,272]{1,0:T(8,128)S(1)} %add_select_fusion, f32[8,2,2,272]{3,0,2,1:T(8,128)S(1)} %slice.52), kind=kOutput, calls=%fused_computation.4 | convolution fusion | flops 29001728 | bytes 78336 | tf_op jit(solution)/shard_map/brct,bts->brcs/dot_general | solution.py:158
  23.3 0.2 reshape.129
  23.5 0.2 reshape.130
  23.7 0.1 broadcast_in_dim.11
  23.8 0.2 maximum_bitcast_fusion
  24.0 0.9 copy.78
  24.9 7.8 %all-to-all-start.1 = ((f32[128,2,2,86]{3,1,2,0:T(2,128)}), f32[128,2,2,86]{3,1,2,0:T(2,128)S(1)}, u32[]{:S(2)}, u32[]{:S(2)}) async-start(f32[128,2,2,86]{3,1,2,0:T(2,128)} %bitcast.15), calls=%async_computation.1 | async-start | bytes 524288 | tf_op jit(solution)/shard_map/all_to_all | solution.py:168
  32.8 8.9 %convolution_convert_fusion = bf16[17,2,256]{2,1,0:T(2,128)(2,1)S(1)} fusion(bf16[17,2,2176]{2,1,0:T(2,128)(2,1)S(1)} %copy-done, bf16[17,2176,256]{2,1,0:T(8,128)(2,1)} %param.16), kind=kOutput, calls=%fused_computation.13 | convolution fusion | flops 37888512 | bytes 19105280 | tf_op jit(solution)/shard_map/ocn,onq->ocq/dot_general | solution.py:173
  41.7 0.2 copy.80
  41.9 1.5 %all-to-all-done.1 = f32[128,2,2,86]{3,1,2,0:T(2,128)S(1)} async-done(((f32[128,2,2,86]{3,1,2,0:T(2,128)}), f32[128,2,2,86]{3,1,2,0:T(2,128)S(1)}, u32[]{:S(2)}, u32[]{:S(2)}) %all-to-all-start.1) | async-done | bytes 176160 | tf_op jit(solution)/shard_map/all_to_all | solution.py:168
  43.4 0.1 copy.79
  43.4 0.2 slice_reduce_fusion
  43.6 0.1 fusion.15
  43.8 0.7 pad_convert_fusion.1.w_ref
  44.5 6.9 %shard_map.136 = f32[2,256,128]{2,1,0:T(8,128)} custom-call(f32[520,128]{1,0:T(8,128)} %pad_convert_fusion.k_ref, f32[2,256,128]{2,1,0:T(8,128)} %pad_convert_fusion.1.w_ref), custom_call_target="tpu_custom_call" | custom-call | tf_op jit(solution)/shard_map/pallas_call | solution.py:127
  51.3 1.0 %copy.104 = f32[2,128,2,85]{3,2,0,1:T(2,128)S(1)} copy(f32[2,128,2,85]{3,2,1,0:T(2,128)} %bitcast.89) | data formatting | bytes 348160 | tf_op jit(solution)/shard_map/reshape | solution.py:185
  52.4 18.7 %all_to_all.45 = f32[128,2,2,85]{3,1,2,0:T(2,128)S(1)} all-to-all(f32[128,2,2,85]{3,1,2,0:T(2,128)S(1)} %bitcast.90), channel_id=1, replica_groups=mesh['lat'=16,'freq'=8] {'lat','freq'}, dimensions={0} | all-to-all | bytes 348160 | tf_op jit(solution)/shard_map/all_to_all | solution.py:186
  71.1 0.2 copy.103
  71.2 0.1 slice.58
  71.4 0.3 reshape.136
  71.6 0.0 copy-start.3
  71.7 0.2 reshape.135
  71.8 1.7 %fusion.1 = f32[8,2,2,272]{3,2,1,0:T(2,128)S(1)} fusion(f32[8,2,2,272]{3,2,1,0:T(2,128)S(1)} %reshape.135, s32[8,272]{1,0:T(8,128)S(1)} %add_select_fusion), kind=kOutput, calls=%fused_computation.3 | convolution fusion | flops 29001728 | bytes 78336 | tf_op jit(solution)/shard_map/brcs,bts->brct/dot_general | solution.py:189
  73.6 0.2 pad_maximum_fusion.1
  73.8 0.0 copy-start.7
  73.8 0.8 reshape.137
  74.7 2.3 %fusion.21 = f32[8,2,18,300]{3,2,1,0:T(8,128)S(1)} fusion(f32[8,2,150,18]{3,2,1,0:T(8,128)S(1)} %reshape.137, f32[150,300,1,1]{1,0,3,2:T(8,128)S(1)} %copy-done.3), kind=kOutput, calls=%fused_computation.52 | convolution fusion | flops 155520000 | bytes 698400 | tf_op jit(solution)/shard_map/brms,mn->brsn/dot_general | solution.py:70
  76.9 0.0 copy-start.2
  76.9 0.2 subtract_bitcast_fusion
  77.2 0.7 copy-done.2
  77.9 1.0 %fusion.8 = f32[2,144,150]{2,1,0:T(8,128)S(1)} fusion(f32[2,8,18,144,1]{3,2,4,0,1:T(8,128)S(1)} %copy-done.2, f32[1,8,2,18,150]{4,3,2,1,0:T(8,128)S(1)} %get-tuple-element.12, f32[1,8,2,18,150]{4,3,2,1,0:T(8,128)S(1)} %get-tuple-element.11), kind=kOutput, calls=%fused_computation.12 | convolution fusion | flops 149428800 | bytes 684288 | tf_op jit(solution)/shard_map/pbrsn,pbsa->ran/dot_general | solution.py:84
  78.9 0.1 all_to_all.37
  79.1 0.1 copy.85
  79.2 11.3 %all_to_all.46 = f32[2,8,2700]{2,0,1:T(2,128)S(1)} all-to-all(f32[2,8,2700]{2,0,1:T(2,128)S(1)} %copy.85), channel_id=1, replica_groups=mesh['lat'=16,'freq'=8] {'freq'}, dimensions={1} | all-to-all | bytes 345600 | tf_op jit(solution)/shard_map/all_to_all | solution.py:193
  90.5 0.8 all_to_all.40
  (20 shorter events, 0.1 us)
Async XLA Ops:
  0.0 32.8 %copy-start = (bf16[17,2,2176]{2,1,0:T(2,128)(2,1)S(1)}, bf16[17,2,2176]{2,1,0:T(2,128)(2,1)}, u32[]{:S(2)}) copy-start(bf16[17,2,2176]{2,1,0:T(2,128)(2,1)} %param.15) | copy-start | bytes 443908
  1.7 16.2 %all-to-all-start = ((f32[8,2,2700]{2,1,0:T(2,128)}), f32[8,2,2700]{2,1,0:T(2,128)S(1)}, u32[]{:S(2)}, u32[]{:S(2)}) async-start(f32[8,2,2700]{2,1,0:T(2,128)} %all_to_all.32), calls=%async_computation | async-start | bytes 360448 | tf_op jit(solution)/shard_map/all_to_all | solution.py:156
  10.6 2.1 %copy-start.1 = (bf16[511,1350]{0,1:T(8,128)(2,1)S(1)}, bf16[511,1350]{0,1:T(8,128)(2,1)}, u32[]{:S(2)}) copy-start(bf16[511,1350]{0,1:T(8,128)(2,1)} %param.19) | copy-start | bytes 4139104
  13.4 0.7 copy-start.10
  13.6 4.6 %copy-start.5 = (f32[144,288,1]{1,0,2:T(8,128)S(1)}, f32[144,288,1]{1,0,2:T(8,128)}, u32[]{:S(2)}) copy-start(f32[144,288,1]{1,0,2:T(8,128)} %constant.120) | copy-start | bytes 497668
  13.7 5.4 %copy-start.8 = (f32[150,144]{1,0:T(8,128)S(1)}, f32[150,144]{1,0:T(8,128)}, u32[]{:S(2)}) copy-start(f32[150,144]{1,0:T(8,128)} %constant.100.clone) | copy-start | bytes 259204
  13.8 5.4 %copy-start.9 = (f32[150,144]{1,0:T(8,128)S(1)}, f32[150,144]{1,0:T(8,128)}, u32[]{:S(2)}) copy-start(f32[150,144]{1,0:T(8,128)} %constant.99.clone) | copy-start | bytes 259204
  18.0 1.4 %copy-start.4 = (f32[300,150,1]{0,1,2:T(8,128)S(1)}, f32[300,150,1]{0,1,2:T(8,128)}, u32[]{:S(2)}) copy-start(f32[300,150,1]{0,1,2:T(8,128)} %constant.121) | copy-start | bytes 540004
  24.9 18.4 %all-to-all-start.1 = ((f32[128,2,2,86]{3,1,2,0:T(2,128)}), f32[128,2,2,86]{3,1,2,0:T(2,128)S(1)}, u32[]{:S(2)}, u32[]{:S(2)}) async-start(f32[128,2,2,86]{3,1,2,0:T(2,128)} %bitcast.15), calls=%async_computation.1 | async-start | bytes 524288 | tf_op jit(solution)/shard_map/all_to_all | solution.py:168
  71.6 3.0 %copy-start.3 = (f32[150,300,1,1]{1,0,3,2:T(8,128)S(1)}, f32[150,300,1,1]{1,0,3,2:T(8,128)}, u32[]{:S(2)}) copy-start(f32[150,300,1,1]{1,0,3,2:T(8,128)} %constant.122) | copy-start | bytes 540004
  73.8 3.1 %copy-start.6 = (f32[8,18,150]{2,1,0:T(8,128)S(1)}, f32[8,18,150]{2,1,0:T(8,128)}, u32[]{:S(2)}) copy-start(f32[8,18,150]{2,1,0:T(8,128)} %constant.103.clone) | copy-start | bytes 259204
  73.8 3.1 %copy-start.7 = (f32[8,18,150]{2,1,0:T(8,128)S(1)}, f32[8,18,150]{2,1,0:T(8,128)}, u32[]{:S(2)}) copy-start(f32[8,18,150]{2,1,0:T(8,128)} %constant.104.clone) | copy-start | bytes 259204
  76.9 1.0 %copy-start.2 = (f32[2,8,18,144,1]{3,2,4,0,1:T(8,128)S(1)}, f32[2,8,18,144,1]{3,2,4,0,1:T(8,128)}, u32[]{:S(2)}) copy-start(f32[2,8,18,144,1]{3,2,4,0,1:T(8,128)} %constant.123) | copy-start | bytes 497668

commit v10 on v9

--- a/solution.py
+++ b/solution.py
@@ -12,7 +12,7 @@
 PH = 75
 
 
-highest = lax.Precision.HIGHEST
+precise = lax.Precision.HIGH
 
 
 def angle_table(first, second, period):
@@ -29,7 +29,7 @@
     first_index = np.arange(PA)
     theta_one = angle_table(first_index[:, None], first_index[None, :], PA)
     stage_one = constant(np.concatenate([np.cos(theta_one), -np.sin(theta_one)], axis=1))
-    section = jnp.einsum("rab,ak->rbk", grid, stage_one, precision=highest)
+    section = jnp.einsum("rab,ak->rbk", grid, stage_one, precision=precise)
     section_re = section[..., :PA]
     section_im = section[..., PA:]
     second_index = np.arange(PB)
@@ -47,7 +47,7 @@
     stage_two = constant(
         np.concatenate([np.concatenate([cos_two, -sin_two], axis=1), np.concatenate([sin_two, cos_two], axis=1)])
     )
-    spec = jnp.einsum("rbk,bm->rkm", turned, stage_two, precision=highest)
+    spec = jnp.einsum("rbk,bm->rkm", turned, stage_two, precision=precise)
     scale = (2.0 / L) ** 0.5
     stacked = spec.reshape(rows, PA, 2, PH).transpose(2, 0, 1, 3) * scale
     span = PA // bands
@@ -67,7 +67,7 @@
     stage_two = constant(
         np.concatenate([np.concatenate([cos_two, sin_two], axis=1), np.concatenate([-sin_two, cos_two], axis=1)])
     )
-    middle = jnp.einsum("brms,mn->brsn", parts, stage_two, precision=highest)
+    middle = jnp.einsum("brms,mn->brsn", parts, stage_two, precision=precise)
     middle_re = middle[..., :PB]
     middle_im = middle[..., PB:]
     band_ids = np.arange(bands)
@@ -81,7 +81,7 @@
     first_index = np.arange(PA)
     theta_one = angle_table(freq_one[:, :, None], first_index[None, None, :], PA)
     stage_one = constant(np.stack([np.cos(theta_one), -np.sin(theta_one)]))
-    grid = jnp.einsum("pbrsn,pbsa->ran", turned, stage_one, precision=highest)
+    grid = jnp.einsum("pbrsn,pbsa->ran", turned, stage_one, precision=precise)
     return grid * (2.0 / L) ** 0.5
 
 
@@ -155,7 +155,7 @@
 
     whole_rows = lax.all_to_all(gravity, "freq", split_axis=0, concat_axis=1, tiled=True)
     terms = forward_bands(whole_rows.reshape(mine, PA, PB), bands)
-    own = jnp.einsum("brct,bts->brcs", terms[..., :held], selector, precision=highest)
+    own = jnp.einsum("brct,bts->brcs", terms[..., :held], selector, precision=precise)
     own = own.reshape(bands, mine, 2, blocks, per_slot)
     rest = jnp.pad(terms[..., held:], ((0, 0), (0, 0), (0, 0), (0, padded - band_width)))
     rest = rest.reshape(bands, mine, 2, blocks, share)
@@ -186,7 +186,7 @@
     by_source = lax.all_to_all(stokes, everyone, split_axis=0, concat_axis=0, tiled=True)
     by_source = by_source.reshape(blocks, bands, mine, 2, sub).transpose(1, 2, 3, 0, 4)
     slots_back = by_source[..., :per_slot].reshape(bands, mine, 2, held)
-    slots_back = jnp.einsum("brcs,bts->brct", slots_back, selector, precision=highest)
+    slots_back = jnp.einsum("brcs,bts->brct", slots_back, selector, precision=precise)
     rest_back = by_source[..., per_slot:].reshape(bands, mine, 2, blocks * share)
     by_band = jnp.concatenate([slots_back, rest_back], axis=3)[..., :band_width]
     grid_rows = inverse_rows(by_band, bands)

time: 91.8 us -> 88.7 us (0.966)
  matrix products: 17.4 us -> 14.3 us
    dot_general x6, matrix products: 8.47 us -> 5.37 us  [the longest x1 1.24 us: per_device(): jnp.einsum('brcs,bts->brct', slots_back, selector, precision=precise)]
where the time goes in v10:
time: 88.7 us; the launch traced here: 88.2 us
  blocking collectives  30 us (34%)
  starting transfers between devices  15.7 us (18%)
  matrix products  14.3 us (16%)
  local copies, waits for them, and re-layouts  13.9 us (16%)
  Pallas kernels  6.86 us (8%)
  waiting for transfers between devices  4.17 us (5%)
  other arithmetic  2.85 us (3%)
    all_to_all x1, blocking collectives, per_device(): lax.all_to_all(stokes, everyone, split_axis=0, concat_axis=0, tiled=True)  18.7 us
    all_to_all x1, blocking collectives, per_device(): lax.all_to_all(grid_rows.reshape(mine, L), 'freq', split_axis=1, concat_a...  11.3 us
    dot_general x1, matrix products, per_device(): jnp.einsum('ocn,onq->ocq', coef, legendre, preferred_element_type=jnp.flo...  8.94 us
    all_to_all x1, starting transfers between devices, per_device(): lax.all_to_all(gravity, 'freq', split_axis=0, concat_axis=1, tiled=True)  7.89 us
    all_to_all x1, starting transfers between devices, per_device(): lax.all_to_all(payload, everyone, split_axis=0, concat_axis=0, tiled=True)  7.8 us
    pallas_call x1, Pallas kernels, toeplitz_stokes(): pl.pallas_call(stokes_body, out_shape=jax.ShapeDtypeStruct((2, total, LAN...  6.86 us
    unnamed x23, local copies, waits for them, and re-layouts  2.9 us
    all_to_all x1, waiting for transfers between devices, per_device(): lax.all_to_all(gravity, 'freq', split_axis=0, concat_axis=1, tiled=True)  2.69 us
  transfers between devices with their start and end apart: 2, of which 2 were waited for; matrix products, arithmetic and copies ran while one was open for 16% of the time, Pallas kernels for 0%

profile of v10, /device:TPU:0, one launch (start us, length us, event | category | flops | bytes accessed | tf_op | source)
XLA Modules:
  0.0 88.2 jit_solution(10834983478070323597)
XLA Ops:
  0.0 1.7 %all_to_all.32 = f32[8,2,2700]{2,1,0:T(2,128)} reshape(f32[16,2700]{1,0:T(8,128)} %param.14) | data formatting | bytes 345600 | tf_op jit(solution)/shard_map/all_to_all | solution.py:156
  1.7 7.9 %all-to-all-start = ((f32[8,2,2700]{2,1,0:T(2,128)}), f32[8,2,2700]{2,1,0:T(2,128)S(1)}, u32[]{:S(2)}, u32[]{:S(2)}) async-start(f32[8,2,2700]{2,1,0:T(2,128)} %all_to_all.32), calls=%async_computation | async-start | bytes 360448 | tf_op jit(solution)/shard_map/all_to_all | solution.py:156
  9.6 0.9 %reshape.124 = s32[16,8,17]{2,1,0:T(8,128)S(1)} reshape(s32[2176]{0:T(1024)} %param.17) | data formatting | bytes 17408 | tf_op jit(solution)/shard_map/reshape | solution.py:151
  10.6 0.1 reshape.125
  10.6 0.0 copy-start.1
  10.7 0.1 fusion.19
  10.8 0.1 compare_and_fusion
  10.9 1.9 %copy.71 = bf16[511,1350]{1,0:T(8,128)(2,1)S(1)} copy(bf16[511,1350]{0,1:T(8,128)(2,1)} %param.19) | data formatting | bytes 2759400 | tf_op args[5]
  12.8 0.6 gather_fusion
  13.4 0.0 copy-start.10
  13.4 0.1 copy.70
  13.6 0.0 copy-start.5
  13.6 0.2 pad_dynamic-slice_fusion
  13.8 0.0 copy-start.9
  13.8 0.1 pad_maximum_fusion.2
  13.9 0.2 copy-done.10
  14.1 0.1 multiply_cosine_fusion
  14.2 0.4 rev.3
  14.6 0.7 pad_convert_fusion.k_ref
  15.3 2.7 %all-to-all-done = f32[8,2,2700]{2,1,0:T(2,128)S(1)} async-done(((f32[8,2,2700]{2,1,0:T(2,128)}), f32[8,2,2700]{2,1,0:T(2,128)S(1)}, u32[]{:S(2)}, u32[]{:S(2)}) %all-to-all-start) | async-done | bytes 172832 | tf_op jit(solution)/shard_map/all_to_all | solution.py:156
  18.0 0.0 copy-start.4
  18.0 0.1 reshape.126
  18.2 0.6 convolution_bitcast_fusion
  18.8 0.2 multiply_add_fusion
  19.0 0.8 convolution_multiply_fusion
  19.8 0.2 mul.109
  20.0 0.5 copy.75
  20.6 0.5 reshape.128
  21.1 0.1 slice.53
  21.2 1.0 %fusion.3 = f32[8,2,2,272]{3,2,1,0:T(2,128)S(1)} fusion(s32[8,272]{1,0:T(8,128)S(1)} %add_select_fusion, f32[8,2,2,272]{3,0,2,1:T(8,128)S(1)} %slice.52), kind=kOutput, calls=%fused_computation.4 | convolution fusion | flops 14796800 | bytes 78336 | tf_op jit(solution)/shard_map/brct,bts->brcs/dot_general | solution.py:158
  22.1 0.2 reshape.129
  22.4 0.2 reshape.130
  22.6 0.1 broadcast_in_dim.11
  22.7 0.2 maximum_bitcast_fusion
  22.9 0.9 %copy.78 = f32[16,8,2,2,86]{4,2,3,1,0:T(2,128)} copy(f32[16,8,2,2,86]{4,0,1,3,2:T(8,128)S(1)} %maximum_bitcast_fusion) | data formatting | bytes 352256 | tf_op jit(solution)/shard_map/transpose | solution.py:165
  23.8 7.8 %all-to-all-start.1 = ((f32[128,2,2,86]{3,1,2,0:T(2,128)}), f32[128,2,2,86]{3,1,2,0:T(2,128)S(1)}, u32[]{:S(2)}, u32[]{:S(2)}) async-start(f32[128,2,2,86]{3,1,2,0:T(2,128)} %bitcast.15), calls=%async_computation.1 | async-start | bytes 524288 | tf_op jit(solution)/shard_map/all_to_all | solution.py:168
  31.6 8.9 %convolution_convert_fusion = bf16[17,2,256]{2,1,0:T(2,128)(2,1)S(1)} fusion(bf16[17,2,2176]{2,1,0:T(2,128)(2,1)S(1)} %copy-done, bf16[17,2176,256]{2,1,0:T(8,128)(2,1)} %param.16), kind=kOutput, calls=%fused_computation.13 | convolution fusion | flops 37888512 | bytes 19105280 | tf_op jit(solution)/shard_map/ocn,onq->ocq/dot_general | solution.py:173
  40.5 0.2 copy.80
  40.7 1.5 %all-to-all-done.1 = f32[128,2,2,86]{3,1,2,0:T(2,128)S(1)} async-done(((f32[128,2,2,86]{3,1,2,0:T(2,128)}), f32[128,2,2,86]{3,1,2,0:T(2,128)S(1)}, u32[]{:S(2)}, u32[]{:S(2)}) %all-to-all-start.1) | async-done | bytes 176160 | tf_op jit(solution)/shard_map/all_to_all | solution.py:168
  42.2 0.1 copy.79
  42.3 0.2 slice_reduce_fusion
  42.5 0.1 fusion.15
  42.6 0.7 pad_convert_fusion.1.w_ref
  43.3 6.9 %shard_map.136 = f32[2,256,128]{2,1,0:T(8,128)} custom-call(f32[520,128]{1,0:T(8,128)} %pad_convert_fusion.k_ref, f32[2,256,128]{2,1,0:T(8,128)} %pad_convert_fusion.1.w_ref), custom_call_target="tpu_custom_call" | custom-call | tf_op jit(solution)/shard_map/pallas_call | solution.py:127
  50.2 1.0 %copy.104 = f32[2,128,2,85]{3,2,0,1:T(2,128)S(1)} copy(f32[2,128,2,85]{3,2,1,0:T(2,128)} %bitcast.89) | data formatting | bytes 348160 | tf_op jit(solution)/shard_map/reshape | solution.py:185
  51.2 18.7 %all_to_all.45 = f32[128,2,2,85]{3,1,2,0:T(2,128)S(1)} all-to-all(f32[128,2,2,85]{3,1,2,0:T(2,128)S(1)} %bitcast.90), channel_id=1, replica_groups=mesh['lat'=16,'freq'=8] {'lat','freq'}, dimensions={0} | all-to-all | bytes 348160 | tf_op jit(solution)/shard_map/all_to_all | solution.py:186
  69.9 0.2 copy.103
  70.1 0.1 slice.58
  70.2 0.3 reshape.136
  70.5 0.0 copy-start.3
  70.5 0.2 reshape.135
  70.7 1.2 %fusion.1 = f32[8,2,2,272]{3,2,1,0:T(2,128)S(1)} fusion(f32[8,2,2,272]{3,2,1,0:T(2,128)S(1)} %reshape.135, s32[8,272]{1,0:T(8,128)S(1)} %add_select_fusion), kind=kOutput, calls=%fused_computation.3 | convolution fusion | flops 14796800 | bytes 78336 | tf_op jit(solution)/shard_map/brcs,bts->brct/dot_general | solution.py:189
  71.9 0.2 pad_maximum_fusion.1
  72.2 0.0 copy-start.7
  72.2 0.8 reshape.137
  73.0 1.2 %fusion.21 = f32[8,2,18,300]{3,2,1,0:T(8,128)S(1)} fusion(f32[8,2,150,18]{3,2,1,0:T(8,128)S(1)} %reshape.137, f32[150,300,1,1]{1,0,3,2:T(8,128)S(1)} %copy-done.3), kind=kOutput, calls=%fused_computation.52 | convolution fusion | flops 77760000 | bytes 698400 | tf_op jit(solution)/shard_map/brms,mn->brsn/dot_general | solution.py:70
  74.2 0.0 copy-start.2
  74.3 0.2 subtract_bitcast_fusion
  74.5 0.7 copy-done.2
  75.2 0.6 fusion.8
  75.8 0.1 all_to_all.37
  76.0 0.1 copy.85
  76.1 11.3 %all_to_all.46 = f32[2,8,2700]{2,0,1:T(2,128)S(1)} all-to-all(f32[2,8,2700]{2,0,1:T(2,128)S(1)} %copy.85), channel_id=1, replica_groups=mesh['lat'=16,'freq'=8] {'freq'}, dimensions={1} | all-to-all | bytes 345600 | tf_op jit(solution)/shard_map/all_to_all | solution.py:193
  87.4 0.8 all_to_all.40
  (20 shorter events, 0.1 us)
Async XLA Ops:
  0.0 31.6 %copy-start = (bf16[17,2,2176]{2,1,0:T(2,128)(2,1)S(1)}, bf16[17,2,2176]{2,1,0:T(2,128)(2,1)}, u32[]{:S(2)}) copy-start(bf16[17,2,2176]{2,1,0:T(2,128)(2,1)} %param.15) | copy-start | bytes 443908
  1.7 16.2 %all-to-all-start = ((f32[8,2,2700]{2,1,0:T(2,128)}), f32[8,2,2700]{2,1,0:T(2,128)S(1)}, u32[]{:S(2)}, u32[]{:S(2)}) async-start(f32[8,2,2700]{2,1,0:T(2,128)} %all_to_all.32), calls=%async_computation | async-start | bytes 360448 | tf_op jit(solution)/shard_map/all_to_all | solution.py:156
  10.6 2.1 %copy-start.1 = (bf16[511,1350]{0,1:T(8,128)(2,1)S(1)}, bf16[511,1350]{0,1:T(8,128)(2,1)}, u32[]{:S(2)}) copy-start(bf16[511,1350]{0,1:T(8,128)(2,1)} %param.19) | copy-start | bytes 4139104
  13.4 0.7 copy-start.10
  13.6 4.6 %copy-start.5 = (f32[144,288,1]{1,0,2:T(8,128)S(1)}, f32[144,288,1]{1,0,2:T(8,128)}, u32[]{:S(2)}) copy-start(f32[144,288,1]{1,0,2:T(8,128)} %constant.120) | copy-start | bytes 497668
  13.7 5.0 %copy-start.8 = (f32[150,144]{1,0:T(8,128)S(1)}, f32[150,144]{1,0:T(8,128)}, u32[]{:S(2)}) copy-start(f32[150,144]{1,0:T(8,128)} %constant.100.clone) | copy-start | bytes 259204
  13.8 5.0 %copy-start.9 = (f32[150,144]{1,0:T(8,128)S(1)}, f32[150,144]{1,0:T(8,128)}, u32[]{:S(2)}) copy-start(f32[150,144]{1,0:T(8,128)} %constant.99.clone) | copy-start | bytes 259204
  18.0 1.0 %copy-start.4 = (f32[300,150,1]{0,1,2:T(8,128)S(1)}, f32[300,150,1]{0,1,2:T(8,128)}, u32[]{:S(2)}) copy-start(f32[300,150,1]{0,1,2:T(8,128)} %constant.121) | copy-start | bytes 540004
  23.8 18.4 %all-to-all-start.1 = ((f32[128,2,2,86]{3,1,2,0:T(2,128)}), f32[128,2,2,86]{3,1,2,0:T(2,128)S(1)}, u32[]{:S(2)}, u32[]{:S(2)}) async-start(f32[128,2,2,86]{3,1,2,0:T(2,128)} %bitcast.15), calls=%async_computation.1 | async-start | bytes 524288 | tf_op jit(solution)/shard_map/all_to_all | solution.py:168
  70.5 2.5 %copy-start.3 = (f32[150,300,1,1]{1,0,3,2:T(8,128)S(1)}, f32[150,300,1,1]{1,0,3,2:T(8,128)}, u32[]{:S(2)}) copy-start(f32[150,300,1,1]{1,0,3,2:T(8,128)} %constant.122) | copy-start | bytes 540004
  72.2 2.1 %copy-start.6 = (f32[8,18,150]{2,1,0:T(8,128)S(1)}, f32[8,18,150]{2,1,0:T(8,128)}, u32[]{:S(2)}) copy-start(f32[8,18,150]{2,1,0:T(8,128)} %constant.103.clone) | copy-start | bytes 259204
  72.2 2.1 %copy-start.7 = (f32[8,18,150]{2,1,0:T(8,128)S(1)}, f32[8,18,150]{2,1,0:T(8,128)}, u32[]{:S(2)}) copy-start(f32[8,18,150]{2,1,0:T(8,128)} %constant.104.clone) | copy-start | bytes 259204
  74.2 1.0 %copy-start.2 = (f32[2,8,18,144,1]{3,2,4,0,1:T(8,128)S(1)}, f32[2,8,18,144,1]{3,2,4,0,1:T(8,128)}, u32[]{:S(2)}) copy-start(f32[2,8,18,144,1]{3,2,4,0,1:T(8,128)} %constant.123) | copy-start | bytes 497668

commit v11 on v10

--- a/solution.py
+++ b/solution.py
@@ -55,7 +55,7 @@
     return stacked.reshape(bands, rows, 2, PH * span)
 
 
-def inverse_rows(spectra, bands):
+def inverse_rows(spectra, bands, band_self):
     rows = spectra.shape[1]
     span = PA // bands
     parts = spectra.reshape(bands, rows, 2 * PH, span)
@@ -81,6 +81,7 @@
     first_index = np.arange(PA)
     theta_one = angle_table(freq_one[:, :, None], first_index[None, None, :], PA)
     stage_one = constant(np.stack([np.cos(theta_one), -np.sin(theta_one)]))
+    stage_one = lax.dynamic_slice_in_dim(stage_one, band_self * span, span, 3)
     grid = jnp.einsum("pbrsn,pbsa->ran", turned, stage_one, precision=precise)
     return grid * (2.0 / L) ** 0.5
 
@@ -182,15 +183,16 @@
         jnp.pad(kernel, ((0, 0), (0, padded - band_width))), held + block_self * share, share, 1
     )
     stokes = toeplitz_stokes(jnp.concatenate([kernel_own, kernel_rest], axis=1), weighted)
-    stokes = stokes.reshape(2, devices, mine, sub).transpose(1, 2, 0, 3)
+    stokes = stokes.reshape(2, blocks, rows, sub).transpose(1, 2, 0, 3)
+    stokes = jnp.broadcast_to(stokes[:, None], (blocks, bands, rows, 2, sub)).reshape(devices, rows, 2, sub)
     by_source = lax.all_to_all(stokes, everyone, split_axis=0, concat_axis=0, tiled=True)
-    by_source = by_source.reshape(blocks, bands, mine, 2, sub).transpose(1, 2, 3, 0, 4)
-    slots_back = by_source[..., :per_slot].reshape(bands, mine, 2, held)
+    by_source = by_source.reshape(blocks, bands, rows, 2, sub).transpose(1, 2, 3, 0, 4)
+    slots_back = by_source[..., :per_slot].reshape(bands, rows, 2, held)
     slots_back = jnp.einsum("brcs,bts->brct", slots_back, selector, precision=precise)
-    rest_back = by_source[..., per_slot:].reshape(bands, mine, 2, blocks * share)
+    rest_back = by_source[..., per_slot:].reshape(bands, rows, 2, blocks * share)
     by_band = jnp.concatenate([slots_back, rest_back], axis=3)[..., :band_width]
-    grid_rows = inverse_rows(by_band, bands)
-    geoid = lax.all_to_all(grid_rows.reshape(mine, L), "freq", split_axis=1, concat_axis=0, tiled=True)
+    grid_rows = inverse_rows(by_band, bands, band_self)
+    geoid = grid_rows.reshape(rows, L // bands)
     return geoid
 
 

time: 88.7 us -> 130 us (1.47)
  blocking collectives: 30 us -> 0 us
  waiting for transfers between devices: 4.17 us -> 33.5 us
  local copies, waits for them, and re-layouts: 13.9 us -> 33.4 us
  matrix products: 14.3 us -> 27.2 us
  starting transfers between devices: 15.7 us -> 23.9 us
    all_to_all x2 -> x0, blocking collectives: 30 us -> none  [the longest x1 18.7 us: per_device(): lax.all_to_all(stokes, everyone, split_axis=0, concat_axis=0, tiled=True)]
    all_to_all x0 -> x1, waiting for transfers between devices: none -> 29.1 us  [per_device(): lax.all_to_all(stokes, everyone, split_axis=0, concat_axis=0, tiled=True)]
    dot_general x1, matrix products: 1.21 us -> 11.1 us  [inverse_rows(): middle = jnp.einsum('brms,mn->brsn', parts, stage_two, precision=precise)]
    all_to_all x0 -> x1, starting transfers between devices: none -> 8.48 us  [per_device(): lax.all_to_all(stokes, everyone, split_axis=0, concat_axis=0, tiled=True)]
    slice x1 -> x4, local copies, waits for them, and re-layouts: 0.12 us -> 7.75 us  [the longest x2 4.49 us: per_device(): by_source[..., per_slot:].reshape(bands, rows, 2, blocks * share)]
    reshape x1, local copies, waits for them, and re-layouts: 0.81 us -> 7.9 us  [inverse_rows(): parts = spectra.reshape(bands, rows, 2 * PH, span)]
    reshape x4 -> x3, local copies, waits for them, and re-layouts: 1.65 us -> 5.84 us  [the longest x1 2.65 us: per_device(): slots_back = by_source[..., :per_slot].reshape(bands, rows, 2, held)]
    dot_general x1, matrix products: 0.58 us -> 3.57 us  [inverse_rows(): grid = jnp.einsum('pbrsn,pbsa->ran', turned, stage_one, precision=precise)]
  transfers between devices with their start and end apart: 2 -> 3, of which waited for: 2 -> 3; matrix products, arithmetic and copies ran while one was open for 16% -> 11% of each run, Pallas kernels for 0% -> 0%
where the time goes in v11:
time: 130 us; the launch traced here: 129 us
  waiting for transfers between devices  33.5 us (26%)
  local copies, waits for them, and re-layouts  33.4 us (26%)
  matrix products  27.2 us (21%)
  starting transfers between devices  23.9 us (18%)
  Pallas kernels  6.85 us (5%)
  other arithmetic  3.75 us (3%)
    all_to_all x1, waiting for transfers between devices, per_device(): lax.all_to_all(stokes, everyone, split_axis=0, concat_axis=0, tiled=True)  29.1 us
    dot_general x1, matrix products, inverse_rows(): middle = jnp.einsum('brms,mn->brsn', parts, stage_two, precision=precise)  11.1 us
    dot_general x1, matrix products, per_device(): jnp.einsum('ocn,onq->ocq', coef, legendre, preferred_element_type=jnp.flo...  8.94 us
    all_to_all x1, starting transfers between devices, per_device(): lax.all_to_all(stokes, everyone, split_axis=0, concat_axis=0, tiled=True)  8.48 us
    reshape x1, local copies, waits for them, and re-layouts, inverse_rows(): parts = spectra.reshape(bands, rows, 2 * PH, span)  7.9 us
    all_to_all x1, starting transfers between devices, per_device(): lax.all_to_all(gravity, 'freq', split_axis=0, concat_axis=1, tiled=True)  7.89 us
    all_to_all x1, starting transfers between devices, per_device(): lax.all_to_all(payload, everyone, split_axis=0, concat_axis=0, tiled=True)  7.52 us
    pallas_call x1, Pallas kernels, toeplitz_stokes(): pl.pallas_call(stokes_body, out_shape=jax.ShapeDtypeStruct((2, total, LAN...  6.85 us
  transfers between devices with their start and end apart: 3, of which 3 were waited for; matrix products, arithmetic and copies ran while one was open for 11% of the time, Pallas kernels for 0%

profile of v11, /device:TPU:0, one launch (start us, length us, event | category | flops | bytes accessed | tf_op | source)
XLA Modules:
  0.0 129.0 jit_solution(394227208609567808)
XLA Ops:
  0.0 0.0 copy-start
  0.0 1.8 %all_to_all.18 = f32[8,2,2700]{2,1,0:T(2,128)} reshape(f32[16,2700]{1,0:T(8,128)} %param.14) | data formatting | bytes 345600 | tf_op jit(solution)/shard_map/all_to_all | solution.py:157
  1.8 7.9 %all-to-all-start = ((f32[8,2,2700]{2,1,0:T(2,128)}), f32[8,2,2700]{2,1,0:T(2,128)S(1)}, u32[]{:S(2)}, u32[]{:S(2)}) async-start(f32[8,2,2700]{2,1,0:T(2,128)} %all_to_all.18), calls=%async_computation | async-start | bytes 360448 | tf_op jit(solution)/shard_map/all_to_all | solution.py:157
  9.7 0.9 reshape.126
  10.6 0.1 reshape.127
  10.8 0.1 fusion.29
  10.8 0.1 compare_and_fusion
  10.9 0.0 copy-start.11
  10.9 1.8 %copy.74 = bf16[511,1350]{1,0:T(8,128)(2,1)S(1)} copy(bf16[511,1350]{0,1:T(8,128)(2,1)} %param.19) | data formatting | bytes 2759400 | tf_op args[5]
  12.8 0.0 copy-start.6
  12.8 0.6 gather_fusion
  13.4 0.0 copy-start.9
  13.4 0.0 copy-start.10
  13.4 0.1 copy.73
  13.6 0.2 pad_dynamic-slice_fusion
  13.7 0.1 pad_maximum_fusion.2
  13.8 0.0 copy-done.11
  13.9 0.1 multiply_cosine_fusion
  14.0 0.4 rev.3
  14.4 0.7 pad_convert_fusion.k_ref
  15.1 3.0 %all-to-all-done = f32[8,2,2700]{2,1,0:T(2,128)S(1)} async-done(((f32[8,2,2700]{2,1,0:T(2,128)}), f32[8,2,2700]{2,1,0:T(2,128)S(1)}, u32[]{:S(2)}, u32[]{:S(2)}) %all-to-all-start) | async-done | bytes 172832 | tf_op jit(solution)/shard_map/all_to_all | solution.py:157
  18.1 0.1 reshape.128
  18.2 0.6 convolution_bitcast_fusion
  18.9 0.0 copy-done.10
  18.9 0.2 multiply_add_fusion
  19.1 0.8 convolution_multiply_fusion
  19.9 0.2 mul.113
  20.1 0.5 copy.78
  20.6 0.5 reshape.130
  21.1 0.1 slice.53
  21.3 1.0 fusion.5
  22.2 0.2 reshape.132
  22.5 0.2 reshape.131
  22.6 0.1 broadcast_in_dim.16
  22.7 0.2 maximum_bitcast_fusion
  22.9 0.9 copy.81
  23.8 7.5 %all-to-all-start.1 = ((f32[128,2,2,86]{3,1,2,0:T(2,128)}), f32[128,2,2,86]{3,1,2,0:T(2,128)S(1)}, u32[]{:S(2)}, u32[]{:S(2)}) async-start(f32[128,2,2,86]{3,1,2,0:T(2,128)} %bitcast.17), calls=%async_computation.1 | async-start | bytes 524288 | tf_op jit(solution)/shard_map/all_to_all | solution.py:169
  31.4 8.9 %convolution_convert_fusion = bf16[17,2,256]{2,1,0:T(2,128)(2,1)S(1)} fusion(bf16[17,2,2176]{2,1,0:T(2,128)(2,1)S(1)} %copy-done, bf16[17,2176,256]{2,1,0:T(8,128)(2,1)} %param.16), kind=kOutput, calls=%fused_computation.19 | convolution fusion | flops 37888512 | bytes 19105280 | tf_op jit(solution)/shard_map/ocn,onq->ocq/dot_general | solution.py:174
  40.3 0.2 copy.83
  40.5 1.5 %all-to-all-done.1 = f32[128,2,2,86]{3,1,2,0:T(2,128)S(1)} async-done(((f32[128,2,2,86]{3,1,2,0:T(2,128)}), f32[128,2,2,86]{3,1,2,0:T(2,128)S(1)}, u32[]{:S(2)}, u32[]{:S(2)}) %all-to-all-start.1) | async-done | bytes 176160 | tf_op jit(solution)/shard_map/all_to_all | solution.py:169
  42.0 0.1 copy.82
  42.1 0.2 slice_reduce_fusion
  42.2 0.1 fusion.25
  42.4 0.7 pad_convert_fusion.1.w_ref
  43.1 6.9 %shard_map.136 = f32[2,256,128]{2,1,0:T(8,128)} custom-call(f32[520,128]{1,0:T(8,128)} %pad_convert_fusion.k_ref, f32[2,256,128]{2,1,0:T(8,128)} %pad_convert_fusion.1.w_ref), custom_call_target="tpu_custom_call" | custom-call | tf_op jit(solution)/shard_map/pallas_call | solution.py:128
  49.9 1.0 copy.84
  50.9 1.6 %broadcast_in_dim.17 = f32[16,8,16,2,85]{4,2,3,1,0:T(8,128)} broadcast(f32[16,16,2,85]{3,1,2,0:T(8,128)S(1)} %copy.84), dimensions={0,2,3,4} | broadcast | bytes 1566720 | tf_op jit(solution)/shard_map/broadcast_in_dim | solution.py:187
  52.5 8.5 %all-to-all-start.2 = ((f32[128,16,2,85]{3,1,2,0:T(8,128)}), f32[128,16,2,85]{3,1,2,0:T(8,128)S(1)}, u32[]{:S(2)}, u32[]{:S(2)}) async-start(f32[128,16,2,85]{3,1,2,0:T(8,128)} %bitcast.89), calls=%async_computation.2 | async-start | bytes 4194304 | tf_op jit(solution)/shard_map/all_to_all | solution.py:188
  61.0 29.1 %all-to-all-done.2 = f32[128,16,2,85]{3,1,2,0:T(8,128)S(1)} async-done(((f32[128,16,2,85]{3,1,2,0:T(8,128)}), f32[128,16,2,85]{3,1,2,0:T(8,128)S(1)}, u32[]{:S(2)}, u32[]{:S(2)}) %all-to-all-start.2) | async-done | bytes 1392672 | tf_op jit(solution)/shard_map/all_to_all | solution.py:188
  90.1 2.0 %slice.58 = f32[8,16,2,16,68]{4,1,2,0,3:T(8,128)} slice(f32[8,16,2,16,85]{4,1,2,0,3:T(8,128)S(1)} %bitcast.87), slice={[0:8], [0:16], [0:2], [0:16], [17:85]} | slice | bytes 2228224 | tf_op jit(solution)/shard_map/slice | solution.py:192
  92.0 2.5 %copy.85 = f32[8,16,2,16,17]{4,3,1,2,0:T(8,128)} copy(f32[8,16,2,16,17]{4,1,2,0,3:T(8,128)S(1)} %bitcast.88) | data formatting | bytes 557056 | tf_op jit(solution)/shard_map/slice | solution.py:190
  94.5 2.7 %reshape.138 = f32[8,16,2,272]{3,1,2,0:T(8,128)S(1)} reshape(f32[8,16,2,16,17]{4,3,1,2,0:T(8,128)} %copy.85) | data formatting | bytes 557056 | tf_op jit(solution)/shard_map/reshape | solution.py:190
  97.2 1.3 %fusion.3 = f32[8,16,2,272]{3,1,2,0:T(8,128)S(1)} fusion(f32[8,16,2,272]{3,1,2,0:T(8,128)S(1)} %reshape.138, s32[8,272]{1,0:T(8,128)S(1)} %add_select_fusion), kind=kOutput, calls=%fused_computation.6 | convolution fusion | flops 114231296 | bytes 565760 | tf_op jit(solution)/shard_map/brcs,bts->brct/dot_general | solution.py:191
  98.5 2.5 %copy.86 = f32[8,16,2,16,68]{4,3,1,2,0:T(8,128)} copy(f32[8,16,2,16,68]{4,1,2,0,3:T(8,128)S(1)} %copy-done.2) | data formatting | bytes 2228224 | tf_op jit(solution)/shard_map/slice | solution.py:192
  101.0 2.3 %reshape.139 = f32[8,16,2,1088]{3,1,2,0:T(8,128)S(1)} reshape(f32[8,16,2,16,68]{4,3,1,2,0:T(8,128)} %copy.86) | data formatting | bytes 2228224 | tf_op jit(solution)/shard_map/reshape | solution.py:192
  103.4 0.4 pad_maximum_fusion.1
  103.8 0.7 copy.87
  104.5 0.0 copy-start.5
  104.5 7.9 %reshape.140 = f32[8,16,150,18]{3,2,1,0:T(8,128)} reshape(f32[8,16,2,1350]{3,2,1,0:T(2,128)S(1)} %copy.87) | data formatting | bytes 2764800 | tf_op jit(solution)/shard_map/reshape | solution.py:61
  112.5 11.1 %fusion.32 = f32[8,16,18,300]{3,2,1,0:T(8,128)S(1)} fusion(f32[8,16,150,18]{3,2,1,0:T(8,128)} %reshape.140, f32[150,300,1,1]{1,0,3,2:T(8,128)S(1)} %copy-done.5), kind=kOutput, calls=%fused_computation.54 | convolution fusion | flops 622080000 | bytes 4327200 | tf_op jit(solution)/shard_map/brms,mn->brsn/dot_general | solution.py:70
  123.5 1.0 subtract_bitcast_fusion
  124.5 0.0 copy-start.1
  124.5 3.6 %fusion.15 = f32[16,18,150]{2,1,0:T(8,128)S(1)} fusion(f32[2,8,18,144]{2,3,0,1:T(8,128)} %constant.109.clone, s32[]{:T(128)S(6)} %select_n.48, f32[1,8,16,18,150]{4,3,2,1,0:T(8,128)S(1)} %get-tuple-element.12, f32[1,8,16,18,150]{4,3,2,1,0:T(8,128)S(1)} %get-tuple-element.11), kind=kOutput, calls=%fused_computation.17 | convolution fusion | flops 75384000 | bytes 3134212 | tf_op jit(solution)/shard_map/pbrsn,pbsa->ran/dot_general | solution.py:85
  128.1 0.8 reshape.141
  (23 shorter events, 0.1 us)
Async XLA Ops:
  0.0 31.4 %copy-start = (bf16[17,2,2176]{2,1,0:T(2,128)(2,1)S(1)}, bf16[17,2,2176]{2,1,0:T(2,128)(2,1)}, u32[]{:S(2)}) copy-start(bf16[17,2,2176]{2,1,0:T(2,128)(2,1)} %param.15) | copy-start | bytes 443908
  0.0 12.8 %copy-start.3 = (bf16[511,1350]{0,1:T(8,128)(2,1)S(1)}, bf16[511,1350]{0,1:T(8,128)(2,1)}, u32[]{:S(2)}) copy-start(bf16[511,1350]{0,1:T(8,128)(2,1)} %param.19) | copy-start | bytes 4139104
  1.8 16.2 %all-to-all-start = ((f32[8,2,2700]{2,1,0:T(2,128)}), f32[8,2,2700]{2,1,0:T(2,128)S(1)}, u32[]{:S(2)}, u32[]{:S(2)}) async-start(f32[8,2,2700]{2,1,0:T(2,128)} %all_to_all.18), calls=%async_computation | async-start | bytes 360448 | tf_op jit(solution)/shard_map/all_to_all | solution.py:157
  10.9 2.9 %copy-start.11 = (s32[16]{0:T(128)S(1)}, s32[16]{0:T(128)}, u32[]{:S(2)}) copy-start(s32[16]{0:T(128)} %param.18) | copy-start | bytes 196
  12.8 5.5 %copy-start.6 = (f32[144,288,1]{1,0,2:T(8,128)S(1)}, f32[144,288,1]{1,0,2:T(8,128)}, u32[]{:S(2)}) copy-start(f32[144,288,1]{1,0,2:T(8,128)} %constant.124) | copy-start | bytes 497668
  13.4 5.5 %copy-start.9 = (f32[150,144]{1,0:T(8,128)S(1)}, f32[150,144]{1,0:T(8,128)}, u32[]{:S(2)}) copy-start(f32[150,144]{1,0:T(8,128)} %constant.104.clone) | copy-start | bytes 259204
  13.4 5.5 %copy-start.10 = (f32[150,144]{1,0:T(8,128)S(1)}, f32[150,144]{1,0:T(8,128)}, u32[]{:S(2)}) copy-start(f32[150,144]{1,0:T(8,128)} %constant.103.clone) | copy-start | bytes 259204
  13.6 5.5 %copy-start.4 = (f32[300,150,1]{0,1,2:T(8,128)S(1)}, f32[300,150,1]{0,1,2:T(8,128)}, u32[]{:S(2)}) copy-start(f32[300,150,1]{0,1,2:T(8,128)} %constant.125) | copy-start | bytes 540004
  23.8 18.1 %all-to-all-start.1 = ((f32[128,2,2,86]{3,1,2,0:T(2,128)}), f32[128,2,2,86]{3,1,2,0:T(2,128)S(1)}, u32[]{:S(2)}, u32[]{:S(2)}) async-start(f32[128,2,2,86]{3,1,2,0:T(2,128)} %bitcast.17), calls=%async_computation.1 | async-start | bytes 524288 | tf_op jit(solution)/shard_map/all_to_all | solution.py:169
  52.5 37.5 %all-to-all-start.2 = ((f32[128,16,2,85]{3,1,2,0:T(8,128)}), f32[128,16,2,85]{3,1,2,0:T(8,128)S(1)}, u32[]{:S(2)}, u32[]{:S(2)}) async-start(f32[128,16,2,85]{3,1,2,0:T(8,128)} %bitcast.89), calls=%async_computation.2 | async-start | bytes 4194304 | tf_op jit(solution)/shard_map/all_to_all | solution.py:188
  94.5 4.0 %copy-start.2 = (f32[8,16,2,16,68]{4,1,2,0,3:T(8,128)S(1)}, f32[8,16,2,16,68]{4,1,2,0,3:T(8,128)}, u32[]{:S(2)}) copy-start(f32[8,16,2,16,68]{4,1,2,0,3:T(8,128)} %slice.58) | copy-start | bytes 3342340
  104.5 7.9 %copy-start.5 = (f32[150,300,1,1]{1,0,3,2:T(8,128)S(1)}, f32[150,300,1,1]{1,0,3,2:T(8,128)}, u32[]{:S(2)}) copy-start(f32[150,300,1,1]{1,0,3,2:T(8,128)} %constant.126) | copy-start | bytes 540004
  112.5 11.1 %copy-start.7 = (f32[8,18,150]{2,1,0:T(8,128)S(1)}, f32[8,18,150]{2,1,0:T(8,128)}, u32[]{:S(2)}) copy-start(f32[8,18,150]{2,1,0:T(8,128)} %constant.108.clone) | copy-start | bytes 259204
  112.5 11.1 %copy-start.8 = (f32[8,18,150]{2,1,0:T(8,128)S(1)}, f32[8,18,150]{2,1,0:T(8,128)}, u32[]{:S(2)}) copy-start(f32[8,18,150]{2,1,0:T(8,128)} %constant.107.clone) | copy-start | bytes 259204
  124.5 4.4 %copy-start.1 = (bf16[17,2,2176]{2,1,0:T(2,128)(2,1)S(1)}, bf16[17,2,2176]{2,1,0:T(2,128)(2,1)}, u32[]{:S(2)}) copy-start(bf16[17,2,2176]{2,1,0:T(2,128)(2,1)} %param.15) | copy-start | bytes 443908

commit v12 on v10

--- a/solution.py
+++ b/solution.py
@@ -111,7 +111,7 @@
             return acc_re, acc_im
 
         zero = jnp.zeros((CHUNK, LANE), jnp.float32)
-        acc_re, acc_im = lax.fori_loop(0, steps, step, (zero, zero))
+        acc_re, acc_im = lax.fori_loop(0, steps, step, (zero, zero), unroll=2)
         o_ref[0, part * CHUNK : (part + 1) * CHUNK, :] = acc_re
         o_ref[1, part * CHUNK : (part + 1) * CHUNK, :] = acc_im
 

time: 88.7 us -> 88.4 us (level)
  no operation moved by 1% of the time
where the time goes in v12:
time: 88.4 us; the launch traced here: 87.9 us
  blocking collectives  30 us (34%)
  starting transfers between devices  15.7 us (18%)
  matrix products  14.3 us (16%)
  local copies, waits for them, and re-layouts  13.9 us (16%)
  Pallas kernels  6.61 us (7%)
  waiting for transfers between devices  4.17 us (5%)
  other arithmetic  2.85 us (3%)
    all_to_all x1, blocking collectives, per_device(): lax.all_to_all(stokes, everyone, split_axis=0, concat_axis=0, tiled=True)  18.7 us
    all_to_all x1, blocking collectives, per_device(): lax.all_to_all(grid_rows.reshape(mine, L), 'freq', split_axis=1, concat_a...  11.3 us
    dot_general x1, matrix products, per_device(): jnp.einsum('ocn,onq->ocq', coef, legendre, preferred_element_type=jnp.flo...  8.94 us
    all_to_all x1, starting transfers between devices, per_device(): lax.all_to_all(gravity, 'freq', split_axis=0, concat_axis=1, tiled=True)  7.89 us
    all_to_all x1, starting transfers between devices, per_device(): lax.all_to_all(payload, everyone, split_axis=0, concat_axis=0, tiled=True)  7.8 us
    pallas_call x1, Pallas kernels, toeplitz_stokes(): pl.pallas_call(stokes_body, out_shape=jax.ShapeDtypeStruct((2, total, LAN...  6.61 us
    unnamed x23, local copies, waits for them, and re-layouts  2.9 us
    all_to_all x1, waiting for transfers between devices, per_device(): lax.all_to_all(gravity, 'freq', split_axis=0, concat_axis=1, tiled=True)  2.69 us
  transfers between devices with their start and end apart: 2, of which 2 were waited for; matrix products, arithmetic and copies ran while one was open for 16% of the time, Pallas kernels for 0%

profile of v12, /device:TPU:0, one launch (start us, length us, event | category | flops | bytes accessed | tf_op | source)
XLA Modules:
  0.0 87.9 jit_solution(6720495271063109533)
XLA Ops:
  0.0 1.7 %all_to_all.32 = f32[8,2,2700]{2,1,0:T(2,128)} reshape(f32[16,2700]{1,0:T(8,128)} %param.14) | data formatting | bytes 345600 | tf_op jit(solution)/shard_map/all_to_all | solution.py:156
  1.7 7.9 %all-to-all-start = ((f32[8,2,2700]{2,1,0:T(2,128)}), f32[8,2,2700]{2,1,0:T(2,128)S(1)}, u32[]{:S(2)}, u32[]{:S(2)}) async-start(f32[8,2,2700]{2,1,0:T(2,128)} %all_to_all.32), calls=%async_computation | async-start | bytes 360448 | tf_op jit(solution)/shard_map/all_to_all | solution.py:156
  9.6 0.9 %reshape.124 = s32[16,8,17]{2,1,0:T(8,128)S(1)} reshape(s32[2176]{0:T(1024)} %param.17) | data formatting | bytes 17408 | tf_op jit(solution)/shard_map/reshape | solution.py:151
  10.6 0.1 reshape.125
  10.6 0.0 copy-start.1
  10.7 0.1 fusion.19
  10.8 0.1 compare_and_fusion
  10.9 1.9 %copy.71 = bf16[511,1350]{1,0:T(8,128)(2,1)S(1)} copy(bf16[511,1350]{0,1:T(8,128)(2,1)} %param.19) | data formatting | bytes 2759400 | tf_op args[5]
  12.8 0.6 gather_fusion
  13.4 0.0 copy-start.10
  13.4 0.1 copy.70
  13.6 0.0 copy-start.5
  13.6 0.2 pad_dynamic-slice_fusion
  13.8 0.0 copy-start.9
  13.8 0.1 pad_maximum_fusion.2
  13.9 0.2 copy-done.10
  14.1 0.1 multiply_cosine_fusion
  14.2 0.4 rev.3
  14.6 0.7 pad_convert_fusion.k_ref
  15.3 2.7 %all-to-all-done = f32[8,2,2700]{2,1,0:T(2,128)S(1)} async-done(((f32[8,2,2700]{2,1,0:T(2,128)}), f32[8,2,2700]{2,1,0:T(2,128)S(1)}, u32[]{:S(2)}, u32[]{:S(2)}) %all-to-all-start) | async-done | bytes 172832 | tf_op jit(solution)/shard_map/all_to_all | solution.py:156
  18.0 0.0 copy-start.4
  18.0 0.1 reshape.126
  18.2 0.6 convolution_bitcast_fusion
  18.8 0.2 multiply_add_fusion
  19.0 0.8 convolution_multiply_fusion
  19.8 0.2 mul.109
  20.0 0.5 copy.75
  20.6 0.5 reshape.128
  21.1 0.1 slice.53
  21.2 1.0 %fusion.3 = f32[8,2,2,272]{3,2,1,0:T(2,128)S(1)} fusion(s32[8,272]{1,0:T(8,128)S(1)} %add_select_fusion, f32[8,2,2,272]{3,0,2,1:T(8,128)S(1)} %slice.52), kind=kOutput, calls=%fused_computation.4 | convolution fusion | flops 14796800 | bytes 78336 | tf_op jit(solution)/shard_map/brct,bts->brcs/dot_general | solution.py:158
  22.1 0.2 reshape.129
  22.4 0.2 reshape.130
  22.6 0.1 broadcast_in_dim.11
  22.7 0.2 maximum_bitcast_fusion
  22.9 0.9 %copy.78 = f32[16,8,2,2,86]{4,2,3,1,0:T(2,128)} copy(f32[16,8,2,2,86]{4,0,1,3,2:T(8,128)S(1)} %maximum_bitcast_fusion) | data formatting | bytes 352256 | tf_op jit(solution)/shard_map/transpose | solution.py:165
  23.8 7.8 %all-to-all-start.1 = ((f32[128,2,2,86]{3,1,2,0:T(2,128)}), f32[128,2,2,86]{3,1,2,0:T(2,128)S(1)}, u32[]{:S(2)}, u32[]{:S(2)}) async-start(f32[128,2,2,86]{3,1,2,0:T(2,128)} %bitcast.15), calls=%async_computation.1 | async-start | bytes 524288 | tf_op jit(solution)/shard_map/all_to_all | solution.py:168
  31.6 8.9 %convolution_convert_fusion = bf16[17,2,256]{2,1,0:T(2,128)(2,1)S(1)} fusion(bf16[17,2,2176]{2,1,0:T(2,128)(2,1)S(1)} %copy-done, bf16[17,2176,256]{2,1,0:T(8,128)(2,1)} %param.16), kind=kOutput, calls=%fused_computation.13 | convolution fusion | flops 37888512 | bytes 19105280 | tf_op jit(solution)/shard_map/ocn,onq->ocq/dot_general | solution.py:173
  40.5 0.2 copy.80
  40.7 1.5 %all-to-all-done.1 = f32[128,2,2,86]{3,1,2,0:T(2,128)S(1)} async-done(((f32[128,2,2,86]{3,1,2,0:T(2,128)}), f32[128,2,2,86]{3,1,2,0:T(2,128)S(1)}, u32[]{:S(2)}, u32[]{:S(2)}) %all-to-all-start.1) | async-done | bytes 176160 | tf_op jit(solution)/shard_map/all_to_all | solution.py:168
  42.2 0.1 copy.79
  42.3 0.2 slice_reduce_fusion
  42.5 0.1 fusion.15
  42.6 0.7 pad_convert_fusion.1.w_ref
  43.3 6.6 %shard_map.136 = f32[2,256,128]{2,1,0:T(8,128)} custom-call(f32[520,128]{1,0:T(8,128)} %pad_convert_fusion.k_ref, f32[2,256,128]{2,1,0:T(8,128)} %pad_convert_fusion.1.w_ref), custom_call_target="tpu_custom_call" | custom-call | tf_op jit(solution)/shard_map/pallas_call | solution.py:127
  49.9 1.0 %copy.104 = f32[2,128,2,85]{3,2,0,1:T(2,128)S(1)} copy(f32[2,128,2,85]{3,2,1,0:T(2,128)} %bitcast.89) | data formatting | bytes 348160 | tf_op jit(solution)/shard_map/reshape | solution.py:185
  51.0 18.7 %all_to_all.45 = f32[128,2,2,85]{3,1,2,0:T(2,128)S(1)} all-to-all(f32[128,2,2,85]{3,1,2,0:T(2,128)S(1)} %bitcast.90), channel_id=1, replica_groups=mesh['lat'=16,'freq'=8] {'lat','freq'}, dimensions={0} | all-to-all | bytes 348160 | tf_op jit(solution)/shard_map/all_to_all | solution.py:186
  69.7 0.2 copy.103
  69.8 0.1 slice.58
  70.0 0.3 reshape.136
  70.2 0.0 copy-start.3
  70.2 0.2 reshape.135
  70.4 1.2 %fusion.1 = f32[8,2,2,272]{3,2,1,0:T(2,128)S(1)} fusion(f32[8,2,2,272]{3,2,1,0:T(2,128)S(1)} %reshape.135, s32[8,272]{1,0:T(8,128)S(1)} %add_select_fusion), kind=kOutput, calls=%fused_computation.3 | convolution fusion | flops 14796800 | bytes 78336 | tf_op jit(solution)/shard_map/brcs,bts->brct/dot_general | solution.py:189
  71.7 0.2 pad_maximum_fusion.1
  71.9 0.0 copy-start.7
  71.9 0.8 reshape.137
  72.7 1.2 %fusion.21 = f32[8,2,18,300]{3,2,1,0:T(8,128)S(1)} fusion(f32[8,2,150,18]{3,2,1,0:T(8,128)S(1)} %reshape.137, f32[150,300,1,1]{1,0,3,2:T(8,128)S(1)} %copy-done.3), kind=kOutput, calls=%fused_computation.52 | convolution fusion | flops 77760000 | bytes 698400 | tf_op jit(solution)/shard_map/brms,mn->brsn/dot_general | solution.py:70
  74.0 0.0 copy-start.2
  74.0 0.2 subtract_bitcast_fusion
  74.2 0.7 copy-done.2
  75.0 0.6 fusion.8
  75.6 0.1 all_to_all.37
  75.7 0.1 copy.85
  75.8 11.3 %all_to_all.46 = f32[2,8,2700]{2,0,1:T(2,128)S(1)} all-to-all(f32[2,8,2700]{2,0,1:T(2,128)S(1)} %copy.85), channel_id=1, replica_groups=mesh['lat'=16,'freq'=8] {'freq'}, dimensions={1} | all-to-all | bytes 345600 | tf_op jit(solution)/shard_map/all_to_all | solution.py:193
  87.1 0.8 all_to_all.40
  (20 shorter events, 0.1 us)
Async XLA Ops:
  0.0 31.6 %copy-start = (bf16[17,2,2176]{2,1,0:T(2,128)(2,1)S(1)}, bf16[17,2,2176]{2,1,0:T(2,128)(2,1)}, u32[]{:S(2)}) copy-start(bf16[17,2,2176]{2,1,0:T(2,128)(2,1)} %param.15) | copy-start | bytes 443908
  1.7 16.2 %all-to-all-start = ((f32[8,2,2700]{2,1,0:T(2,128)}), f32[8,2,2700]{2,1,0:T(2,128)S(1)}, u32[]{:S(2)}, u32[]{:S(2)}) async-start(f32[8,2,2700]{2,1,0:T(2,128)} %all_to_all.32), calls=%async_computation | async-start | bytes 360448 | tf_op jit(solution)/shard_map/all_to_all | solution.py:156
  10.6 2.1 %copy-start.1 = (bf16[511,1350]{0,1:T(8,128)(2,1)S(1)}, bf16[511,1350]{0,1:T(8,128)(2,1)}, u32[]{:S(2)}) copy-start(bf16[511,1350]{0,1:T(8,128)(2,1)} %param.19) | copy-start | bytes 4139104
  13.4 0.7 copy-start.10
  13.6 4.6 %copy-start.5 = (f32[144,288,1]{1,0,2:T(8,128)S(1)}, f32[144,288,1]{1,0,2:T(8,128)}, u32[]{:S(2)}) copy-start(f32[144,288,1]{1,0,2:T(8,128)} %constant.120) | copy-start | bytes 497668
  13.7 5.0 %copy-start.8 = (f32[150,144]{1,0:T(8,128)S(1)}, f32[150,144]{1,0:T(8,128)}, u32[]{:S(2)}) copy-start(f32[150,144]{1,0:T(8,128)} %constant.100.clone) | copy-start | bytes 259204
  13.8 5.0 %copy-start.9 = (f32[150,144]{1,0:T(8,128)S(1)}, f32[150,144]{1,0:T(8,128)}, u32[]{:S(2)}) copy-start(f32[150,144]{1,0:T(8,128)} %constant.99.clone) | copy-start | bytes 259204
  18.0 1.0 %copy-start.4 = (f32[300,150,1]{0,1,2:T(8,128)S(1)}, f32[300,150,1]{0,1,2:T(8,128)}, u32[]{:S(2)}) copy-start(f32[300,150,1]{0,1,2:T(8,128)} %constant.121) | copy-start | bytes 540004
  23.8 18.4 %all-to-all-start.1 = ((f32[128,2,2,86]{3,1,2,0:T(2,128)}), f32[128,2,2,86]{3,1,2,0:T(2,128)S(1)}, u32[]{:S(2)}, u32[]{:S(2)}) async-start(f32[128,2,2,86]{3,1,2,0:T(2,128)} %bitcast.15), calls=%async_computation.1 | async-start | bytes 524288 | tf_op jit(solution)/shard_map/all_to_all | solution.py:168
  70.2 2.5 %copy-start.3 = (f32[150,300,1,1]{1,0,3,2:T(8,128)S(1)}, f32[150,300,1,1]{1,0,3,2:T(8,128)}, u32[]{:S(2)}) copy-start(f32[150,300,1,1]{1,0,3,2:T(8,128)} %constant.122) | copy-start | bytes 540004
  71.9 2.1 %copy-start.6 = (f32[8,18,150]{2,1,0:T(8,128)S(1)}, f32[8,18,150]{2,1,0:T(8,128)}, u32[]{:S(2)}) copy-start(f32[8,18,150]{2,1,0:T(8,128)} %constant.103.clone) | copy-start | bytes 259204
  71.9 2.1 %copy-start.7 = (f32[8,18,150]{2,1,0:T(8,128)S(1)}, f32[8,18,150]{2,1,0:T(8,128)}, u32[]{:S(2)}) copy-start(f32[8,18,150]{2,1,0:T(8,128)} %constant.104.clone) | copy-start | bytes 259204
  74.0 1.0 %copy-start.2 = (f32[2,8,18,144,1]{3,2,4,0,1:T(8,128)S(1)}, f32[2,8,18,144,1]{3,2,4,0,1:T(8,128)}, u32[]{:S(2)}) copy-start(f32[2,8,18,144,1]{3,2,4,0,1:T(8,128)} %constant.123) | copy-start | bytes 497668

commit v13 on v10

--- a/solution.py
+++ b/solution.py
@@ -130,6 +130,16 @@
         scratch_shapes=[pltpu.VMEM((SHIFTS, span, LANE), jnp.float32)],
     )(flipped, source)
     return out[:, :, :width]
+
+
+def exchanged(chunks, own, count):
+    arrived = [chunks[own]]
+    for shift in range(1, count):
+        piece = lax.dynamic_index_in_dim(chunks, (own + shift) % count, 0, keepdims=False)
+        route = [(i, (i + shift) % count) for i in range(count)]
+        arrived.append(lax.ppermute(piece, "freq", route))
+    by_shift = jnp.stack([arrived[(-j) % count] for j in range(count)])
+    return jnp.roll(by_shift, own, axis=0)
 
 
 def per_device(gravity, coef, legendre, order_table, band_rows, kernel):
@@ -190,7 +200,8 @@
     rest_back = by_source[..., per_slot:].reshape(bands, mine, 2, blocks * share)
     by_band = jnp.concatenate([slots_back, rest_back], axis=3)[..., :band_width]
     grid_rows = inverse_rows(by_band, bands)
-    geoid = lax.all_to_all(grid_rows.reshape(mine, L), "freq", split_axis=1, concat_axis=0, tiled=True)
+    geoid = exchanged(grid_rows.reshape(mine, bands, L // bands).transpose(1, 0, 2), band_self, bands)
+    geoid = geoid.reshape(rows, L // bands)
     return geoid
 
 

time: 88.7 us -> 98.4 us (1.11)
  blocking collectives: 30 us -> 0 us
  starting transfers between devices: 15.7 us -> 36.5 us
  waiting for transfers between devices: 4.17 us -> 21.8 us
  local copies, waits for them, and re-layouts: 13.9 us -> 14.9 us
    all_to_all x2 -> x0, blocking collectives: 30 us -> none  [the longest x1 18.7 us: per_device(): lax.all_to_all(stokes, everyone, split_axis=0, concat_axis=0, tiled=True)]
    ppermute x0 -> x7, starting transfers between devices: none -> 12.3 us  [exchanged(): arrived.append(lax.ppermute(piece, 'freq', route))]
    all_to_all x0 -> x1, waiting for transfers between devices: none -> 10.3 us  [per_device(): lax.all_to_all(stokes, everyone, split_axis=0, concat_axis=0, tiled=True)]
    all_to_all x0 -> x1, starting transfers between devices: none -> 8.48 us  [per_device(): lax.all_to_all(stokes, everyone, split_axis=0, concat_axis=0, tiled=True)]
    ppermute x0 -> x7, waiting for transfers between devices: none -> 7.33 us  [exchanged(): arrived.append(lax.ppermute(piece, 'freq', route))]
    all_to_all x3 -> x0, local copies, waits for them, and re-layouts: 1.02 us -> none  [per_device(): lax.all_to_all(grid_rows.reshape(mine, L), 'freq', split_axis=1, concat_a...]
    unnamed x23 -> x45, local copies, waits for them, and re-layouts: 2.9 us -> 3.14 us
  transfers between devices with their start and end apart: 2 -> 10, of which waited for: 2 -> 6; matrix products, arithmetic and copies ran while one was open for 16% -> 15% of each run, Pallas kernels for 0% -> 0%
where the time goes in v13:
time: 98.4 us; the launch traced here: 97.9 us
  starting transfers between devices  36.5 us (37%)
  waiting for transfers between devices  21.8 us (22%)
  local copies, waits for them, and re-layouts  14.9 us (15%)
  matrix products  14.3 us (15%)
  Pallas kernels  6.86 us (7%)
  other arithmetic  2.85 us (3%)
    ppermute x7, starting transfers between devices, exchanged(): arrived.append(lax.ppermute(piece, 'freq', route))  12.3 us
    all_to_all x1, waiting for transfers between devices, per_device(): lax.all_to_all(stokes, everyone, split_axis=0, concat_axis=0, tiled=True)  10.3 us
    dot_general x1, matrix products, per_device(): jnp.einsum('ocn,onq->ocq', coef, legendre, preferred_element_type=jnp.flo...  8.94 us
    all_to_all x1, starting transfers between devices, per_device(): lax.all_to_all(stokes, everyone, split_axis=0, concat_axis=0, tiled=True)  8.48 us
    all_to_all x1, starting transfers between devices, per_device(): lax.all_to_all(gravity, 'freq', split_axis=0, concat_axis=1, tiled=True)  7.89 us
    all_to_all x1, starting transfers between devices, per_device(): lax.all_to_all(payload, everyone, split_axis=0, concat_axis=0, tiled=True)  7.81 us
    ppermute x7, waiting for transfers between devices, exchanged(): arrived.append(lax.ppermute(piece, 'freq', route))  7.33 us
    pallas_call x1, Pallas kernels, toeplitz_stokes(): pl.pallas_call(stokes_body, out_shape=jax.ShapeDtypeStruct((2, total, LAN...  6.86 us
  transfers between devices with their start and end apart: 10, of which 6 were waited for; matrix products, arithmetic and copies ran while one was open for 15% of the time, Pallas kernels for 0%

profile of v13, /device:TPU:0, one launch (start us, length us, event | category | flops | bytes accessed | tf_op | source)
XLA Modules:
  0.0 97.9 jit_solution(13718877747319287233)
XLA Ops:
  0.0 1.7 %all_to_all.18 = f32[8,2,2700]{2,1,0:T(2,128)} reshape(f32[16,2700]{1,0:T(8,128)} %param.14) | data formatting | bytes 345600 | tf_op jit(solution)/shard_map/all_to_all | solution.py:166
  1.7 7.9 %all-to-all-start = ((f32[8,2,2700]{2,1,0:T(2,128)}), f32[8,2,2700]{2,1,0:T(2,128)S(1)}, u32[]{:S(2)}, u32[]{:S(2)}) async-start(f32[8,2,2700]{2,1,0:T(2,128)} %all_to_all.18), calls=%async_computation | async-start | bytes 360448 | tf_op jit(solution)/shard_map/all_to_all | solution.py:166
  9.6 0.9 reshape.140
  10.6 0.1 reshape.141
  10.7 0.1 fusion.19
  10.9 1.9 %copy.67 = bf16[511,1350]{1,0:T(8,128)(2,1)S(1)} copy(bf16[511,1350]{0,1:T(8,128)(2,1)} %param.19) | data formatting | bytes 2759400 | tf_op args[5]
  12.8 0.6 gather_fusion
  13.4 0.1 copy.66
  13.6 0.2 pad_dynamic-slice_fusion
  13.8 0.1 pad_maximum_fusion.2
  13.9 0.2 copy-done.10
  14.1 0.1 multiply_cosine_fusion
  14.2 0.4 rev.3
  14.6 0.7 pad_convert_fusion.k_ref
  15.3 2.7 %all-to-all-done = f32[8,2,2700]{2,1,0:T(2,128)S(1)} async-done(((f32[8,2,2700]{2,1,0:T(2,128)}), f32[8,2,2700]{2,1,0:T(2,128)S(1)}, u32[]{:S(2)}, u32[]{:S(2)}) %all-to-all-start) | async-done | bytes 172832 | tf_op jit(solution)/shard_map/all_to_all | solution.py:166
  18.0 0.1 reshape.142
  18.2 0.6 convolution_bitcast_fusion
  18.8 0.2 multiply_add_fusion
  19.0 0.8 convolution_multiply_fusion
  19.8 0.2 mul.109
  20.0 0.5 copy.71
  20.6 0.5 reshape.144
  21.1 0.1 slice.53
  21.2 1.0 fusion.3
  22.1 0.2 reshape.145
  22.4 0.2 reshape.146
  22.6 0.1 broadcast_in_dim.11
  22.7 0.2 maximum_bitcast_fusion
  22.9 0.9 copy.74
  23.8 7.8 %all-to-all-start.1 = ((f32[128,2,2,86]{3,1,2,0:T(2,128)}), f32[128,2,2,86]{3,1,2,0:T(2,128)S(1)}, u32[]{:S(2)}, u32[]{:S(2)}) async-start(f32[128,2,2,86]{3,1,2,0:T(2,128)} %bitcast.15), calls=%async_computation.1 | async-start | bytes 524288 | tf_op jit(solution)/shard_map/all_to_all | solution.py:178
  31.6 8.9 %convolution_convert_fusion = bf16[17,2,256]{2,1,0:T(2,128)(2,1)S(1)} fusion(bf16[17,2,2176]{2,1,0:T(2,128)(2,1)S(1)} %copy-done, bf16[17,2176,256]{2,1,0:T(8,128)(2,1)} %param.16), kind=kOutput, calls=%fused_computation.13 | convolution fusion | flops 37888512 | bytes 19105280 | tf_op jit(solution)/shard_map/ocn,onq->ocq/dot_general | solution.py:183
  40.6 0.2 copy.76
  40.7 1.5 %all-to-all-done.1 = f32[128,2,2,86]{3,1,2,0:T(2,128)S(1)} async-done(((f32[128,2,2,86]{3,1,2,0:T(2,128)}), f32[128,2,2,86]{3,1,2,0:T(2,128)S(1)}, u32[]{:S(2)}, u32[]{:S(2)}) %all-to-all-start.1) | async-done | bytes 176160 | tf_op jit(solution)/shard_map/all_to_all | solution.py:178
  42.2 0.1 copy.75
  42.3 0.2 slice_reduce_fusion
  42.5 0.1 fusion.15
  42.6 0.7 pad_convert_fusion.1.w_ref
  43.3 6.9 %shard_map.136 = f32[2,256,128]{2,1,0:T(8,128)} custom-call(f32[520,128]{1,0:T(8,128)} %pad_convert_fusion.k_ref, f32[2,256,128]{2,1,0:T(8,128)} %pad_convert_fusion.1.w_ref), custom_call_target="tpu_custom_call" | custom-call | tf_op jit(solution)/shard_map/pallas_call | solution.py:127
  50.2 1.8 %copy.116 = f32[2,128,2,85]{3,2,0,1:T(2,128)} copy(f32[2,128,2,85]{3,2,1,0:T(2,128)} %bitcast.133) | data formatting | bytes 348160 | tf_op jit(solution)/shard_map/reshape | solution.py:195
  51.9 8.5 %all-to-all-start.2 = ((f32[128,2,2,85]{3,1,2,0:T(2,128)}), f32[128,2,2,85]{3,1,2,0:T(2,128)S(1)}, u32[]{:S(2)}, u32[]{:S(2)}) async-start(f32[128,2,2,85]{3,1,2,0:T(2,128)} %bitcast.118), calls=%async_computation.2 | async-start | bytes 524288 | tf_op jit(solution)/shard_map/all_to_all | solution.py:196
  60.5 10.3 %all-to-all-done.2 = f32[128,2,2,85]{3,1,2,0:T(2,128)S(1)} async-done(((f32[128,2,2,85]{3,1,2,0:T(2,128)}), f32[128,2,2,85]{3,1,2,0:T(2,128)S(1)}, u32[]{:S(2)}, u32[]{:S(2)}) %all-to-all-start.2) | async-done | bytes 174112 | tf_op jit(solution)/shard_map/all_to_all | solution.py:196
  70.8 0.2 copy.115
  71.0 0.1 slice.58
  71.1 0.3 reshape.152
  71.4 0.2 reshape.151
  71.6 1.2 %fusion.1 = f32[8,2,2,272]{3,2,1,0:T(2,128)S(1)} fusion(f32[8,2,2,272]{3,2,1,0:T(2,128)S(1)} %reshape.151, s32[8,272]{1,0:T(8,128)S(1)} %add_select_fusion), kind=kOutput, calls=%fused_computation.3 | convolution fusion | flops 14796800 | bytes 78336 | tf_op jit(solution)/shard_map/brcs,bts->brct/dot_general | solution.py:199
  72.8 0.2 pad_maximum_fusion.1
  73.1 0.8 reshape.153
  73.9 1.2 %fusion.21 = f32[8,2,18,300]{3,2,1,0:T(8,128)S(1)} fusion(f32[8,2,150,18]{3,2,1,0:T(8,128)S(1)} %reshape.153, f32[150,300,1,1]{1,0,3,2:T(8,128)S(1)} %copy-done.3), kind=kOutput, calls=%fused_computation.84 | convolution fusion | flops 77760000 | bytes 698400 | tf_op jit(solution)/shard_map/brms,mn->brsn/dot_general | solution.py:70
  75.2 0.2 subtract_bitcast_fusion
  75.4 0.7 copy-done.2
  76.1 0.6 fusion.8
  76.7 0.1 reshape.154
  76.9 0.1 constant_dynamic-slice_fusion.1
  77.0 1.1 %collective-permute-start = (f32[2,2700]{1,0:T(2,128)S(1)}, f32[2,2700]{1,0:T(2,128)S(1)}, u32[]{:S(2)}, u32[]{:S(2)}) collective-permute-start(f32[2,2700]{1,0:T(2,128)S(1)} %bitcast.144), channel_id=1, source_target_pairs={{0,7},{1,0},{2,1},{3,2},{4,3},{5,4},{6,5},{7,6},{8,15},{9,8},{10,9... | collective-permute-start | bytes 64808 | tf_op jit(solution)/shard_map/ppermute | solution.py:140
  78.2 2.2 %collective-permute-start.1 = (f32[2,2700]{1,0:T(2,128)S(1)}, f32[2,2700]{1,0:T(2,128)S(1)}, u32[]{:S(2)}, u32[]{:S(2)}) collective-permute-start(f32[2,2700]{1,0:T(2,128)S(1)} %bitcast.143), channel_id=1, source_target_pairs={{0,6},{1,7},{2,0},{3,1},{4,2},{5,3},{6,4},{7,5},{8,14},{9,15},{10,... | collective-permute-start | bytes 64808 | tf_op jit(solution)/shard_map/ppermute | solution.py:140
  80.4 2.1 %collective-permute-start.2 = (f32[2,2700]{1,0:T(2,128)S(1)}, f32[2,2700]{1,0:T(2,128)S(1)}, u32[]{:S(2)}, u32[]{:S(2)}) collective-permute-start(f32[2,2700]{1,0:T(2,128)S(1)} %bitcast.139), channel_id=1, source_target_pairs={{0,5},{1,6},{2,7},{3,0},{4,1},{5,2},{6,3},{7,4},{8,13},{9,14},{10,... | collective-permute-start | bytes 64808 | tf_op jit(solution)/shard_map/ppermute | solution.py:140
  82.6 1.0 %collective-permute-start.3 = (f32[2,2700]{1,0:T(2,128)S(1)}, f32[2,2700]{1,0:T(2,128)S(1)}, u32[]{:S(2)}, u32[]{:S(2)}) collective-permute-start(f32[2,2700]{1,0:T(2,128)S(1)} %bitcast.140), channel_id=1, source_target_pairs={{0,4},{1,5},{2,6},{3,7},{4,0},{5,1},{6,2},{7,3},{8,12},{9,13},{10,... | collective-permute-start | bytes 64808 | tf_op jit(solution)/shard_map/ppermute | solution.py:140
  83.6 2.8 %collective-permute-start.4 = (f32[2,2700]{1,0:T(2,128)S(1)}, f32[2,2700]{1,0:T(2,128)S(1)}, u32[]{:S(2)}, u32[]{:S(2)}) collective-permute-start(f32[2,2700]{1,0:T(2,128)S(1)} %bitcast.141), channel_id=1, source_target_pairs={{0,3},{1,4},{2,5},{3,6},{4,7},{5,0},{6,1},{7,2},{8,11},{9,12},{10,... | collective-permute-start | bytes 64808 | tf_op jit(solution)/shard_map/ppermute | solution.py:140
  86.5 2.9 %collective-permute-start.5 = (f32[2,2700]{1,0:T(2,128)S(1)}, f32[2,2700]{1,0:T(2,128)S(1)}, u32[]{:S(2)}, u32[]{:S(2)}) collective-permute-start(f32[2,2700]{1,0:T(2,128)S(1)} %bitcast.142), channel_id=1, source_target_pairs={{0,2},{1,3},{2,4},{3,5},{4,6},{5,7},{6,0},{7,1},{8,10},{9,11},{10,... | collective-permute-start | bytes 64808 | tf_op jit(solution)/shard_map/ppermute | solution.py:140
  89.6 0.3 collective-permute-done.4
  89.9 4.5 %collective-permute-done.5 = f32[2,2700]{1,0:T(2,128)S(1)} collective-permute-done((f32[2,2700]{1,0:T(2,128)S(1)}, f32[2,2700]{1,0:T(2,128)S(1)}, u32[]{:S(2)}, u32[]{:S(2)}) %collective-permute-start.5) | collective-permute-done | bytes 21632 | tf_op jit(solution)/shard_map/ppermute | solution.py:140
  94.4 2.5 %collective-permute-done.6 = f32[2,2700]{1,0:T(2,128)S(1)} collective-permute-done((f32[2,2700]{1,0:T(2,128)S(1)}, f32[2,2700]{1,0:T(2,128)S(1)}, u32[]{:S(2)}, u32[]{:S(2)}) %collective-permute-start.6) | collective-permute-done | bytes 21632 | tf_op jit(solution)/shard_map/ppermute | solution.py:140
  97.1 0.8 reshape.155
  (58 shorter events, 0.6 us)
Async XLA Ops:
  0.0 31.6 %copy-start = (bf16[17,2,2176]{2,1,0:T(2,128)(2,1)S(1)}, bf16[17,2,2176]{2,1,0:T(2,128)(2,1)}, u32[]{:S(2)}) copy-start(bf16[17,2,2176]{2,1,0:T(2,128)(2,1)} %param.15) | copy-start | bytes 443908
  1.7 16.2 %all-to-all-start = ((f32[8,2,2700]{2,1,0:T(2,128)}), f32[8,2,2700]{2,1,0:T(2,128)S(1)}, u32[]{:S(2)}, u32[]{:S(2)}) async-start(f32[8,2,2700]{2,1,0:T(2,128)} %all_to_all.18), calls=%async_computation | async-start | bytes 360448 | tf_op jit(solution)/shard_map/all_to_all | solution.py:166
  10.6 2.1 %copy-start.1 = (bf16[511,1350]{0,1:T(8,128)(2,1)S(1)}, bf16[511,1350]{0,1:T(8,128)(2,1)}, u32[]{:S(2)}) copy-start(bf16[511,1350]{0,1:T(8,128)(2,1)} %param.19) | copy-start | bytes 4139104
  13.4 0.7 copy-start.10
  13.6 4.6 %copy-start.5 = (f32[144,288,1]{1,0,2:T(8,128)S(1)}, f32[144,288,1]{1,0,2:T(8,128)}, u32[]{:S(2)}) copy-start(f32[144,288,1]{1,0,2:T(8,128)} %constant.194) | copy-start | bytes 497668
  13.7 5.0 %copy-start.8 = (f32[150,144]{1,0:T(8,128)S(1)}, f32[150,144]{1,0:T(8,128)}, u32[]{:S(2)}) copy-start(f32[150,144]{1,0:T(8,128)} %constant.173.clone) | copy-start | bytes 259204
  13.8 5.0 %copy-start.9 = (f32[150,144]{1,0:T(8,128)S(1)}, f32[150,144]{1,0:T(8,128)}, u32[]{:S(2)}) copy-start(f32[150,144]{1,0:T(8,128)} %constant.174.clone) | copy-start | bytes 259204
  18.0 1.0 %copy-start.4 = (f32[300,150,1]{0,1,2:T(8,128)S(1)}, f32[300,150,1]{0,1,2:T(8,128)}, u32[]{:S(2)}) copy-start(f32[300,150,1]{0,1,2:T(8,128)} %constant.195) | copy-start | bytes 540004
  23.8 18.4 %all-to-all-start.1 = ((f32[128,2,2,86]{3,1,2,0:T(2,128)}), f32[128,2,2,86]{3,1,2,0:T(2,128)S(1)}, u32[]{:S(2)}, u32[]{:S(2)}) async-start(f32[128,2,2,86]{3,1,2,0:T(2,128)} %bitcast.15), calls=%async_computation.1 | async-start | bytes 524288 | tf_op jit(solution)/shard_map/all_to_all | solution.py:178
  51.9 18.9 %all-to-all-start.2 = ((f32[128,2,2,85]{3,1,2,0:T(2,128)}), f32[128,2,2,85]{3,1,2,0:T(2,128)S(1)}, u32[]{:S(2)}, u32[]{:S(2)}) async-start(f32[128,2,2,85]{3,1,2,0:T(2,128)} %bitcast.118), calls=%async_computation.2 | async-start | bytes 524288 | tf_op jit(solution)/shard_map/all_to_all | solution.py:196
  71.4 2.5 %copy-start.3 = (f32[150,300,1,1]{1,0,3,2:T(8,128)S(1)}, f32[150,300,1,1]{1,0,3,2:T(8,128)}, u32[]{:S(2)}) copy-start(f32[150,300,1,1]{1,0,3,2:T(8,128)} %constant.196) | copy-start | bytes 540004
  73.1 2.1 %copy-start.6 = (f32[8,18,150]{2,1,0:T(8,128)S(1)}, f32[8,18,150]{2,1,0:T(8,128)}, u32[]{:S(2)}) copy-start(f32[8,18,150]{2,1,0:T(8,128)} %constant.177.clone) | copy-start | bytes 259204
  73.1 2.1 %copy-start.7 = (f32[8,18,150]{2,1,0:T(8,128)S(1)}, f32[8,18,150]{2,1,0:T(8,128)}, u32[]{:S(2)}) copy-start(f32[8,18,150]{2,1,0:T(8,128)} %constant.178.clone) | copy-start | bytes 259204
  75.1 1.0 %copy-start.2 = (f32[2,8,18,144,1]{3,2,4,0,1:T(8,128)S(1)}, f32[2,8,18,144,1]{3,2,4,0,1:T(8,128)}, u32[]{:S(2)}) copy-start(f32[2,8,18,144,1]{3,2,4,0,1:T(8,128)} %constant.197) | copy-start | bytes 497668
  77.0 9.4 %collective-permute-start = (f32[2,2700]{1,0:T(2,128)S(1)}, f32[2,2700]{1,0:T(2,128)S(1)}, u32[]{:S(2)}, u32[]{:S(2)}) collective-permute-start(f32[2,2700]{1,0:T(2,128)S(1)} %bitcast.144), channel_id=1, source_target_pairs={{0,7},{1,0},{2,1},{3,2},{4,3},{5,4},{6,5},{7,6},{8,15},{9,8},{10,9... | collective-permute-start | bytes 64808 | tf_op jit(solution)/shard_map/ppermute | solution.py:140
  78.2 11.2 %collective-permute-start.1 = (f32[2,2700]{1,0:T(2,128)S(1)}, f32[2,2700]{1,0:T(2,128)S(1)}, u32[]{:S(2)}, u32[]{:S(2)}) collective-permute-start(f32[2,2700]{1,0:T(2,128)S(1)} %bitcast.143), channel_id=1, source_target_pairs={{0,6},{1,7},{2,0},{3,1},{4,2},{5,3},{6,4},{7,5},{8,14},{9,15},{10,... | collective-permute-start | bytes 64808 | tf_op jit(solution)/shard_map/ppermute | solution.py:140
  80.4 9.1 %collective-permute-start.2 = (f32[2,2700]{1,0:T(2,128)S(1)}, f32[2,2700]{1,0:T(2,128)S(1)}, u32[]{:S(2)}, u32[]{:S(2)}) collective-permute-start(f32[2,2700]{1,0:T(2,128)S(1)} %bitcast.139), channel_id=1, source_target_pairs={{0,5},{1,6},{2,7},{3,0},{4,1},{5,2},{6,3},{7,4},{8,13},{9,14},{10,... | collective-permute-start | bytes 64808 | tf_op jit(solution)/shard_map/ppermute | solution.py:140
  82.6 7.0 %collective-permute-start.3 = (f32[2,2700]{1,0:T(2,128)S(1)}, f32[2,2700]{1,0:T(2,128)S(1)}, u32[]{:S(2)}, u32[]{:S(2)}) collective-permute-start(f32[2,2700]{1,0:T(2,128)S(1)} %bitcast.140), channel_id=1, source_target_pairs={{0,4},{1,5},{2,6},{3,7},{4,0},{5,1},{6,2},{7,3},{8,12},{9,13},{10,... | collective-permute-start | bytes 64808 | tf_op jit(solution)/shard_map/ppermute | solution.py:140
  83.6 6.3 %collective-permute-start.4 = (f32[2,2700]{1,0:T(2,128)S(1)}, f32[2,2700]{1,0:T(2,128)S(1)}, u32[]{:S(2)}, u32[]{:S(2)}) collective-permute-start(f32[2,2700]{1,0:T(2,128)S(1)} %bitcast.141), channel_id=1, source_target_pairs={{0,3},{1,4},{2,5},{3,6},{4,7},{5,0},{6,1},{7,2},{8,11},{9,12},{10,... | collective-permute-start | bytes 64808 | tf_op jit(solution)/shard_map/ppermute | solution.py:140
  86.5 7.9 %collective-permute-start.5 = (f32[2,2700]{1,0:T(2,128)S(1)}, f32[2,2700]{1,0:T(2,128)S(1)}, u32[]{:S(2)}, u32[]{:S(2)}) collective-permute-start(f32[2,2700]{1,0:T(2,128)S(1)} %bitcast.142), channel_id=1, source_target_pairs={{0,2},{1,3},{2,4},{3,5},{4,6},{5,7},{6,0},{7,1},{8,10},{9,11},{10,... | collective-permute-start | bytes 64808 | tf_op jit(solution)/shard_map/ppermute | solution.py:140
  89.4 7.5 %collective-permute-start.6 = (f32[2,2700]{1,0:T(2,128)S(1)}, f32[2,2700]{1,0:T(2,128)S(1)}, u32[]{:S(2)}, u32[]{:S(2)}) collective-permute-start(f32[2,2700]{1,0:T(2,128)S(1)} %bitcast.138), channel_id=1, source_target_pairs={{0,1},{1,2},{2,3},{3,4},{4,5},{5,6},{6,7},{7,0},{8,9},{9,10},{10,1... | collective-permute-start | bytes 64808 | tf_op jit(solution)/shard_map/ppermute | solution.py:140

commit v14 on v10

--- a/solution.py
+++ b/solution.py
@@ -90,12 +90,9 @@
 CHUNK = 64
 
 
-def stokes_body(k_ref, w_ref, o_ref, sh_ref):
-    span = sh_ref.shape[1]
+def stokes_body(sh_ref, w_ref, o_ref):
     total = w_ref.shape[1]
     steps = total // SHIFTS
-    for s in range(SHIFTS):
-        sh_ref[s] = k_ref[pl.ds(s, span), :]
     for part in range(total // CHUNK):
 
         def step(a, carry):
@@ -124,11 +121,14 @@
         kernel_cols[::-1].astype(jnp.float32), ((0, span + SHIFTS - taps), (0, LANE - width))
     )
     source = jnp.pad(weighted.astype(jnp.float32).transpose(1, 0, 2), ((0, 0), (0, 0), (0, LANE - width)))
+    shifted = jnp.stack([flipped[s : s + span] for s in range(SHIFTS)])
+    resident = pl.BlockSpec(memory_space=pltpu.VMEM)
     out = pl.pallas_call(
         stokes_body,
+        in_specs=[resident, resident],
+        out_specs=resident,
         out_shape=jax.ShapeDtypeStruct((2, total, LANE), jnp.float32),
-        scratch_shapes=[pltpu.VMEM((SHIFTS, span, LANE), jnp.float32)],
-    )(flipped, source)
+    )(shifted, source)
     return out[:, :, :width]
 
 

time: 88.7 us -> 93.3 us (1.052)
  local copies, waits for them, and re-layouts: 13.9 us -> 18.8 us
  starting transfers between devices: 15.7 us -> 18.4 us
  waiting for transfers between devices: 4.17 us -> 1.48 us
    unnamed x23 -> x30, local copies, waits for them, and re-layouts: 2.9 us -> 6.99 us
    all_to_all x1, starting transfers between devices: 7.8 us -> 10.5 us  [per_device(): lax.all_to_all(payload, everyone, split_axis=0, concat_axis=0, tiled=True)]
    all_to_all x1, waiting for transfers between devices: 2.69 us -> 0.01 us  [per_device(): lax.all_to_all(gravity, 'freq', split_axis=0, concat_axis=1, tiled=True)]
  transfers between devices with their start and end apart: 2 -> 2, of which waited for: 2 -> 1; matrix products, arithmetic and copies ran while one was open for 16% -> 21% of each run, Pallas kernels for 0% -> 0%
where the time goes in v14:
time: 93.3 us; the launch traced here: 92.8 us
  blocking collectives  30 us (32%)
  local copies, waits for them, and re-layouts  18.8 us (20%)
  starting transfers between devices  18.4 us (20%)
  matrix products  14.3 us (15%)
  Pallas kernels  7.33 us (8%)
  other arithmetic  2.15 us (2%)
  waiting for transfers between devices  1.48 us (2%)
    all_to_all x1, blocking collectives, per_device(): lax.all_to_all(stokes, everyone, split_axis=0, concat_axis=0, tiled=True)  18.7 us
    all_to_all x1, blocking collectives, per_device(): lax.all_to_all(grid_rows.reshape(mine, L), 'freq', split_axis=1, concat_a...  11.3 us
    all_to_all x1, starting transfers between devices, per_device(): lax.all_to_all(payload, everyone, split_axis=0, concat_axis=0, tiled=True)  10.5 us
    dot_general x1, matrix products, per_device(): jnp.einsum('ocn,onq->ocq', coef, legendre, preferred_element_type=jnp.flo...  8.94 us
    all_to_all x1, starting transfers between devices, per_device(): lax.all_to_all(gravity, 'freq', split_axis=0, concat_axis=1, tiled=True)  7.89 us
    pallas_call x1, Pallas kernels, toeplitz_stokes(): pl.pallas_call(stokes_body, in_specs=[resident, resident], out_specs=resi...  7.33 us
    unnamed x30, local copies, waits for them, and re-layouts  6.99 us
  transfers between devices with their start and end apart: 2, of which 1 were waited for; matrix products, arithmetic and copies ran while one was open for 21% of the time, Pallas kernels for 0%

profile of v14, /device:TPU:0, one launch (start us, length us, event | category | flops | bytes accessed | tf_op | source)
XLA Modules:
  0.0 92.8 jit_solution(12952173083738368889)
XLA Ops:
  0.0 1.8 %all_to_all.32 = f32[8,2,2700]{2,1,0:T(2,128)} reshape(f32[16,2700]{1,0:T(8,128)} %param.14) | data formatting | bytes 345600 | tf_op jit(solution)/shard_map/all_to_all | solution.py:156
  1.8 7.9 %all-to-all-start = ((f32[8,2,2700]{2,1,0:T(2,128)}), f32[8,2,2700]{2,1,0:T(2,128)S(1)}, u32[]{:S(2)}, u32[]{:S(2)}) async-start(f32[8,2,2700]{2,1,0:T(2,128)} %all_to_all.32), calls=%async_computation | async-start | bytes 360448 | tf_op jit(solution)/shard_map/all_to_all | solution.py:156
  9.7 0.9 reshape.124
  10.6 0.1 reshape.125
  10.8 0.1 fusion.27
  10.8 0.1 compare_and_fusion
  10.9 1.8 %copy.71 = bf16[511,1350]{1,0:T(8,128)(2,1)S(1)} copy(bf16[511,1350]{0,1:T(8,128)(2,1)} %param.19) | data formatting | bytes 2759400 | tf_op args[5]
  12.8 0.6 gather_fusion
  13.3 0.1 copy.70
  13.5 0.2 pad_dynamic-slice_fusion
  13.7 0.1 pad_maximum_fusion.2
  13.8 0.4 rev.3
  14.2 0.7 fusion.22
  15.0 0.7 fusion.21
  15.7 0.7 fusion.20
  16.4 0.7 fusion.19
  17.2 0.7 fusion.18
  17.9 0.7 fusion.17
  18.6 0.7 fusion.16
  19.4 0.7 fusion.15.sh_ref
  20.1 0.1 multiply_cosine_fusion
  20.3 0.1 reshape.126
  20.4 0.6 convolution_bitcast_fusion
  21.0 0.2 multiply_add_fusion
  21.3 0.8 convolution_multiply_fusion
  22.0 0.2 mul.109
  22.3 0.5 copy.75
  22.8 0.5 reshape.128
  23.3 0.1 slice.93
  23.4 1.0 %fusion.3 = f32[8,2,2,272]{3,2,1,0:T(2,128)S(1)} fusion(s32[8,272]{1,0:T(8,128)S(1)} %add_select_fusion, f32[8,2,2,272]{3,0,2,1:T(8,128)S(1)} %slice.92), kind=kOutput, calls=%fused_computation.4 | convolution fusion | flops 14796800 | bytes 78336 | tf_op jit(solution)/shard_map/brct,bts->brcs/dot_general | solution.py:158
  24.4 0.2 reshape.129
  24.6 0.2 reshape.130
  24.8 0.1 broadcast_in_dim.11
  24.9 0.2 maximum_bitcast_fusion
  25.1 0.9 copy.78
  26.1 10.5 %all-to-all-start.1 = ((f32[128,2,2,86]{3,1,2,0:T(2,128)}), f32[128,2,2,86]{3,1,2,0:T(2,128)S(1)}, u32[]{:S(2)}, u32[]{:S(2)}) async-start(f32[128,2,2,86]{3,1,2,0:T(2,128)} %bitcast.23), calls=%async_computation.1 | async-start | bytes 524288 | tf_op jit(solution)/shard_map/all_to_all | solution.py:168
  36.6 8.9 %convolution_convert_fusion = bf16[17,2,256]{2,1,0:T(2,128)(2,1)S(1)} fusion(bf16[17,2,2176]{2,1,0:T(2,128)(2,1)S(1)} %copy-done, bf16[17,2176,256]{2,1,0:T(8,128)(2,1)} %param.16), kind=kOutput, calls=%fused_computation.13 | convolution fusion | flops 37888512 | bytes 19105280 | tf_op jit(solution)/shard_map/ocn,onq->ocq/dot_general | solution.py:173
  45.5 0.2 copy.80
  45.7 1.5 %all-to-all-done.1 = f32[128,2,2,86]{3,1,2,0:T(2,128)S(1)} async-done(((f32[128,2,2,86]{3,1,2,0:T(2,128)}), f32[128,2,2,86]{3,1,2,0:T(2,128)S(1)}, u32[]{:S(2)}, u32[]{:S(2)}) %all-to-all-start.1) | async-done | bytes 176160 | tf_op jit(solution)/shard_map/all_to_all | solution.py:168
  47.1 0.1 copy.79
  47.2 0.2 slice_reduce_fusion
  47.4 0.1 fusion.23
  47.5 0.7 pad_convert_fusion.1.w_ref
  48.3 7.3 %shard_map.136 = f32[2,256,128]{2,1,0:T(8,128)} custom-call(f32[8,512,128]{2,1,0:T(8,128)} %fusion.15.sh_ref, f32[2,256,128]{2,1,0:T(8,128)} %pad_convert_fusion.1.w_ref), custom_call_target="tpu_custom_call" | custom-call | tf_op jit(solution)/shard_map/pallas_call | solution.py:126
  55.6 1.0 %copy.104 = f32[2,128,2,85]{3,2,0,1:T(2,128)S(1)} copy(f32[2,128,2,85]{3,2,1,0:T(2,128)} %bitcast.121) | data formatting | bytes 348160 | tf_op jit(solution)/shard_map/reshape | solution.py:185
  56.6 18.7 %all_to_all.45 = f32[128,2,2,85]{3,1,2,0:T(2,128)S(1)} all-to-all(f32[128,2,2,85]{3,1,2,0:T(2,128)S(1)} %bitcast.122), channel_id=1, replica_groups=mesh['lat'=16,'freq'=8] {'lat','freq'}, dimensions={0} | all-to-all | bytes 348160 | tf_op jit(solution)/shard_map/all_to_all | solution.py:186
  75.3 0.2 copy.103
  75.5 0.0 copy-start.3
  75.5 0.1 slice.98
  75.6 0.3 reshape.136
  75.9 0.2 reshape.135
  76.1 1.2 %fusion.1 = f32[8,2,2,272]{3,2,1,0:T(2,128)S(1)} fusion(f32[8,2,2,272]{3,2,1,0:T(2,128)S(1)} %reshape.135, s32[8,272]{1,0:T(8,128)S(1)} %add_select_fusion), kind=kOutput, calls=%fused_computation.3 | convolution fusion | flops 14796800 | bytes 78336 | tf_op jit(solution)/shard_map/brcs,bts->brct/dot_general | solution.py:189
  77.4 0.0 copy-start.6
  77.4 0.0 copy-start.7
  77.4 0.2 pad_maximum_fusion.1
  77.6 0.8 reshape.137
  78.4 0.0 copy-start.2
  78.4 1.2 %fusion.29 = f32[8,2,18,300]{3,2,1,0:T(8,128)S(1)} fusion(f32[8,2,150,18]{3,2,1,0:T(8,128)S(1)} %reshape.137, f32[150,300,1,1]{1,0,3,2:T(8,128)S(1)} %copy-done.3), kind=kOutput, calls=%fused_computation.68 | convolution fusion | flops 77760000 | bytes 698400 | tf_op jit(solution)/shard_map/brms,mn->brsn/dot_general | solution.py:70
  79.7 0.2 subtract_bitcast_fusion
  79.9 0.6 fusion.8
  80.5 0.1 all_to_all.37
  80.7 0.1 copy.85
  80.8 11.3 %all_to_all.46 = f32[2,8,2700]{2,0,1:T(2,128)S(1)} all-to-all(f32[2,8,2700]{2,0,1:T(2,128)S(1)} %copy.85), channel_id=1, replica_groups=mesh['lat'=16,'freq'=8] {'freq'}, dimensions={1} | all-to-all | bytes 345600 | tf_op jit(solution)/shard_map/all_to_all | solution.py:193
  92.0 0.8 all_to_all.40
  (28 shorter events, 0.2 us)
Async XLA Ops:
  0.0 36.5 %copy-start = (bf16[17,2,2176]{2,1,0:T(2,128)(2,1)S(1)}, bf16[17,2,2176]{2,1,0:T(2,128)(2,1)}, u32[]{:S(2)}) copy-start(bf16[17,2,2176]{2,1,0:T(2,128)(2,1)} %param.15) | copy-start | bytes 443908
  0.0 12.7 %copy-start.1 = (bf16[511,1350]{0,1:T(8,128)(2,1)S(1)}, bf16[511,1350]{0,1:T(8,128)(2,1)}, u32[]{:S(2)}) copy-start(bf16[511,1350]{0,1:T(8,128)(2,1)} %param.19) | copy-start | bytes 4139104
  1.8 18.4 %all-to-all-start = ((f32[8,2,2700]{2,1,0:T(2,128)}), f32[8,2,2700]{2,1,0:T(2,128)S(1)}, u32[]{:S(2)}, u32[]{:S(2)}) async-start(f32[8,2,2700]{2,1,0:T(2,128)} %all_to_all.32), calls=%async_computation | async-start | bytes 360448 | tf_op jit(solution)/shard_map/all_to_all | solution.py:156
  14.2 5.9 %copy-start.10 = (s32[16]{0:T(128)S(1)}, s32[16]{0:T(128)}, u32[]{:S(2)}) copy-start(s32[16]{0:T(128)} %param.18) | copy-start | bytes 196
  15.7 4.7 %copy-start.5 = (f32[144,288,1]{1,0,2:T(8,128)S(1)}, f32[144,288,1]{1,0,2:T(8,128)}, u32[]{:S(2)}) copy-start(f32[144,288,1]{1,0,2:T(8,128)} %constant.120) | copy-start | bytes 497668
  16.4 4.6 %copy-start.8 = (f32[150,144]{1,0:T(8,128)S(1)}, f32[150,144]{1,0:T(8,128)}, u32[]{:S(2)}) copy-start(f32[150,144]{1,0:T(8,128)} %constant.100.clone) | copy-start | bytes 259204
  16.4 4.6 %copy-start.9 = (f32[150,144]{1,0:T(8,128)S(1)}, f32[150,144]{1,0:T(8,128)}, u32[]{:S(2)}) copy-start(f32[150,144]{1,0:T(8,128)} %constant.99.clone) | copy-start | bytes 259204
  18.6 2.6 %copy-start.4 = (f32[300,150,1]{0,1,2:T(8,128)S(1)}, f32[300,150,1]{0,1,2:T(8,128)}, u32[]{:S(2)}) copy-start(f32[300,150,1]{0,1,2:T(8,128)} %constant.121) | copy-start | bytes 540004
  26.1 21.1 %all-to-all-start.1 = ((f32[128,2,2,86]{3,1,2,0:T(2,128)}), f32[128,2,2,86]{3,1,2,0:T(2,128)S(1)}, u32[]{:S(2)}, u32[]{:S(2)}) async-start(f32[128,2,2,86]{3,1,2,0:T(2,128)} %bitcast.23), calls=%async_computation.1 | async-start | bytes 524288 | tf_op jit(solution)/shard_map/all_to_all | solution.py:168
  75.5 2.9 %copy-start.3 = (f32[150,300,1,1]{1,0,3,2:T(8,128)S(1)}, f32[150,300,1,1]{1,0,3,2:T(8,128)}, u32[]{:S(2)}) copy-start(f32[150,300,1,1]{1,0,3,2:T(8,128)} %constant.122) | copy-start | bytes 540004
  77.4 2.3 %copy-start.6 = (f32[8,18,150]{2,1,0:T(8,128)S(1)}, f32[8,18,150]{2,1,0:T(8,128)}, u32[]{:S(2)}) copy-start(f32[8,18,150]{2,1,0:T(8,128)} %constant.103.clone) | copy-start | bytes 259204
  77.4 2.3 %copy-start.7 = (f32[8,18,150]{2,1,0:T(8,128)S(1)}, f32[8,18,150]{2,1,0:T(8,128)}, u32[]{:S(2)}) copy-start(f32[8,18,150]{2,1,0:T(8,128)} %constant.104.clone) | copy-start | bytes 259204
  78.4 1.5 %copy-start.2 = (f32[2,8,18,144,1]{3,2,4,0,1:T(8,128)S(1)}, f32[2,8,18,144,1]{3,2,4,0,1:T(8,128)}, u32[]{:S(2)}) copy-start(f32[2,8,18,144,1]{3,2,4,0,1:T(8,128)} %constant.123) | copy-start | bytes 497668

commit v15 on v10

--- a/solution.py
+++ b/solution.py
@@ -87,7 +87,7 @@
 
 LANE = 128
 SHIFTS = 8
-CHUNK = 64
+CHUNK = 128
 
 
 def stokes_body(k_ref, w_ref, o_ref, sh_ref):

time: 88.7 us -> 90.1 us (1.016)
  Pallas kernels: 6.86 us -> 8.25 us
    pallas_call x1, Pallas kernels: 6.86 us -> 8.25 us  [toeplitz_stokes(): pl.pallas_call(stokes_body, out_shape=jax.ShapeDtypeStruct((2, total, LAN...]
where the time goes in v15:
time: 90.1 us; the launch traced here: 89.5 us
  blocking collectives  30 us (33%)
  starting transfers between devices  15.7 us (17%)
  matrix products  14.3 us (16%)
  local copies, waits for them, and re-layouts  13.9 us (15%)
  Pallas kernels  8.25 us (9%)
  waiting for transfers between devices  4.17 us (5%)
  other arithmetic  2.85 us (3%)
    all_to_all x1, blocking collectives, per_device(): lax.all_to_all(stokes, everyone, split_axis=0, concat_axis=0, tiled=True)  18.7 us
    all_to_all x1, blocking collectives, per_device(): lax.all_to_all(grid_rows.reshape(mine, L), 'freq', split_axis=1, concat_a...  11.3 us
    dot_general x1, matrix products, per_device(): jnp.einsum('ocn,onq->ocq', coef, legendre, preferred_element_type=jnp.flo...  8.94 us
    pallas_call x1, Pallas kernels, toeplitz_stokes(): pl.pallas_call(stokes_body, out_shape=jax.ShapeDtypeStruct((2, total, LAN...  8.25 us
    all_to_all x1, starting transfers between devices, per_device(): lax.all_to_all(gravity, 'freq', split_axis=0, concat_axis=1, tiled=True)  7.89 us
    all_to_all x1, starting transfers between devices, per_device(): lax.all_to_all(payload, everyone, split_axis=0, concat_axis=0, tiled=True)  7.8 us
    unnamed x23, local copies, waits for them, and re-layouts  2.9 us
    all_to_all x1, waiting for transfers between devices, per_device(): lax.all_to_all(gravity, 'freq', split_axis=0, concat_axis=1, tiled=True)  2.69 us
  transfers between devices with their start and end apart: 2, of which 2 were waited for; matrix products, arithmetic and copies ran while one was open for 16% of the time, Pallas kernels for 0%

profile of v15, /device:TPU:0, one launch (start us, length us, event | category | flops | bytes accessed | tf_op | source)
XLA Modules:
  0.0 89.5 jit_solution(17123171727987650289)
XLA Ops:
  0.0 1.7 %all_to_all.32 = f32[8,2,2700]{2,1,0:T(2,128)} reshape(f32[16,2700]{1,0:T(8,128)} %param.14) | data formatting | bytes 345600 | tf_op jit(solution)/shard_map/all_to_all | solution.py:156
  1.7 7.9 %all-to-all-start = ((f32[8,2,2700]{2,1,0:T(2,128)}), f32[8,2,2700]{2,1,0:T(2,128)S(1)}, u32[]{:S(2)}, u32[]{:S(2)}) async-start(f32[8,2,2700]{2,1,0:T(2,128)} %all_to_all.32), calls=%async_computation | async-start | bytes 360448 | tf_op jit(solution)/shard_map/all_to_all | solution.py:156
  9.6 0.9 %reshape.124 = s32[16,8,17]{2,1,0:T(8,128)S(1)} reshape(s32[2176]{0:T(1024)} %param.17) | data formatting | bytes 17408 | tf_op jit(solution)/shard_map/reshape | solution.py:151
  10.6 0.1 reshape.125
  10.6 0.0 copy-start.1
  10.7 0.1 fusion.19
  10.8 0.1 compare_and_fusion
  10.9 1.9 %copy.71 = bf16[511,1350]{1,0:T(8,128)(2,1)S(1)} copy(bf16[511,1350]{0,1:T(8,128)(2,1)} %param.19) | data formatting | bytes 2759400 | tf_op args[5]
  12.8 0.6 gather_fusion
  13.4 0.0 copy-start.10
  13.4 0.1 copy.70
  13.6 0.0 copy-start.5
  13.6 0.2 pad_dynamic-slice_fusion
  13.8 0.0 copy-start.9
  13.8 0.1 pad_maximum_fusion.2
  13.9 0.2 copy-done.10
  14.1 0.1 multiply_cosine_fusion
  14.2 0.4 rev.3
  14.6 0.7 pad_convert_fusion.k_ref
  15.3 2.7 %all-to-all-done = f32[8,2,2700]{2,1,0:T(2,128)S(1)} async-done(((f32[8,2,2700]{2,1,0:T(2,128)}), f32[8,2,2700]{2,1,0:T(2,128)S(1)}, u32[]{:S(2)}, u32[]{:S(2)}) %all-to-all-start) | async-done | bytes 172832 | tf_op jit(solution)/shard_map/all_to_all | solution.py:156
  18.0 0.0 copy-start.4
  18.0 0.1 reshape.126
  18.2 0.6 convolution_bitcast_fusion
  18.8 0.2 multiply_add_fusion
  19.0 0.8 convolution_multiply_fusion
  19.8 0.2 mul.109
  20.0 0.5 copy.75
  20.6 0.5 reshape.128
  21.1 0.1 slice.53
  21.2 1.0 %fusion.3 = f32[8,2,2,272]{3,2,1,0:T(2,128)S(1)} fusion(s32[8,272]{1,0:T(8,128)S(1)} %add_select_fusion, f32[8,2,2,272]{3,0,2,1:T(8,128)S(1)} %slice.52), kind=kOutput, calls=%fused_computation.4 | convolution fusion | flops 14796800 | bytes 78336 | tf_op jit(solution)/shard_map/brct,bts->brcs/dot_general | solution.py:158
  22.1 0.2 reshape.129
  22.4 0.2 reshape.130
  22.6 0.1 broadcast_in_dim.11
  22.7 0.2 maximum_bitcast_fusion
  22.9 0.9 %copy.78 = f32[16,8,2,2,86]{4,2,3,1,0:T(2,128)} copy(f32[16,8,2,2,86]{4,0,1,3,2:T(8,128)S(1)} %maximum_bitcast_fusion) | data formatting | bytes 352256 | tf_op jit(solution)/shard_map/transpose | solution.py:165
  23.8 7.8 %all-to-all-start.1 = ((f32[128,2,2,86]{3,1,2,0:T(2,128)}), f32[128,2,2,86]{3,1,2,0:T(2,128)S(1)}, u32[]{:S(2)}, u32[]{:S(2)}) async-start(f32[128,2,2,86]{3,1,2,0:T(2,128)} %bitcast.15), calls=%async_computation.1 | async-start | bytes 524288 | tf_op jit(solution)/shard_map/all_to_all | solution.py:168
  31.6 8.9 %convolution_convert_fusion = bf16[17,2,256]{2,1,0:T(2,128)(2,1)S(1)} fusion(bf16[17,2,2176]{2,1,0:T(2,128)(2,1)S(1)} %copy-done, bf16[17,2176,256]{2,1,0:T(8,128)(2,1)} %param.16), kind=kOutput, calls=%fused_computation.13 | convolution fusion | flops 37888512 | bytes 19105280 | tf_op jit(solution)/shard_map/ocn,onq->ocq/dot_general | solution.py:173
  40.5 0.2 copy.80
  40.7 1.5 %all-to-all-done.1 = f32[128,2,2,86]{3,1,2,0:T(2,128)S(1)} async-done(((f32[128,2,2,86]{3,1,2,0:T(2,128)}), f32[128,2,2,86]{3,1,2,0:T(2,128)S(1)}, u32[]{:S(2)}, u32[]{:S(2)}) %all-to-all-start.1) | async-done | bytes 176160 | tf_op jit(solution)/shard_map/all_to_all | solution.py:168
  42.2 0.1 copy.79
  42.3 0.2 slice_reduce_fusion
  42.5 0.1 fusion.15
  42.6 0.7 pad_convert_fusion.1.w_ref
  43.3 8.2 %shard_map.136 = f32[2,256,128]{2,1,0:T(8,128)} custom-call(f32[520,128]{1,0:T(8,128)} %pad_convert_fusion.k_ref, f32[2,256,128]{2,1,0:T(8,128)} %pad_convert_fusion.1.w_ref), custom_call_target="tpu_custom_call" | custom-call | tf_op jit(solution)/shard_map/pallas_call | solution.py:127
  51.6 1.0 %copy.104 = f32[2,128,2,85]{3,2,0,1:T(2,128)S(1)} copy(f32[2,128,2,85]{3,2,1,0:T(2,128)} %bitcast.89) | data formatting | bytes 348160 | tf_op jit(solution)/shard_map/reshape | solution.py:185
  52.6 18.7 %all_to_all.45 = f32[128,2,2,85]{3,1,2,0:T(2,128)S(1)} all-to-all(f32[128,2,2,85]{3,1,2,0:T(2,128)S(1)} %bitcast.90), channel_id=1, replica_groups=mesh['lat'=16,'freq'=8] {'lat','freq'}, dimensions={0} | all-to-all | bytes 348160 | tf_op jit(solution)/shard_map/all_to_all | solution.py:186
  71.3 0.2 copy.103
  71.5 0.1 slice.58
  71.6 0.3 reshape.136
  71.9 0.0 copy-start.3
  71.9 0.2 reshape.135
  72.1 1.2 %fusion.1 = f32[8,2,2,272]{3,2,1,0:T(2,128)S(1)} fusion(f32[8,2,2,272]{3,2,1,0:T(2,128)S(1)} %reshape.135, s32[8,272]{1,0:T(8,128)S(1)} %add_select_fusion), kind=kOutput, calls=%fused_computation.3 | convolution fusion | flops 14796800 | bytes 78336 | tf_op jit(solution)/shard_map/brcs,bts->brct/dot_general | solution.py:189
  73.3 0.2 pad_maximum_fusion.1
  73.6 0.0 copy-start.7
  73.6 0.8 reshape.137
  74.4 1.2 %fusion.21 = f32[8,2,18,300]{3,2,1,0:T(8,128)S(1)} fusion(f32[8,2,150,18]{3,2,1,0:T(8,128)S(1)} %reshape.137, f32[150,300,1,1]{1,0,3,2:T(8,128)S(1)} %copy-done.3), kind=kOutput, calls=%fused_computation.52 | convolution fusion | flops 77760000 | bytes 698400 | tf_op jit(solution)/shard_map/brms,mn->brsn/dot_general | solution.py:70
  75.6 0.0 copy-start.2
  75.6 0.2 subtract_bitcast_fusion
  75.9 0.7 copy-done.2
  76.6 0.6 fusion.8
  77.2 0.1 all_to_all.37
  77.4 0.1 copy.85
  77.5 11.3 %all_to_all.46 = f32[2,8,2700]{2,0,1:T(2,128)S(1)} all-to-all(f32[2,8,2700]{2,0,1:T(2,128)S(1)} %copy.85), channel_id=1, replica_groups=mesh['lat'=16,'freq'=8] {'freq'}, dimensions={1} | all-to-all | bytes 345600 | tf_op jit(solution)/shard_map/all_to_all | solution.py:193
  88.7 0.8 all_to_all.40
  (20 shorter events, 0.1 us)
Async XLA Ops:
  0.0 31.6 %copy-start = (bf16[17,2,2176]{2,1,0:T(2,128)(2,1)S(1)}, bf16[17,2,2176]{2,1,0:T(2,128)(2,1)}, u32[]{:S(2)}) copy-start(bf16[17,2,2176]{2,1,0:T(2,128)(2,1)} %param.15) | copy-start | bytes 443908
  1.7 16.2 %all-to-all-start = ((f32[8,2,2700]{2,1,0:T(2,128)}), f32[8,2,2700]{2,1,0:T(2,128)S(1)}, u32[]{:S(2)}, u32[]{:S(2)}) async-start(f32[8,2,2700]{2,1,0:T(2,128)} %all_to_all.32), calls=%async_computation | async-start | bytes 360448 | tf_op jit(solution)/shard_map/all_to_all | solution.py:156
  10.6 2.1 %copy-start.1 = (bf16[511,1350]{0,1:T(8,128)(2,1)S(1)}, bf16[511,1350]{0,1:T(8,128)(2,1)}, u32[]{:S(2)}) copy-start(bf16[511,1350]{0,1:T(8,128)(2,1)} %param.19) | copy-start | bytes 4139104
  13.4 0.7 copy-start.10
  13.6 4.6 %copy-start.5 = (f32[144,288,1]{1,0,2:T(8,128)S(1)}, f32[144,288,1]{1,0,2:T(8,128)}, u32[]{:S(2)}) copy-start(f32[144,288,1]{1,0,2:T(8,128)} %constant.120) | copy-start | bytes 497668
  13.7 5.0 %copy-start.8 = (f32[150,144]{1,0:T(8,128)S(1)}, f32[150,144]{1,0:T(8,128)}, u32[]{:S(2)}) copy-start(f32[150,144]{1,0:T(8,128)} %constant.100.clone) | copy-start | bytes 259204
  13.8 5.0 %copy-start.9 = (f32[150,144]{1,0:T(8,128)S(1)}, f32[150,144]{1,0:T(8,128)}, u32[]{:S(2)}) copy-start(f32[150,144]{1,0:T(8,128)} %constant.99.clone) | copy-start | bytes 259204
  18.0 1.0 %copy-start.4 = (f32[300,150,1]{0,1,2:T(8,128)S(1)}, f32[300,150,1]{0,1,2:T(8,128)}, u32[]{:S(2)}) copy-start(f32[300,150,1]{0,1,2:T(8,128)} %constant.121) | copy-start | bytes 540004
  23.8 18.4 %all-to-all-start.1 = ((f32[128,2,2,86]{3,1,2,0:T(2,128)}), f32[128,2,2,86]{3,1,2,0:T(2,128)S(1)}, u32[]{:S(2)}, u32[]{:S(2)}) async-start(f32[128,2,2,86]{3,1,2,0:T(2,128)} %bitcast.15), calls=%async_computation.1 | async-start | bytes 524288 | tf_op jit(solution)/shard_map/all_to_all | solution.py:168
  71.9 2.5 %copy-start.3 = (f32[150,300,1,1]{1,0,3,2:T(8,128)S(1)}, f32[150,300,1,1]{1,0,3,2:T(8,128)}, u32[]{:S(2)}) copy-start(f32[150,300,1,1]{1,0,3,2:T(8,128)} %constant.122) | copy-start | bytes 540004
  73.5 2.1 %copy-start.6 = (f32[8,18,150]{2,1,0:T(8,128)S(1)}, f32[8,18,150]{2,1,0:T(8,128)}, u32[]{:S(2)}) copy-start(f32[8,18,150]{2,1,0:T(8,128)} %constant.103.clone) | copy-start | bytes 259204
  73.6 2.1 %copy-start.7 = (f32[8,18,150]{2,1,0:T(8,128)S(1)}, f32[8,18,150]{2,1,0:T(8,128)}, u32[]{:S(2)}) copy-start(f32[8,18,150]{2,1,0:T(8,128)} %constant.104.clone) | copy-start | bytes 259204
  75.6 1.0 %copy-start.2 = (f32[2,8,18,144,1]{3,2,4,0,1:T(8,128)S(1)}, f32[2,8,18,144,1]{3,2,4,0,1:T(8,128)}, u32[]{:S(2)}) copy-start(f32[2,8,18,144,1]{3,2,4,0,1:T(8,128)} %constant.123) | copy-start | bytes 497668

commit v16 on v15

--- a/solution.py
+++ b/solution.py
@@ -87,7 +87,7 @@
 
 LANE = 128
 SHIFTS = 8
-CHUNK = 128
+CHUNK = 32
 
 
 def stokes_body(k_ref, w_ref, o_ref, sh_ref):

time: 90.1 us -> 89.1 us (0.989)
  Pallas kernels: 8.25 us -> 7.27 us
    pallas_call x1, Pallas kernels: 8.25 us -> 7.27 us  [toeplitz_stokes(): pl.pallas_call(stokes_body, out_shape=jax.ShapeDtypeStruct((2, total, LAN...]
where the time goes in v16:
time: 89.1 us; the launch traced here: 88.6 us
  blocking collectives  30 us (34%)
  starting transfers between devices  15.7 us (18%)
  matrix products  14.3 us (16%)
  local copies, waits for them, and re-layouts  13.9 us (16%)
  Pallas kernels  7.27 us (8%)
  waiting for transfers between devices  4.17 us (5%)
  other arithmetic  2.85 us (3%)
    all_to_all x1, blocking collectives, per_device(): lax.all_to_all(stokes, everyone, split_axis=0, concat_axis=0, tiled=True)  18.7 us
    all_to_all x1, blocking collectives, per_device(): lax.all_to_all(grid_rows.reshape(mine, L), 'freq', split_axis=1, concat_a...  11.3 us
    dot_general x1, matrix products, per_device(): jnp.einsum('ocn,onq->ocq', coef, legendre, preferred_element_type=jnp.flo...  8.94 us
    all_to_all x1, starting transfers between devices, per_device(): lax.all_to_all(gravity, 'freq', split_axis=0, concat_axis=1, tiled=True)  7.89 us
    all_to_all x1, starting transfers between devices, per_device(): lax.all_to_all(payload, everyone, split_axis=0, concat_axis=0, tiled=True)  7.8 us
    pallas_call x1, Pallas kernels, toeplitz_stokes(): pl.pallas_call(stokes_body, out_shape=jax.ShapeDtypeStruct((2, total, LAN...  7.27 us
    unnamed x23, local copies, waits for them, and re-layouts  2.9 us
    all_to_all x1, waiting for transfers between devices, per_device(): lax.all_to_all(gravity, 'freq', split_axis=0, concat_axis=1, tiled=True)  2.69 us
  transfers between devices with their start and end apart: 2, of which 2 were waited for; matrix products, arithmetic and copies ran while one was open for 16% of the time, Pallas kernels for 0%

profile of v16, /device:TPU:0, one launch (start us, length us, event | category | flops | bytes accessed | tf_op | source)
XLA Modules:
  0.0 88.6 jit_solution(10252294192049985818)
XLA Ops:
  0.0 1.7 %all_to_all.32 = f32[8,2,2700]{2,1,0:T(2,128)} reshape(f32[16,2700]{1,0:T(8,128)} %param.14) | data formatting | bytes 345600 | tf_op jit(solution)/shard_map/all_to_all | solution.py:156
  1.7 7.9 %all-to-all-start = ((f32[8,2,2700]{2,1,0:T(2,128)}), f32[8,2,2700]{2,1,0:T(2,128)S(1)}, u32[]{:S(2)}, u32[]{:S(2)}) async-start(f32[8,2,2700]{2,1,0:T(2,128)} %all_to_all.32), calls=%async_computation | async-start | bytes 360448 | tf_op jit(solution)/shard_map/all_to_all | solution.py:156
  9.6 0.9 %reshape.124 = s32[16,8,17]{2,1,0:T(8,128)S(1)} reshape(s32[2176]{0:T(1024)} %param.17) | data formatting | bytes 17408 | tf_op jit(solution)/shard_map/reshape | solution.py:151
  10.6 0.1 reshape.125
  10.6 0.0 copy-start.1
  10.7 0.1 fusion.19
  10.8 0.1 compare_and_fusion
  10.9 1.9 %copy.71 = bf16[511,1350]{1,0:T(8,128)(2,1)S(1)} copy(bf16[511,1350]{0,1:T(8,128)(2,1)} %param.19) | data formatting | bytes 2759400 | tf_op args[5]
  12.8 0.6 gather_fusion
  13.4 0.0 copy-start.10
  13.4 0.1 copy.70
  13.6 0.0 copy-start.5
  13.6 0.2 pad_dynamic-slice_fusion
  13.8 0.0 copy-start.9
  13.8 0.1 pad_maximum_fusion.2
  13.9 0.2 copy-done.10
  14.1 0.1 multiply_cosine_fusion
  14.2 0.4 rev.3
  14.6 0.7 pad_convert_fusion.k_ref
  15.3 2.7 %all-to-all-done = f32[8,2,2700]{2,1,0:T(2,128)S(1)} async-done(((f32[8,2,2700]{2,1,0:T(2,128)}), f32[8,2,2700]{2,1,0:T(2,128)S(1)}, u32[]{:S(2)}, u32[]{:S(2)}) %all-to-all-start) | async-done | bytes 172832 | tf_op jit(solution)/shard_map/all_to_all | solution.py:156
  18.0 0.0 copy-start.4
  18.0 0.1 reshape.126
  18.2 0.6 convolution_bitcast_fusion
  18.8 0.2 multiply_add_fusion
  19.0 0.8 convolution_multiply_fusion
  19.8 0.2 mul.109
  20.0 0.5 copy.75
  20.6 0.5 reshape.128
  21.1 0.1 slice.53
  21.2 1.0 %fusion.3 = f32[8,2,2,272]{3,2,1,0:T(2,128)S(1)} fusion(s32[8,272]{1,0:T(8,128)S(1)} %add_select_fusion, f32[8,2,2,272]{3,0,2,1:T(8,128)S(1)} %slice.52), kind=kOutput, calls=%fused_computation.4 | convolution fusion | flops 14796800 | bytes 78336 | tf_op jit(solution)/shard_map/brct,bts->brcs/dot_general | solution.py:158
  22.1 0.2 reshape.129
  22.4 0.2 reshape.130
  22.6 0.1 broadcast_in_dim.11
  22.7 0.2 maximum_bitcast_fusion
  22.9 0.9 %copy.78 = f32[16,8,2,2,86]{4,2,3,1,0:T(2,128)} copy(f32[16,8,2,2,86]{4,0,1,3,2:T(8,128)S(1)} %maximum_bitcast_fusion) | data formatting | bytes 352256 | tf_op jit(solution)/shard_map/transpose | solution.py:165
  23.8 7.8 %all-to-all-start.1 = ((f32[128,2,2,86]{3,1,2,0:T(2,128)}), f32[128,2,2,86]{3,1,2,0:T(2,128)S(1)}, u32[]{:S(2)}, u32[]{:S(2)}) async-start(f32[128,2,2,86]{3,1,2,0:T(2,128)} %bitcast.15), calls=%async_computation.1 | async-start | bytes 524288 | tf_op jit(solution)/shard_map/all_to_all | solution.py:168
  31.6 8.9 %convolution_convert_fusion = bf16[17,2,256]{2,1,0:T(2,128)(2,1)S(1)} fusion(bf16[17,2,2176]{2,1,0:T(2,128)(2,1)S(1)} %copy-done, bf16[17,2176,256]{2,1,0:T(8,128)(2,1)} %param.16), kind=kOutput, calls=%fused_computation.13 | convolution fusion | flops 37888512 | bytes 19105280 | tf_op jit(solution)/shard_map/ocn,onq->ocq/dot_general | solution.py:173
  40.5 0.2 copy.80
  40.7 1.5 %all-to-all-done.1 = f32[128,2,2,86]{3,1,2,0:T(2,128)S(1)} async-done(((f32[128,2,2,86]{3,1,2,0:T(2,128)}), f32[128,2,2,86]{3,1,2,0:T(2,128)S(1)}, u32[]{:S(2)}, u32[]{:S(2)}) %all-to-all-start.1) | async-done | bytes 176160 | tf_op jit(solution)/shard_map/all_to_all | solution.py:168
  42.2 0.1 copy.79
  42.3 0.2 slice_reduce_fusion
  42.5 0.1 fusion.15
  42.6 0.7 pad_convert_fusion.1.w_ref
  43.3 7.3 %shard_map.136 = f32[2,256,128]{2,1,0:T(8,128)} custom-call(f32[520,128]{1,0:T(8,128)} %pad_convert_fusion.k_ref, f32[2,256,128]{2,1,0:T(8,128)} %pad_convert_fusion.1.w_ref), custom_call_target="tpu_custom_call" | custom-call | tf_op jit(solution)/shard_map/pallas_call | solution.py:127
  50.6 1.0 %copy.104 = f32[2,128,2,85]{3,2,0,1:T(2,128)S(1)} copy(f32[2,128,2,85]{3,2,1,0:T(2,128)} %bitcast.89) | data formatting | bytes 348160 | tf_op jit(solution)/shard_map/reshape | solution.py:185
  51.6 18.7 %all_to_all.45 = f32[128,2,2,85]{3,1,2,0:T(2,128)S(1)} all-to-all(f32[128,2,2,85]{3,1,2,0:T(2,128)S(1)} %bitcast.90), channel_id=1, replica_groups=mesh['lat'=16,'freq'=8] {'lat','freq'}, dimensions={0} | all-to-all | bytes 348160 | tf_op jit(solution)/shard_map/all_to_all | solution.py:186
  70.3 0.2 copy.103
  70.5 0.1 slice.58
  70.6 0.3 reshape.136
  70.9 0.0 copy-start.3
  70.9 0.2 reshape.135
  71.1 1.2 %fusion.1 = f32[8,2,2,272]{3,2,1,0:T(2,128)S(1)} fusion(f32[8,2,2,272]{3,2,1,0:T(2,128)S(1)} %reshape.135, s32[8,272]{1,0:T(8,128)S(1)} %add_select_fusion), kind=kOutput, calls=%fused_computation.3 | convolution fusion | flops 14796800 | bytes 78336 | tf_op jit(solution)/shard_map/brcs,bts->brct/dot_general | solution.py:189
  72.3 0.2 pad_maximum_fusion.1
  72.6 0.0 copy-start.7
  72.6 0.8 reshape.137
  73.4 1.2 %fusion.21 = f32[8,2,18,300]{3,2,1,0:T(8,128)S(1)} fusion(f32[8,2,150,18]{3,2,1,0:T(8,128)S(1)} %reshape.137, f32[150,300,1,1]{1,0,3,2:T(8,128)S(1)} %copy-done.3), kind=kOutput, calls=%fused_computation.52 | convolution fusion | flops 77760000 | bytes 698400 | tf_op jit(solution)/shard_map/brms,mn->brsn/dot_general | solution.py:70
  74.6 0.0 copy-start.2
  74.7 0.2 subtract_bitcast_fusion
  74.9 0.7 copy-done.2
  75.6 0.6 fusion.8
  76.2 0.1 all_to_all.37
  76.4 0.1 copy.85
  76.5 11.3 %all_to_all.46 = f32[2,8,2700]{2,0,1:T(2,128)S(1)} all-to-all(f32[2,8,2700]{2,0,1:T(2,128)S(1)} %copy.85), channel_id=1, replica_groups=mesh['lat'=16,'freq'=8] {'freq'}, dimensions={1} | all-to-all | bytes 345600 | tf_op jit(solution)/shard_map/all_to_all | solution.py:193
  87.8 0.8 all_to_all.40
  (20 shorter events, 0.1 us)
Async XLA Ops:
  0.0 31.6 %copy-start = (bf16[17,2,2176]{2,1,0:T(2,128)(2,1)S(1)}, bf16[17,2,2176]{2,1,0:T(2,128)(2,1)}, u32[]{:S(2)}) copy-start(bf16[17,2,2176]{2,1,0:T(2,128)(2,1)} %param.15) | copy-start | bytes 443908
  1.7 16.2 %all-to-all-start = ((f32[8,2,2700]{2,1,0:T(2,128)}), f32[8,2,2700]{2,1,0:T(2,128)S(1)}, u32[]{:S(2)}, u32[]{:S(2)}) async-start(f32[8,2,2700]{2,1,0:T(2,128)} %all_to_all.32), calls=%async_computation | async-start | bytes 360448 | tf_op jit(solution)/shard_map/all_to_all | solution.py:156
  10.6 2.1 %copy-start.1 = (bf16[511,1350]{0,1:T(8,128)(2,1)S(1)}, bf16[511,1350]{0,1:T(8,128)(2,1)}, u32[]{:S(2)}) copy-start(bf16[511,1350]{0,1:T(8,128)(2,1)} %param.19) | copy-start | bytes 4139104
  13.4 0.7 copy-start.10
  13.6 4.6 %copy-start.5 = (f32[144,288,1]{1,0,2:T(8,128)S(1)}, f32[144,288,1]{1,0,2:T(8,128)}, u32[]{:S(2)}) copy-start(f32[144,288,1]{1,0,2:T(8,128)} %constant.120) | copy-start | bytes 497668
  13.7 5.0 %copy-start.8 = (f32[150,144]{1,0:T(8,128)S(1)}, f32[150,144]{1,0:T(8,128)}, u32[]{:S(2)}) copy-start(f32[150,144]{1,0:T(8,128)} %constant.100.clone) | copy-start | bytes 259204
  13.8 5.0 %copy-start.9 = (f32[150,144]{1,0:T(8,128)S(1)}, f32[150,144]{1,0:T(8,128)}, u32[]{:S(2)}) copy-start(f32[150,144]{1,0:T(8,128)} %constant.99.clone) | copy-start | bytes 259204
  18.0 1.0 %copy-start.4 = (f32[300,150,1]{0,1,2:T(8,128)S(1)}, f32[300,150,1]{0,1,2:T(8,128)}, u32[]{:S(2)}) copy-start(f32[300,150,1]{0,1,2:T(8,128)} %constant.121) | copy-start | bytes 540004
  23.8 18.4 %all-to-all-start.1 = ((f32[128,2,2,86]{3,1,2,0:T(2,128)}), f32[128,2,2,86]{3,1,2,0:T(2,128)S(1)}, u32[]{:S(2)}, u32[]{:S(2)}) async-start(f32[128,2,2,86]{3,1,2,0:T(2,128)} %bitcast.15), calls=%async_computation.1 | async-start | bytes 524288 | tf_op jit(solution)/shard_map/all_to_all | solution.py:168
  70.9 2.5 %copy-start.3 = (f32[150,300,1,1]{1,0,3,2:T(8,128)S(1)}, f32[150,300,1,1]{1,0,3,2:T(8,128)}, u32[]{:S(2)}) copy-start(f32[150,300,1,1]{1,0,3,2:T(8,128)} %constant.122) | copy-start | bytes 540004
  72.6 2.1 %copy-start.6 = (f32[8,18,150]{2,1,0:T(8,128)S(1)}, f32[8,18,150]{2,1,0:T(8,128)}, u32[]{:S(2)}) copy-start(f32[8,18,150]{2,1,0:T(8,128)} %constant.103.clone) | copy-start | bytes 259204
  72.6 2.1 %copy-start.7 = (f32[8,18,150]{2,1,0:T(8,128)S(1)}, f32[8,18,150]{2,1,0:T(8,128)}, u32[]{:S(2)}) copy-start(f32[8,18,150]{2,1,0:T(8,128)} %constant.104.clone) | copy-start | bytes 259204
  74.6 1.0 %copy-start.2 = (f32[2,8,18,144,1]{3,2,4,0,1:T(8,128)S(1)}, f32[2,8,18,144,1]{3,2,4,0,1:T(8,128)}, u32[]{:S(2)}) copy-start(f32[2,8,18,144,1]{3,2,4,0,1:T(8,128)} %constant.123) | copy-start | bytes 497668
